TPU v7x, 512 devices: a whole 4x8x8 slice. The times are simulated.
512 devices in a mesh: lon: 32 (over y, x), tm: 16 (over z, core).
Axes of the slice: x: 4, y: 8, z: 8, core: 2. Of those that a mesh axis runs over, the one named last changes fastest.
Arguments:
- anomalies: bfloat16 [4096, 8192], P('lon', 'tm'), may hold values from -200 to 200, as said below
- neighbor_ids: int32 [16, 3], replicated, may hold values from 0 to 15, as said below
- neighbor_counts: int32 [16], replicated, may hold values from 1 to 3
- lag_set: int32 [9], replicated, may hold values from 0 to 128, as said below
Outputs:
- network: float32 [4096, 6912], P(('lon', 'tm'))
Inputs may be any that keep to these rules, and one draw needn't show every extreme that they name: `neighbor_ids`: row b lists 3 distinct blocks, each within loop distance 2 of block b (b itself may appear); only the first neighbor_counts[b] slots are used. `lag_set`: 9 distinct lags. Real-valued anomalies; no point's series is constant.
All inputs are finite; a program needn't handle non-finite values.
Results may differ from a plain program's by a relative error of at most 0.0037.
Values may be sent and summed in bfloat16 or wider, within the bound.
No kernel may reach another device: no remote copies, remote signals or barrier semaphores. Data moves between devices by JAX's collectives and lax.ppermute only.
A program may use at most 64 MiB of HBM per device.

v0:
```python
import jax
import jax.numpy as jnp
from jax import lax
from jax.sharding import PartitionSpec as P

LMAX = 128
NLAG = 9
K_SLOTS = 3
REACH = 2


def joined(part, axis, combine):
    gathered = jax.tree.map(lambda a: lax.all_gather(a, axis), part)

    def take(source):
        return jax.tree.map(lambda a: lax.dynamic_index_in_dim(a, source, 0, False), gathered)

    return lax.fori_loop(
        1, lax.axis_size(axis), lambda source, state: combine(state, take(source)), take(0)
    )


def shifted(value, axis, by):
    size = lax.axis_size(axis)
    pairs = [(i, i + by) for i in range(size) if 0 <= i + by < size]
    return lax.ppermute(value, axis, pairs)


def from_partner(value, axis, stride):
    mask = 2**stride
    pairs = [(source, source ^ mask) for source in range(lax.axis_size(axis))]
    return lax.ppermute(value, axis, pairs)


def shifted_2(value, axis, by):
    size = lax.axis_size(axis)
    return lax.ppermute(value, axis, [(i, (i + by) % size) for i in range(size)])


def chan_merge(earlier, later):
    count_first, mean_first, square_first = earlier
    count_second, mean_second, square_second = later
    merged = count_first + count_second
    delta = mean_second - mean_first
    new_mean = mean_first + delta * (count_second / merged)
    new_square = (
        square_first + square_second + delta * delta * (count_first * count_second / merged)
    )
    return (merged, new_mean, new_square)


def left_operand(own_rows, lag_days, days_dev):
    return jnp.concatenate(
        [own_rows[:, :days_dev], lax.dynamic_slice_in_dim(own_rows, lag_days, days_dev, 1)], 1
    )


def right_product(left_side, columns, lag_days, days_dev):
    right_side = jnp.concatenate(
        [lax.dynamic_slice_in_dim(columns, lag_days, days_dev, 1), columns[:, :days_dev]], 1
    )
    return lax.dot_general(
        left_side, right_side, (((1,), (1,)), ((), ())), preferred_element_type=jnp.float32
    )


def local(anomalies, neighbor_ids, neighbor_counts, lag_set):
    half_rows, days_dev = anomalies.shape
    tm_size = lax.axis_size("tm")
    blocks = lax.axis_size("lon") // 2
    block_width = 2 * half_rows
    total_days = days_dev * tm_size
    values = anomalies.astype(jnp.float32)
    shard_mean = jnp.mean(values, axis=1)
    shard_square = jnp.sum(jnp.square(values - shard_mean[:, None]), axis=1)
    shard_count = jnp.full((1,), days_dev, jnp.float32)
    merged_count, point_mean, point_m2 = joined(
        (shard_count, shard_mean, shard_square), "tm", chan_merge
    )
    spread = jnp.sqrt(point_m2 / merged_count + 1e-06)
    standardized = ((values - point_mean[:, None]) / spread[:, None]).astype(jnp.bfloat16)
    margin = shifted(standardized[:, :LMAX], "tm", -1)
    extended = jnp.concatenate([standardized, margin], 1)
    partner = from_partner(extended, "lon", 0)
    lon_index = lax.axis_index("lon")
    parity = lon_index % 2
    own_block = jnp.where(
        parity == 0,
        jnp.concatenate([extended, partner], 0),
        jnp.concatenate([partner, extended], 0),
    )
    block_index = lon_index // 2
    later_blocks = []
    earlier_blocks = []
    for offset in range(1, REACH + 1):
        later_blocks.append(shifted_2(own_block, "lon", -2 * offset))
        earlier_blocks.append(shifted_2(own_block, "lon", 2 * offset))
    candidates = jnp.stack(earlier_blocks[::-1] + [own_block] + later_blocks, 0)
    block_ids = lax.dynamic_index_in_dim(neighbor_ids, block_index, 0, keepdims=False)
    live_count = lax.dynamic_index_in_dim(neighbor_counts, block_index, 0, keepdims=False)
    positions = (block_ids - block_index + REACH) % blocks

    def term_rows(row_count):
        slot_columns = [
            lax.dynamic_index_in_dim(candidates, positions[slot_index], 0, keepdims=False)
            for slot_index in range(K_SLOTS)
        ]
        by_slot = [[] for slot_index in range(K_SLOTS)]
        for lag_index in range(NLAG):
            left_side = left_operand(extended, lag_set[lag_index], days_dev)
            for slot_index in range(K_SLOTS):
                by_slot[slot_index].append(
                    right_product(left_side, slot_columns[slot_index], lag_set[lag_index], days_dev)
                )
        products = [item for slot_list in by_slot for item in slot_list]
        return jnp.stack(products, 1).reshape(row_count, -1)

    out_rows = half_rows // tm_size
    summed = lax.psum(term_rows(half_rows), "tm")
    comoment = lax.dynamic_slice_in_dim(summed, lax.axis_index("tm") * out_rows, out_rows, 0)
    comoment = comoment.reshape(out_rows, K_SLOTS, NLAG, block_width)
    denominator = 2.0 * (total_days - lag_set).astype(jnp.float32)
    is_live = jnp.arange(K_SLOTS, dtype=jnp.int32) < live_count
    linked = jnp.where(
        is_live[None, :, None, None], comoment / denominator[None, None, :, None], 0.0
    )
    squares = jnp.sum(jnp.square(linked), axis=(1, 2, 3))
    row_scale = jnp.sqrt(squares / (live_count * NLAG * block_width).astype(jnp.float32) + 1e-06)
    return (linked / row_scale[:, None, None, None]).reshape(out_rows, -1)


def solution(mesh):
    return jax.shard_map(
        local,
        mesh=mesh,
        in_specs=(P("lon", "tm"), P(), P(), P()),
        out_specs=P(("lon", "tm"), None),
        check_vma=False,
    )
```

profile of v0, /device:TPU:6, one launch (start us, length us, event | category | flops | bytes accessed | tf_op | source)
XLA Modules:
  0.0 342.4 jit_solution(14211399032186157105)
XLA Ops:
  6.5 1.3 dynamic-slice.54
  8.6 32.0 %all-reduce = f32[16]{0:T(128)S(1)} all-reduce(f32[16]{0:T(128)S(1)} %dynamic-update-slice), channel_id=1, replica_groups=mesh['lon'=32,'tm'=16] {'tm'}, use_global_device_ids=true, to_apply=%add | all-reduce | flops 16 | bytes 128
  40.6 1.0 convert_reduce_fusion
  41.6 1.1 fusion.61
  42.7 14.1 %all-gather.3 = f32[16,1,128]{2,1,0:T(1,128)S(1)} all-gather(f32[1,1,128]{2,1,0:T(1,128)S(1)} %bitcast.237), channel_id=3, replica_groups=mesh['lon'=32,'tm'=16] {'tm'}, dimensions={0}, use_global_device_ids=true | all-gather | bytes 8704 | tf_op jit(solution)/shard_map/all_gather | solution.py:13
  56.8 16.0 %all-gather.2 = f32[16,1,128]{2,1,0:T(1,128)S(1)} all-gather(f32[1,1,128]{2,1,0:T(1,128)S(1)} %get-tuple-element.256), channel_id=2, replica_groups=mesh['lon'=32,'tm'=16] {'tm'}, dimensions={0}, use_global_device_ids=true | all-gather | bytes 8704 | tf_op jit(solution)/shard_map/all_gather | solution.py:13
  72.8 39.3 %while.19 = (s32[]{:T(128)}, f32[1]{0:T(128)}, f32[128]{0:T(128)S(1)}, f32[128]{0:T(128)S(1)}, f32[16,1]{0,1:T(1,128)S(1)}, /*index=5*/f32[16,128]{1,0:T(8,128)S...) while((s32[]{:T(128)}, f32[1]{0:T(128)}, f32[128]{0:T(128)S(1)}, f32[128]{0:T(128)S(1)}, ...), condition=%wide.region_3.4_spmd, body=%wide.region_2.3_spmd.sunk | while | flops 905 | bytes 3295 | solution.py:18
  112.1 1.0 fusion.63
  113.1 1.3 collective-permute-start
  116.2 2.7 collective-permute-start.1
  123.8 3.5 %collective-permute-start.2 = (bf16[256,640]{1,0:T(8,128)(2,1)S(1)}, bf16[256,640]{1,0:T(8,128)(2,1)S(1)}, u32[]{:S(2)}, u32[]{:S(2)}) collective-permute-start(bf16[256,640]{1,0:T(8,128)(2,1)S(1)} %maximum_select_fusion), channel_id=1, source_target_pairs={{0,64},{16,80},{32,96},{48,112},{64,128},{80,144},{96,160},{112,17... | collective-permute-start | bytes 983048 | tf_op jit(solution)/shard_map/ppermute | solution.py:37
  127.3 1.7 fusion.107
  148.2 4.3 %collective-permute-start.3 = (bf16[256,640]{1,0:T(8,128)(2,1)S(1)}, bf16[256,640]{1,0:T(8,128)(2,1)S(1)}, u32[]{:S(2)}, u32[]{:S(2)}) collective-permute-start(bf16[256,640]{1,0:T(8,128)(2,1)S(1)} %maximum_select_fusion), channel_id=1, source_target_pairs={{0,32},{16,48},{32,64},{48,80},{64,96},{80,112},{96,128},{112,144}... | collective-permute-start | bytes 983048 | tf_op jit(solution)/shard_map/ppermute | solution.py:37
  152.9 3.0 collective-permute-start.4
  155.9 4.0 %collective-permute-start.5 = (bf16[256,640]{1,0:T(8,128)(2,1)S(1)}, bf16[256,640]{1,0:T(8,128)(2,1)S(1)}, u32[]{:S(2)}, u32[]{:S(2)}) collective-permute-start(bf16[256,640]{1,0:T(8,128)(2,1)S(1)} %maximum_select_fusion), channel_id=1, source_target_pairs={{0,448},{16,464},{32,480},{48,496},{64,0},{80,16},{96,32},{112,48}... | collective-permute-start | bytes 983048 | tf_op jit(solution)/shard_map/ppermute | solution.py:37
  160.0 8.7 %collective-permute-done.3 = bf16[256,640]{1,0:T(8,128)(2,1)S(1)} collective-permute-done((bf16[256,640]{1,0:T(8,128)(2,1)S(1)}, bf16[256,640]{1,0:T(8,128)(2,1)S(1)}, u32[]{:S(2)}, u32[]{:S(2)}) %collective-permute-start.3) | collective-permute-done | bytes 327712 | tf_op jit(solution)/shard_map/ppermute | solution.py:37
  169.1 4.5 %dynamic-slice_bitcast_fusion.3 = (bf16[256,512]{1,0:T(8,128)(2,1)S(1)}, bf16[256,512]{1,0:T(8,128)(2,1)S(1)}, bf16[256,512]{1,0:T(8,128)(2,1)S(1)}, bf16[256,51...) fusion(bf16[5,256,640]{2,1,0:T(8,128)(2,1)S(1)} %bitcast_dynami, ...), kind=kLoop, calls=%fused_computation.153 | loop fusion | bytes 14155824 | tf_op jit(solution)/shard_map/dynamic_slice | solution.py:60
  173.7 1.0 fusion.31
  175.6 1.0 fusion.29
  176.5 1.0 fusion.28
  177.5 0.9 fusion.27
  178.4 1.0 fusion.26
  179.4 1.0 fusion.25
  180.3 1.0 fusion.24
  181.3 1.0 fusion.23
  182.3 0.9 fusion.22
  183.2 1.0 fusion.21
  184.2 1.0 fusion.20
  185.1 1.0 fusion.19
  186.1 1.0 fusion.18
  187.0 1.0 fusion.17
  188.0 1.0 fusion.16
  189.0 1.0 fusion.15
  189.9 1.0 fusion.14
  190.9 1.0 fusion.13
  191.8 0.9 fusion.12
  192.8 0.9 fusion.11
  193.7 1.0 fusion.10
  194.7 1.0 fusion.9
  195.6 1.0 fusion.8
  196.6 0.9 fusion.7
  197.6 0.9 fusion.6
  198.5 1.0 fusion.5
  199.5 3.3 copy.9
  202.8 3.0 copy.10
  208.5 124.2 %all-reduce.3.cloned.1.call-done = f32[128,6912]{1,0:T(8,128)} async-done(((f32[128,6912]{1,0:T(8,128)}), f32[128,6912]{1,0:T(8,128)}) %all-reduce.3.cloned.1.call-update) | async-done | bytes 3538960 | tf_op jit(solution)/shard_map/psum | solution.py:119
  332.7 1.1 multiply_reduce_fusion
  333.9 1.7 broadcast_divide_fusion
  (73 shorter events, 17.2 us)
Async XLA Ops:
  6.5 326.2 %all-reduce.3.cloned.1.call-start = ((), (), s32[]{:S(2)}) async-start(), calls=%async_computation | async-start | bytes 7077888 | tf_op jit(solution)/shard_map/psum | solution.py:119
  113.1 3.1 collective-permute-start
  116.2 7.4 %collective-permute-start.1 = (bf16[128,640]{1,0:T(8,128)(2,1)S(1)}, bf16[128,640]{1,0:T(8,128)(2,1)S(1)}, u32[]{:S(2)}, u32[]{:S(2)}) collective-permute-start(bf16[128,640]{1,0:T(8,128)(2,1)S(1)} %get-tuple-element.242), channel_id=1, source_target_pairs={{0,16},{16,0},{32,48},{48,32},{64,80},{80,64},{96,112},{112,96},{1... | collective-permute-start | bytes 491528 | tf_op jit(solution)/shard_map/ppermute | solution.py:32
  123.8 36.2 %collective-permute-start.2 = (bf16[256,640]{1,0:T(8,128)(2,1)S(1)}, bf16[256,640]{1,0:T(8,128)(2,1)S(1)}, u32[]{:S(2)}, u32[]{:S(2)}) collective-permute-start(bf16[256,640]{1,0:T(8,128)(2,1)S(1)} %maximum_select_fusion), channel_id=1, source_target_pairs={{0,64},{16,80},{32,96},{48,112},{64,128},{80,144},{96,160},{112,17... | collective-permute-start | bytes 983048 | tf_op jit(solution)/shard_map/ppermute | solution.py:37
  148.2 20.4 %collective-permute-start.3 = (bf16[256,640]{1,0:T(8,128)(2,1)S(1)}, bf16[256,640]{1,0:T(8,128)(2,1)S(1)}, u32[]{:S(2)}, u32[]{:S(2)}) collective-permute-start(bf16[256,640]{1,0:T(8,128)(2,1)S(1)} %maximum_select_fusion), channel_id=1, source_target_pairs={{0,32},{16,48},{32,64},{48,80},{64,96},{80,112},{96,128},{112,144}... | collective-permute-start | bytes 983048 | tf_op jit(solution)/shard_map/ppermute | solution.py:37
  152.9 15.9 %collective-permute-start.4 = (bf16[256,640]{1,0:T(8,128)(2,1)S(1)}, bf16[256,640]{1,0:T(8,128)(2,1)S(1)}, u32[]{:S(2)}, u32[]{:S(2)}) collective-permute-start(bf16[256,640]{1,0:T(8,128)(2,1)S(1)} %maximum_select_fusion), channel_id=1, source_target_pairs={{0,480},{16,496},{32,0},{48,16},{64,32},{80,48},{96,64},{112,80},{... | collective-permute-start | bytes 983048 | tf_op jit(solution)/shard_map/ppermute | solution.py:37
  155.9 13.0 %collective-permute-start.5 = (bf16[256,640]{1,0:T(8,128)(2,1)S(1)}, bf16[256,640]{1,0:T(8,128)(2,1)S(1)}, u32[]{:S(2)}, u32[]{:S(2)}) collective-permute-start(bf16[256,640]{1,0:T(8,128)(2,1)S(1)} %maximum_select_fusion), channel_id=1, source_target_pairs={{0,448},{16,464},{32,480},{48,496},{64,0},{80,16},{96,32},{112,48}... | collective-permute-start | bytes 983048 | tf_op jit(solution)/shard_map/ppermute | solution.py:37
  205.8 0.7 copy-start.1
  205.8 2.0 copy-start
Sparse Core Ops, SparseCore 0:
  205.9 126.7 all-reduce.2
where the time goes:
time: 344 us; the launch traced here: 342 us
  waiting for transfers between devices  134 us (39%)
  blocking collectives  62 us (18%)
  between operations  36.8 us (11%)
  loops' own time  30.2 us (9%)
  matrix products  25.8 us (8%)
  local copies, waits for them, and re-layouts  25.6 us (7%)
  starting transfers between devices  18.9 us (5%)
  other arithmetic  9.09 us (3%)
    psum x1, waiting for transfers between devices, local(): summed = lax.psum(term_rows(half_rows), 'tm')  124 us
    unnamed x1, blocking collectives  32 us
    another operation x1, loops' own time, joined(): lax.fori_loop(1, lax.axis_size(axis), lambda source, state: combine(state...  30.2 us
    all_gather x2, blocking collectives, joined(): gathered = jax.tree.map(lambda a: lax.all_gather(a, axis), part)  30 us
    dot_general x27, matrix products, right_product(): lax.dot_general(left_side, right_side, (((1,), (1,)), ((), ())), preferre...  25.8 us
    ppermute x4, starting transfers between devices, shifted_2(): lax.ppermute(value, axis, [(i, (i + by) % size) for i in range(size)])  14.8 us
    dynamic_slice x17, local copies, waits for them, and re-layouts, take(): lax.dynamic_index_in_dim(a, source, 0, False)  8.78 us
    ppermute x4, waiting for transfers between devices, shifted_2(): lax.ppermute(value, axis, [(i, (i + by) % size) for i in range(size)])  8.71 us
  transfers between devices with their start and end apart: 7, of which 4 were waited for; matrix products, arithmetic and copies ran while one was open for 2% of the time, Pallas kernels for 0%

commit v1 on v0

v1 whole, which is shorter than its diff:
```python
import jax
import jax.numpy as jnp
from jax import lax
from jax.sharding import PartitionSpec as P

LMAX = 128
NLAG = 9
K_SLOTS = 3
REACH = 2


def shifted(value, axis, by):
    size = lax.axis_size(axis)
    pairs = [(i, i + by) for i in range(size) if 0 <= i + by < size]
    return lax.ppermute(value, axis, pairs)


def from_partner(value, axis, stride):
    mask = 2**stride
    pairs = [(source, source ^ mask) for source in range(lax.axis_size(axis))]
    return lax.ppermute(value, axis, pairs)


def shifted_2(value, axis, by):
    size = lax.axis_size(axis)
    return lax.ppermute(value, axis, [(i, (i + by) % size) for i in range(size)])


def local(anomalies, neighbor_ids, neighbor_counts, lag_set):
    half_rows, days_dev = anomalies.shape
    tm_size = lax.axis_size("tm")
    blocks = lax.axis_size("lon") // 2
    block_width = 2 * half_rows
    total_days = days_dev * tm_size
    values = anomalies.astype(jnp.float32)
    shard_mean = jnp.mean(values, axis=1)
    shard_square = jnp.sum(jnp.square(values - shard_mean[:, None]), axis=1)
    stats = lax.all_gather(jnp.stack([shard_mean, shard_square], 0), "tm")
    means, squares = stats[:, 0], stats[:, 1]
    point_mean = jnp.mean(means, axis=0)
    point_m2 = jnp.sum(squares, axis=0) + days_dev * jnp.sum(
        jnp.square(means - point_mean[None, :]), axis=0
    )
    spread = jnp.sqrt(point_m2 / total_days + 1e-06)
    standardized = ((values - point_mean[:, None]) / spread[:, None]).astype(jnp.bfloat16)
    margin = shifted(standardized[:, :LMAX], "tm", -1)
    extended = jnp.concatenate([standardized, margin], 1)
    partner = from_partner(extended, "lon", 0)
    lon_index = lax.axis_index("lon")
    parity = lon_index % 2
    own_block = jnp.where(
        parity == 0,
        jnp.concatenate([extended, partner], 0),
        jnp.concatenate([partner, extended], 0),
    )
    block_index = lon_index // 2
    later_blocks = []
    earlier_blocks = []
    for offset in range(1, REACH + 1):
        later_blocks.append(shifted_2(own_block, "lon", -2 * offset))
        earlier_blocks.append(shifted_2(own_block, "lon", 2 * offset))
    candidates = jnp.stack(earlier_blocks[::-1] + [own_block] + later_blocks, 0)
    block_ids = lax.dynamic_index_in_dim(neighbor_ids, block_index, 0, keepdims=False)
    live_count = lax.dynamic_index_in_dim(neighbor_counts, block_index, 0, keepdims=False)
    positions = (block_ids - block_index + REACH) % blocks

    padded = jnp.concatenate(
        [
            jnp.zeros((half_rows, LMAX), jnp.bfloat16),
            extended[:, :days_dev],
            jnp.zeros((half_rows, LMAX), jnp.bfloat16),
        ],
        1,
    )
    left_rows = []
    for lag_index in range(NLAG):
        lag_days = lag_set[lag_index]
        left_rows.append(
            jnp.concatenate(
                [
                    lax.dynamic_slice_in_dim(padded, LMAX - lag_days, days_dev + LMAX, 1),
                    lax.dynamic_slice_in_dim(extended, lag_days, days_dev, 1),
                ],
                1,
            )
        )
    left = jnp.concatenate(left_rows, 0)
    right_rows = []
    for slot_index in range(K_SLOTS):
        columns = lax.dynamic_index_in_dim(candidates, positions[slot_index], 0, keepdims=False)
        right_rows.append(jnp.concatenate([columns, columns[:, :days_dev]], 1))
    right = jnp.concatenate(right_rows, 0)
    product = lax.dot_general(
        left, right, (((1,), (1,)), ((), ())), preferred_element_type=jnp.float32
    )
    product = product.reshape(NLAG, half_rows, K_SLOTS, block_width)
    product = product.transpose(1, 2, 0, 3).reshape(half_rows, -1)

    out_rows = half_rows // tm_size
    comoment = lax.psum_scatter(product, "tm", scatter_dimension=0, tiled=True)
    comoment = comoment.reshape(out_rows, K_SLOTS, NLAG, block_width)
    denominator = 2.0 * (total_days - lag_set).astype(jnp.float32)
    is_live = jnp.arange(K_SLOTS, dtype=jnp.int32) < live_count
    linked = jnp.where(
        is_live[None, :, None, None], comoment / denominator[None, None, :, None], 0.0
    )
    squares = jnp.sum(jnp.square(linked), axis=(1, 2, 3))
    row_scale = jnp.sqrt(squares / (live_count * NLAG * block_width).astype(jnp.float32) + 1e-06)
    return (linked / row_scale[:, None, None, None]).reshape(out_rows, -1)


def solution(mesh):
    return jax.shard_map(
        local,
        mesh=mesh,
        in_specs=(P("lon", "tm"), P(), P(), P()),
        out_specs=P(("lon", "tm"), None),
        check_vma=False,
    )
```

time: 344 us -> 193 us (0.56)
  waiting for transfers between devices: 134 us -> 73.9 us
  blocking collectives: 62 us -> 23.2 us
  loops' own time: 30.2 us -> 0 us
  matrix products: 25.8 us -> 2.49 us
  between operations: 36.8 us -> 48.3 us
  local copies, waits for them, and re-layouts: 25.6 us -> 16.5 us
    psum x1 -> x0, waiting for transfers between devices: 124 us -> none  [local(): summed = lax.psum(term_rows(half_rows), 'tm')]
    reduce_scatter x0 -> x1, waiting for transfers between devices: none -> 59.5 us  [local(): comoment = lax.psum_scatter(product, 'tm', scatter_dimension=0, tiled=True)]
    unnamed x1 -> x0, blocking collectives: 32 us -> none
    another operation x1 -> x0, loops' own time: 30.2 us -> none  [joined(): lax.fori_loop(1, lax.axis_size(axis), lambda source, state: combine(state...]
    dot_general x27 -> x1, matrix products: 25.8 us -> 2.49 us  [local(): lax.dot_general(left, right, (((1,), (1,)), ((), ())), preferred_element_...]
    dynamic_slice x18 -> x1, local copies, waits for them, and re-layouts: 13.3 us -> 0.8 us  [local(): lax.dynamic_slice_in_dim(padded, LMAX - lag_days, days_dev + LMAX, 1)]
    all_gather x2 -> x1, blocking collectives: 30 us -> 23.2 us  [local(): stats = lax.all_gather(jnp.stack([shard_mean, shard_square], 0), 'tm')]
    transpose x0 -> x1, local copies, waits for them, and re-layouts: none -> 4.73 us  [local(): product = product.transpose(1, 2, 0, 3).reshape(half_rows, -1)]
  transfers between devices with their start and end apart: 7 -> 7, of which waited for: 4 -> 4; matrix products, arithmetic and copies ran while one was open for 2% -> 4% of each run, Pallas kernels for 0% -> 0%
where the time goes in v1:
time: 193 us; the launch traced here: 192 us
  waiting for transfers between devices  73.9 us (38%)
  between operations  48.3 us (25%)
  blocking collectives  23.2 us (12%)
  starting transfers between devices  18.7 us (10%)
  local copies, waits for them, and re-layouts  16.5 us (9%)
  other arithmetic  9.14 us (5%)
  matrix products  2.49 us (1%)
    reduce_scatter x1, waiting for transfers between devices, local(): comoment = lax.psum_scatter(product, 'tm', scatter_dimension=0, tiled=True)  59.5 us
    all_gather x1, blocking collectives, local(): stats = lax.all_gather(jnp.stack([shard_mean, shard_square], 0), 'tm')  23.2 us
    ppermute x4, starting transfers between devices, shifted_2(): lax.ppermute(value, axis, [(i, (i + by) % size) for i in range(size)])  14.6 us
    ppermute x4, waiting for transfers between devices, shifted_2(): lax.ppermute(value, axis, [(i, (i + by) % size) for i in range(size)])  9.68 us
    transpose x1, local copies, waits for them, and re-layouts, local(): product = product.transpose(1, 2, 0, 3).reshape(half_rows, -1)  4.73 us
    ppermute x1, waiting for transfers between devices, from_partner(): return lax.ppermute(value, axis, pairs)  4.73 us
    reshape x1, local copies, waits for them, and re-layouts, local(): product = product.reshape(NLAG, half_rows, K_SLOTS, block_width)  3.96 us
  transfers between devices with their start and end apart: 7, of which 4 were waited for; matrix products, arithmetic and copies ran while one was open for 4% of the time, Pallas kernels for 0%

profile of v1, /device:TPU:6, one launch (start us, length us, event | category | flops | bytes accessed | tf_op | source)
XLA Modules:
  0.0 192.2 jit_solution(6140438963194446724)
XLA Ops:
  6.5 0.0 reduce-scatter.4.cloned.1.call-start
  6.5 1.0 convert_reduce_fusion
  7.6 1.1 fusion.14
  8.7 23.2 %all-gather.1 = f32[16,2,128]{2,1,0:T(2,128)S(1)} all-gather(f32[1,2,128]{2,1,0:T(2,128)S(1)} %maximum_bitcast_fusion), channel_id=2, replica_groups=mesh['lon'=32,'tm'=16] {'tm'}, dimensions={0}, use_global_device_ids=true | all-gather | bytes 17408 | tf_op jit(solution)/shard_map/all_gather | solution.py:38
  31.9 1.0 fusion.16
  33.0 1.3 collective-permute-start
  34.3 1.7 fusion.34
  47.3 0.9 fusion.28
  48.3 0.8 constant_dynamic-slice_fusion.1
  49.1 0.7 fusion.33
  72.2 0.0 collective-permute-done
  72.3 2.7 %collective-permute-start.1 = (bf16[128,640]{1,0:T(8,128)(2,1)S(1)}, bf16[128,640]{1,0:T(8,128)(2,1)S(1)}, u32[]{:S(2)}, u32[]{:S(2)}) collective-permute-start(bf16[128,640]{1,0:T(8,128)(2,1)S(1)} %get-tuple-element.20), channel_id=1, source_target_pairs={{0,16},{16,0},{32,48},{48,32},{64,80},{80,64},{96,112},{112,96},{1... | collective-permute-start | bytes 491528 | tf_op jit(solution)/shard_map/ppermute | solution.py:21
  75.0 0.7 fusion.25
  75.9 0.3 fusion.24
  76.4 4.7 %collective-permute-done.1 = bf16[128,640]{1,0:T(8,128)(2,1)S(1)} collective-permute-done((bf16[128,640]{1,0:T(8,128)(2,1)S(1)}, bf16[128,640]{1,0:T(8,128)(2,1)S(1)}, u32[]{:S(2)}, u32[]{:S(2)}) %collective-permute-start.1) | collective-permute-done | bytes 163872 | tf_op jit(solution)/shard_map/ppermute | solution.py:21
  81.1 0.1 maximum_select_fusion
  81.2 3.5 %collective-permute-start.2 = (bf16[256,640]{1,0:T(8,128)(2,1)S(1)}, bf16[256,640]{1,0:T(8,128)(2,1)S(1)}, u32[]{:S(2)}, u32[]{:S(2)}) collective-permute-start(bf16[256,640]{1,0:T(8,128)(2,1)S(1)} %maximum_select_fusion), channel_id=1, source_target_pairs={{0,64},{16,80},{32,96},{48,112},{64,128},{80,144},{96,160},{112,17... | collective-permute-start | bytes 983048 | tf_op jit(solution)/shard_map/ppermute | solution.py:26
  84.7 4.3 %collective-permute-start.3 = (bf16[256,640]{1,0:T(8,128)(2,1)S(1)}, bf16[256,640]{1,0:T(8,128)(2,1)S(1)}, u32[]{:S(2)}, u32[]{:S(2)}) collective-permute-start(bf16[256,640]{1,0:T(8,128)(2,1)S(1)} %maximum_select_fusion), channel_id=1, source_target_pairs={{0,32},{16,48},{32,64},{48,80},{64,96},{80,112},{96,128},{112,144}... | collective-permute-start | bytes 983048 | tf_op jit(solution)/shard_map/ppermute | solution.py:26
  89.1 3.0 %collective-permute-start.4 = (bf16[256,640]{1,0:T(8,128)(2,1)S(1)}, bf16[256,640]{1,0:T(8,128)(2,1)S(1)}, u32[]{:S(2)}, u32[]{:S(2)}) collective-permute-start(bf16[256,640]{1,0:T(8,128)(2,1)S(1)} %maximum_select_fusion), channel_id=1, source_target_pairs={{0,480},{16,496},{32,0},{48,16},{64,32},{80,48},{96,64},{112,80},{... | collective-permute-start | bytes 983048 | tf_op jit(solution)/shard_map/ppermute | solution.py:26
  92.1 3.8 %collective-permute-start.5 = (bf16[256,640]{1,0:T(8,128)(2,1)S(1)}, bf16[256,640]{1,0:T(8,128)(2,1)S(1)}, u32[]{:S(2)}, u32[]{:S(2)}) collective-permute-start(bf16[256,640]{1,0:T(8,128)(2,1)S(1)} %maximum_select_fusion), channel_id=1, source_target_pairs={{0,448},{16,464},{32,480},{48,496},{64,0},{80,16},{96,32},{112,48}... | collective-permute-start | bytes 983048 | tf_op jit(solution)/shard_map/ppermute | solution.py:26
  95.9 0.0 collective-permute-done.2
  96.0 8.6 %collective-permute-done.3 = bf16[256,640]{1,0:T(8,128)(2,1)S(1)} collective-permute-done((bf16[256,640]{1,0:T(8,128)(2,1)S(1)}, bf16[256,640]{1,0:T(8,128)(2,1)S(1)}, u32[]{:S(2)}, u32[]{:S(2)}) %collective-permute-start.3) | collective-permute-done | bytes 327712 | tf_op jit(solution)/shard_map/ppermute | solution.py:26
  104.6 0.1 fusion.12
  104.7 1.1 collective-permute-done.4
  105.8 0.0 collective-permute-done.5
  105.9 0.1 dynamic-slice_bitcast_fusion.2
  106.1 2.5 %fusion = f32[1152,768]{1,0:T(8,128)S(1)} fusion(bf16[1152,1152]{1,0:T(8,128)(2,1)S(1)} %maximum_dynamic-update-slice_fusion, bf16[256,512]{1,0:T(8,128)(2,1)S(1)} %slice.77, bf16[256,640]{1,0:T(8,128)(2,1)S(1)} %get-tuple-element.8, bf16[256,512]{1,0:T(8,128)(2,1)S(1)} %slice.76, bf16[256,640]{1,0:T(8,128)(2,1)S(1)} %get-tuple-element.9, ...), kind=kOutput, calls=%fused_computation | convolution fusion | flops 2049048576 | bytes 7962624 | tf_op jit(solution)/shard_map/dot_general | solution.py:93
  108.6 4.0 %reshape.108 = f32[9,128,3,256]{3,2,1,0:T(4,128)} reshape(f32[1152,768]{1,0:T(8,128)S(1)} %fusion) | data formatting | bytes 7077888 | tf_op jit(solution)/shard_map/reshape | solution.py:96
  112.5 4.7 %copy.10 = f32[128,3,9,256]{0,3,2,1:T(8,128)S(1)} copy(f32[128,3,9,256]{3,1,0,2:T(4,128)} %bitcast.40) | data formatting | bytes 7077888 | tf_op jit(solution)/shard_map/transpose | solution.py:97
  117.3 3.0 %copy.12 = f32[128,6912]{1,0:T(8,128)} copy(f32[128,6912]{0,1:T(8,128)S(1)} %bitcast.41) | data formatting | bytes 7077888
  120.3 0.0 copy-start.1
  120.3 0.0 copy-start
  120.3 0.0 reduce-scatter.4.cloned.1.call-update
  120.3 0.6 copy-done.1
  120.9 0.6 dynamic_slice.72
  121.5 0.6 iota_compare_fusion
  122.2 0.1 broadcast_in_dim.23
  122.3 0.0 copy-done
  122.3 0.1 div.77
  123.0 59.5 %reduce-scatter.4.cloned.1.call-done = f32[8,6912]{1,0:T(8,128)} async-done(((f32[128,6912]{1,0:T(8,128)}), f32[8,6912]{1,0:T(8,128)}) %reduce-scatter.4.cloned.1.call-update) | async-done | bytes 221200 | tf_op jit(solution)/shard_map/reduce_scatter | solution.py:100
  182.6 1.1 multiply_reduce_fusion
  183.7 1.7 broadcast_divide_fusion
  (31 shorter events, 0.7 us)
Async XLA Ops:
  6.5 176.0 %reduce-scatter.4.cloned.1.call-start = ((), (), s32[]{:S(2)}) async-start(), calls=%async_computation.1 | async-start | bytes 3760128 | tf_op jit(solution)/shard_map/reduce_scatter | solution.py:100
  33.0 39.3 %collective-permute-start = (bf16[128,128]{1,0:T(8,128)(2,1)S(1)}, bf16[128,128]{1,0:T(8,128)(2,1)S(1)}, u32[]{:S(2)}, u32[]{:S(2)}) collective-permute-start(bf16[128,128]{1,0:T(8,128)(2,1)S(1)} %slice.74), channel_id=1, source_target_pairs={{1,0},{2,1},{3,2},{4,3},{5,4},{6,5},{7,6},{8,7},{9,8},{10,9},{11,1... | collective-permute-start | bytes 98312 | tf_op jit(solution)/shard_map/ppermute | solution.py:15
  72.3 8.8 %collective-permute-start.1 = (bf16[128,640]{1,0:T(8,128)(2,1)S(1)}, bf16[128,640]{1,0:T(8,128)(2,1)S(1)}, u32[]{:S(2)}, u32[]{:S(2)}) collective-permute-start(bf16[128,640]{1,0:T(8,128)(2,1)S(1)} %get-tuple-element.20), channel_id=1, source_target_pairs={{0,16},{16,0},{32,48},{48,32},{64,80},{80,64},{96,112},{112,96},{1... | collective-permute-start | bytes 491528 | tf_op jit(solution)/shard_map/ppermute | solution.py:21
  81.2 14.8 %collective-permute-start.2 = (bf16[256,640]{1,0:T(8,128)(2,1)S(1)}, bf16[256,640]{1,0:T(8,128)(2,1)S(1)}, u32[]{:S(2)}, u32[]{:S(2)}) collective-permute-start(bf16[256,640]{1,0:T(8,128)(2,1)S(1)} %maximum_select_fusion), channel_id=1, source_target_pairs={{0,64},{16,80},{32,96},{48,112},{64,128},{80,144},{96,160},{112,17... | collective-permute-start | bytes 983048 | tf_op jit(solution)/shard_map/ppermute | solution.py:26
  84.7 19.9 %collective-permute-start.3 = (bf16[256,640]{1,0:T(8,128)(2,1)S(1)}, bf16[256,640]{1,0:T(8,128)(2,1)S(1)}, u32[]{:S(2)}, u32[]{:S(2)}) collective-permute-start(bf16[256,640]{1,0:T(8,128)(2,1)S(1)} %maximum_select_fusion), channel_id=1, source_target_pairs={{0,32},{16,48},{32,64},{48,80},{64,96},{80,112},{96,128},{112,144}... | collective-permute-start | bytes 983048 | tf_op jit(solution)/shard_map/ppermute | solution.py:26
  89.1 16.7 %collective-permute-start.4 = (bf16[256,640]{1,0:T(8,128)(2,1)S(1)}, bf16[256,640]{1,0:T(8,128)(2,1)S(1)}, u32[]{:S(2)}, u32[]{:S(2)}) collective-permute-start(bf16[256,640]{1,0:T(8,128)(2,1)S(1)} %maximum_select_fusion), channel_id=1, source_target_pairs={{0,480},{16,496},{32,0},{48,16},{64,32},{80,48},{96,64},{112,80},{... | collective-permute-start | bytes 983048 | tf_op jit(solution)/shard_map/ppermute | solution.py:26
  92.1 13.7 %collective-permute-start.5 = (bf16[256,640]{1,0:T(8,128)(2,1)S(1)}, bf16[256,640]{1,0:T(8,128)(2,1)S(1)}, u32[]{:S(2)}, u32[]{:S(2)}) collective-permute-start(bf16[256,640]{1,0:T(8,128)(2,1)S(1)} %maximum_select_fusion), channel_id=1, source_target_pairs={{0,448},{16,464},{32,480},{48,496},{64,0},{80,16},{96,32},{112,48}... | collective-permute-start | bytes 983048 | tf_op jit(solution)/shard_map/ppermute | solution.py:26
  120.3 0.7 copy-start.1
  120.3 2.0 %copy-start = (s32[9]{0:T(128)S(1)}, s32[9]{0:T(128)}, u32[]{:S(2)}) copy-start(s32[9]{0:T(128)} %param.7) | copy-start | bytes 112
Sparse Core Ops, SparseCore 0:
  120.4 62.0 reduce-scatter.3

commit v2 on v1

v2 whole, which is shorter than its diff:
```python
import jax
import jax.numpy as jnp
from jax import lax
from jax.sharding import PartitionSpec as P

LMAX = 128
NLAG = 9
K_SLOTS = 3
REACH = 2


def shifted(value, axis, by):
    size = lax.axis_size(axis)
    pairs = [(i, i + by) for i in range(size) if 0 <= i + by < size]
    return lax.ppermute(value, axis, pairs)


def from_partner(value, axis, stride):
    mask = 2**stride
    pairs = [(source, source ^ mask) for source in range(lax.axis_size(axis))]
    return lax.ppermute(value, axis, pairs)


def shifted_2(value, axis, by):
    size = lax.axis_size(axis)
    return lax.ppermute(value, axis, [(i, (i + by) % size) for i in range(size)])


def local(anomalies, neighbor_ids, neighbor_counts, lag_set):
    half_rows, days_dev = anomalies.shape
    tm_size = lax.axis_size("tm")
    lon_size = lax.axis_size("lon")
    blocks = lon_size // 2
    block_width = 2 * half_rows
    total_days = days_dev * tm_size
    margin = shifted(anomalies[:, :LMAX], "tm", -1)
    extended = jnp.concatenate([anomalies, margin], 1)
    lon_index = lax.axis_index("lon")
    parity = lon_index % 2
    block_index = lon_index // 2
    reach = 2 * REACH + 1
    halves = []
    for offset in range(-reach, reach + 1):
        if offset == 0:
            halves.append(extended)
            continue
        pairs = []
        for target in range(lon_size):
            low = -2 * REACH - target % 2
            if low <= offset <= low + 2 * (2 * REACH + 1) - 1:
                pairs.append(((target + offset) % lon_size, target))
        halves.append(lax.ppermute(extended, "lon", pairs))
    halves = jnp.stack(halves, 0)
    block_ids = lax.dynamic_index_in_dim(neighbor_ids, block_index, 0, keepdims=False)
    live_count = lax.dynamic_index_in_dim(neighbor_counts, block_index, 0, keepdims=False)
    positions = (block_ids - block_index + REACH) % blocks
    slot_blocks = []
    for slot_index in range(K_SLOTS):
        first = 2 * (positions[slot_index] - REACH) - parity + reach
        pair = lax.dynamic_slice_in_dim(halves, first, 2, 0)
        slot_blocks.append(pair.reshape(block_width, days_dev + LMAX))
    raw = jnp.concatenate([extended] + slot_blocks, 0)
    values = raw.astype(jnp.float32)
    shard_mean = jnp.mean(values[:, :days_dev], axis=1)
    shard_square = jnp.sum(jnp.square(values[:, :days_dev] - shard_mean[:, None]), axis=1)
    stats = lax.all_gather(jnp.stack([shard_mean, shard_square], 0), "tm")
    means, squares = stats[:, 0], stats[:, 1]
    point_mean = jnp.mean(means, axis=0)
    point_m2 = jnp.sum(squares, axis=0) + days_dev * jnp.sum(
        jnp.square(means - point_mean[None, :]), axis=0
    )
    spread = jnp.sqrt(point_m2 / total_days + 1e-06)
    day = lax.broadcasted_iota(jnp.int32, (1, days_dev + LMAX), 1)
    inside = (day < days_dev) | (lax.axis_index("tm") < tm_size - 1)
    standardized = jnp.where(
        inside, (values - point_mean[:, None]) / spread[:, None], 0.0
    ).astype(jnp.bfloat16)
    own = standardized[:half_rows]

    padded = jnp.concatenate(
        [
            jnp.zeros((half_rows, LMAX), jnp.bfloat16),
            own[:, :days_dev],
            jnp.zeros((half_rows, LMAX), jnp.bfloat16),
        ],
        1,
    )
    left_rows = []
    for lag_index in range(NLAG):
        lag_days = lag_set[lag_index]
        left_rows.append(
            jnp.concatenate(
                [
                    lax.dynamic_slice_in_dim(padded, LMAX - lag_days, days_dev + LMAX, 1),
                    lax.dynamic_slice_in_dim(own, lag_days, days_dev, 1),
                ],
                1,
            )
        )
    left = jnp.stack(left_rows, 1).reshape(half_rows * NLAG, -1)
    right_rows = []
    for slot_index in range(K_SLOTS):
        columns = standardized[half_rows + slot_index * block_width:][:block_width]
        right_rows.append(jnp.concatenate([columns, columns[:, :days_dev]], 1))
    right = jnp.concatenate(right_rows, 0)
    product = lax.dot_general(
        left, right, (((1,), (1,)), ((), ())), preferred_element_type=jnp.float32
    )

    out_rows = half_rows // tm_size
    comoment = lax.psum_scatter(product, "tm", scatter_dimension=0, tiled=True)
    comoment = comoment.reshape(out_rows, NLAG, K_SLOTS, block_width).transpose(0, 2, 1, 3)
    denominator = 2.0 * (total_days - lag_set).astype(jnp.float32)
    is_live = jnp.arange(K_SLOTS, dtype=jnp.int32) < live_count
    linked = jnp.where(
        is_live[None, :, None, None], comoment / denominator[None, None, :, None], 0.0
    )
    squares = jnp.sum(jnp.square(linked), axis=(1, 2, 3))
    row_scale = jnp.sqrt(squares / (live_count * NLAG * block_width).astype(jnp.float32) + 1e-06)
    return (linked / row_scale[:, None, None, None]).reshape(out_rows, -1)


def solution(mesh):
    return jax.shard_map(
        local,
        mesh=mesh,
        in_specs=(P("lon", "tm"), P(), P(), P()),
        out_specs=P(("lon", "tm"), None),
        check_vma=False,
    )
```

time: 193 us -> 197 us (1.021)
  starting transfers between devices: 18.7 us -> 36.2 us
  waiting for transfers between devices: 73.9 us -> 64.4 us
  other arithmetic: 9.14 us -> 3.67 us
  between operations: 48.3 us -> 44.5 us
  matrix products: 2.49 us -> 5.45 us
  local copies, waits for them, and re-layouts: 16.5 us -> 18.7 us
    ppermute x5 -> x10, starting transfers between devices: 17.4 us -> 34.9 us  [local(): halves.append(lax.ppermute(extended, 'lon', pairs))]
    ppermute x5 -> x10, waiting for transfers between devices: 14.4 us -> 3.83 us  [local(): halves.append(lax.ppermute(extended, 'lon', pairs))]
    transpose x1 -> x0, local copies, waits for them, and re-layouts: 4.73 us -> none  [local(): product = product.transpose(1, 2, 0, 3).reshape(half_rows, -1)]
    another operation x2 -> x4, local copies, waits for them, and re-layouts: 0.05 us -> 3.81 us  [the longest x1 3.78 us: local(): left = jnp.stack(left_rows, 1).reshape(half_rows * NLAG, -1)]
    dot_general x1, matrix products: 2.49 us -> 5.45 us  [local(): lax.dot_general(left, right, (((1,), (1,)), ((), ())), preferred_element_...]
    unnamed x8 -> x15, local copies, waits for them, and re-layouts: 3.75 us -> 1.77 us
    reshape x1 -> x2, local copies, waits for them, and re-layouts: 3.96 us -> 5.39 us  [the longest x1 4.34 us: local(): left = jnp.stack(left_rows, 1).reshape(half_rows * NLAG, -1)]
  transfers between devices with their start and end apart: 7 -> 12, of which waited for: 4 -> 3; matrix products, arithmetic and copies ran while one was open for 4% -> 3% of each run, Pallas kernels for 0% -> 0%
where the time goes in v2:
time: 197 us; the launch traced here: 196 us
  waiting for transfers between devices  64.4 us (33%)
  between operations  44.5 us (23%)
  starting transfers between devices  36.2 us (18%)
  blocking collectives  22.7 us (12%)
  local copies, waits for them, and re-layouts  18.7 us (9%)
  matrix products  5.45 us (3%)
  other arithmetic  3.67 us (2%)
    reduce_scatter x1, waiting for transfers between devices, local(): comoment = lax.psum_scatter(product, 'tm', scatter_dimension=0, tiled=True)  60.5 us
    ppermute x10, starting transfers between devices, local(): halves.append(lax.ppermute(extended, 'lon', pairs))  34.9 us
    all_gather x1, blocking collectives, local(): stats = lax.all_gather(jnp.stack([shard_mean, shard_square], 0), 'tm')  22.7 us
    dot_general x1, matrix products, local(): lax.dot_general(left, right, (((1,), (1,)), ((), ())), preferred_element_...  5.45 us
    reshape x1, local copies, waits for them, and re-layouts, local(): left = jnp.stack(left_rows, 1).reshape(half_rows * NLAG, -1)  4.34 us
  transfers between devices with their start and end apart: 12, of which 3 were waited for; matrix products, arithmetic and copies ran while one was open for 3% of the time, Pallas kernels for 0%

profile of v2, /device:TPU:6, one launch (start us, length us, event | category | flops | bytes accessed | tf_op | source)
XLA Modules:
  0.0 195.6 jit_solution(2648676610808467270)
XLA Ops:
  6.5 0.8 slice.81
  7.3 1.3 collective-permute-start
  8.6 0.9 constant_dynamic-update-slice_fusion.1
  9.5 0.9 fusion.26
  10.4 1.7 fusion.31
  12.1 0.0 collective-permute-done
  12.1 1.3 collective-permute-start.1
  13.4 0.7 fusion.32
  44.1 3.5 %collective-permute-start.2 = (bf16[128,640]{1,0:T(8,128)(2,1)S(1)}, bf16[128,640]{1,0:T(8,128)(2,1)S(1)}, u32[]{:S(2)}, u32[]{:S(2)}) collective-permute-start(bf16[128,640]{1,0:T(8,128)(2,1)S(1)} %constant_dynamic-update-slice_fusion), channel_id=1, source_target_pairs={{448,0},{464,16},{480,32},{496,48},{0,64},{16,80},{32,96},{48,112}... | collective-permute-start | bytes 491528 | tf_op jit(solution)/shard_map/ppermute | solution.py:52
  47.5 6.6 %collective-permute-start.3 = (bf16[128,640]{1,0:T(8,128)(2,1)S(1)}, bf16[128,640]{1,0:T(8,128)(2,1)S(1)}, u32[]{:S(2)}, u32[]{:S(2)}) collective-permute-start(bf16[128,640]{1,0:T(8,128)(2,1)S(1)} %constant_dynamic-update-slice_fusion), channel_id=1, source_target_pairs={{464,0},{480,16},{496,32},{0,48},{16,64},{32,80},{48,96},{64,112},... | collective-permute-start | bytes 491528 | tf_op jit(solution)/shard_map/ppermute | solution.py:52
  54.1 5.5 %collective-permute-start.4 = (bf16[128,640]{1,0:T(8,128)(2,1)S(1)}, bf16[128,640]{1,0:T(8,128)(2,1)S(1)}, u32[]{:S(2)}, u32[]{:S(2)}) collective-permute-start(bf16[128,640]{1,0:T(8,128)(2,1)S(1)} %constant_dynamic-update-slice_fusion), channel_id=1, source_target_pairs={{480,0},{496,16},{0,32},{16,48},{32,64},{48,80},{64,96},{80,112},{... | collective-permute-start | bytes 491528 | tf_op jit(solution)/shard_map/ppermute | solution.py:52
  59.7 1.9 collective-permute-start.5
  61.6 0.0 collective-permute-done.1
  61.6 3.9 %collective-permute-start.6 = (bf16[128,640]{1,0:T(8,128)(2,1)S(1)}, bf16[128,640]{1,0:T(8,128)(2,1)S(1)}, u32[]{:S(2)}, u32[]{:S(2)}) collective-permute-start(bf16[128,640]{1,0:T(8,128)(2,1)S(1)} %constant_dynamic-update-slice_fusion), channel_id=1, source_target_pairs={{16,0},{32,16},{48,32},{64,48},{80,64},{96,80},{112,96},{128,112},... | collective-permute-start | bytes 491528 | tf_op jit(solution)/shard_map/ppermute | solution.py:52
  65.6 0.0 collective-permute-done.2
  65.6 1.9 collective-permute-start.7
  67.5 0.0 collective-permute-done.3
  67.6 4.5 %collective-permute-start.8 = (bf16[128,640]{1,0:T(8,128)(2,1)S(1)}, bf16[128,640]{1,0:T(8,128)(2,1)S(1)}, u32[]{:S(2)}, u32[]{:S(2)}) collective-permute-start(bf16[128,640]{1,0:T(8,128)(2,1)S(1)} %constant_dynamic-update-slice_fusion), channel_id=1, source_target_pairs={{48,0},{64,16},{80,32},{96,48},{112,64},{128,80},{144,96},{160,112... | collective-permute-start | bytes 491528 | tf_op jit(solution)/shard_map/ppermute | solution.py:52
  72.1 0.0 collective-permute-done.4
  72.1 3.0 %collective-permute-start.9 = (bf16[128,640]{1,0:T(8,128)(2,1)S(1)}, bf16[128,640]{1,0:T(8,128)(2,1)S(1)}, u32[]{:S(2)}, u32[]{:S(2)}) collective-permute-start(bf16[128,640]{1,0:T(8,128)(2,1)S(1)} %constant_dynamic-update-slice_fusion), channel_id=1, source_target_pairs={{64,0},{80,16},{96,32},{112,48},{128,64},{144,80},{160,96},{176,11... | collective-permute-start | bytes 491528 | tf_op jit(solution)/shard_map/ppermute | solution.py:52
  75.2 2.8 %collective-permute-start.10 = (bf16[128,640]{1,0:T(8,128)(2,1)S(1)}, bf16[128,640]{1,0:T(8,128)(2,1)S(1)}, u32[]{:S(2)}, u32[]{:S(2)}) collective-permute-start(bf16[128,640]{1,0:T(8,128)(2,1)S(1)} %constant_dynamic-update-slice_fusion), channel_id=1, source_target_pairs={{80,0},{112,32},{144,64},{176,96},{208,128},{240,160},{272,192},{3... | collective-permute-start | bytes 491528 | tf_op jit(solution)/shard_map/ppermute | solution.py:52
  78.0 0.0 collective-permute-done.6
  78.0 0.0 collective-permute-done.7
  78.1 2.3 %collective-permute-done.9 = bf16[128,640]{1,0:T(8,128)(2,1)S(1)} collective-permute-done((bf16[128,640]{1,0:T(8,128)(2,1)S(1)}, bf16[128,640]{1,0:T(8,128)(2,1)S(1)}, u32[]{:S(2)}, u32[]{:S(2)}) %collective-permute-start.9) | collective-permute-done | bytes 163872 | tf_op jit(solution)/shard_map/ppermute | solution.py:52
  80.4 1.5 collective-permute-done.10
  82.0 0.1 constant_dynamic-slice_fusion.20
  82.1 0.2 maximum_convert_fusion
  82.3 0.2 slice_reduce_fusion
  82.5 0.4 multiply_reduce_fusion
  82.9 22.7 %all-gather.1 = f32[16,2,896]{2,1,0:T(2,128)S(1)} all-gather(f32[1,2,896]{2,1,0:T(2,128)S(1)} %maximum_bitcast_fusion.9), channel_id=2, replica_groups=mesh['lon'=32,'tm'=16] {'tm'}, dimensions={0}, use_global_device_ids=true | all-gather | bytes 121856 | tf_op jit(solution)/shard_map/all_gather | solution.py:66
  105.6 0.1 slice_reduce_fusion.2
  105.8 0.4 select_convert_fusion
  106.3 0.8 fusion.29
  107.1 0.9 fusion.30
  108.1 0.8 constant_dynamic-slice_fusion.1
  108.9 0.6 constant_dynamic-slice_fusion
  109.9 3.8 %copy.16 = bf16[128,9,1152]{2,1,0:T(8,128)(2,1)} copy(bf16[128,9,1152]{2,0,1:T(8,128)(2,1)S(1)} %fusion.20) | data formatting | bytes 5308416 | tf_op jit(solution)/shard_map/stack | solution.py:100
  113.6 4.3 %reshape.81 = bf16[1152,1152]{1,0:T(8,128)(2,1)S(1)} reshape(bf16[128,9,1152]{2,1,0:T(8,128)(2,1)} %copy.16) | data formatting | bytes 5308416 | tf_op jit(solution)/shard_map/reshape | solution.py:100
  118.0 5.4 %fusion = f32[1152,768]{1,0:T(8,128)} fusion(bf16[1152,1152]{1,0:T(8,128)(2,1)S(1)} %reshape.81, bf16[256,512]{1,0:T(8,128)(2,1)} %get-tuple-element.16, bf16[256,640]{1,0:T(8,128)(2,1)S(1)} %get-tuple-element.13, bf16[256,512]{1,0:T(8,128)(2,1)} %get-tuple-element.17, bf16[256,640]{1,0:T(8,128)(2,1)} %get-tuple-element.14, ...), kind=kOutput, calls=%fused_computation.2 | convolution fusion | flops 2049048576 | bytes 7962624 | tf_op jit(solution)/shard_map/dot_general | solution.py:106
  123.4 0.0 reduce-scatter.2.cloned.1.call-update
  123.5 0.6 copy-done.1
  124.1 0.6 dynamic_slice.71
  125.3 0.7 iota_compare_fusion.1
  126.0 60.5 %reduce-scatter.2.cloned.1.call-done = f32[72,768]{1,0:T(8,128)} async-done(((f32[1152,768]{1,0:T(8,128)}), f32[72,768]{1,0:T(8,128)}) %reduce-scatter.2.cloned.1.call-update) | async-done | bytes 221200 | tf_op jit(solution)/shard_map/reduce_scatter | solution.py:111
  186.6 1.0 reshape.82
  187.6 0.3 multiply_reduce_fusion.1
  187.9 0.1 divide_bitcast_fusion
  188.0 0.7 copy.17
  (42 shorter events, 0.7 us)
Async XLA Ops:
  6.5 180.0 %reduce-scatter.2.cloned.1.call-start = ((), (), s32[]{:S(2)}) async-start(), calls=%async_computation.1 | async-start | bytes 3760128 | tf_op jit(solution)/shard_map/reduce_scatter | solution.py:111
  7.3 4.8 %collective-permute-start = (bf16[128,128]{1,0:T(8,128)(2,1)S(1)}, bf16[128,128]{1,0:T(8,128)(2,1)S(1)}, u32[]{:S(2)}, u32[]{:S(2)}) collective-permute-start(bf16[128,128]{1,0:T(8,128)(2,1)S(1)} %slice.81), channel_id=1, source_target_pairs={{1,0},{2,1},{3,2},{4,3},{5,4},{6,5},{7,6},{8,7},{9,8},{10,9},{11,1... | collective-permute-start | bytes 98312 | tf_op jit(solution)/shard_map/ppermute | solution.py:15
  12.1 49.5 %collective-permute-start.1 = (bf16[128,640]{1,0:T(8,128)(2,1)S(1)}, bf16[128,640]{1,0:T(8,128)(2,1)S(1)}, u32[]{:S(2)}, u32[]{:S(2)}) collective-permute-start(bf16[128,640]{1,0:T(8,128)(2,1)S(1)} %constant_dynamic-update-slice_fusion), channel_id=1, source_target_pairs={{448,16},{480,48},{0,80},{32,112},{64,144},{96,176},{128,208},{160... | collective-permute-start | bytes 491528 | tf_op jit(solution)/shard_map/ppermute | solution.py:52
  44.1 21.5 %collective-permute-start.2 = (bf16[128,640]{1,0:T(8,128)(2,1)S(1)}, bf16[128,640]{1,0:T(8,128)(2,1)S(1)}, u32[]{:S(2)}, u32[]{:S(2)}) collective-permute-start(bf16[128,640]{1,0:T(8,128)(2,1)S(1)} %constant_dynamic-update-slice_fusion), channel_id=1, source_target_pairs={{448,0},{464,16},{480,32},{496,48},{0,64},{16,80},{32,96},{48,112}... | collective-permute-start | bytes 491528 | tf_op jit(solution)/shard_map/ppermute | solution.py:52
  47.5 20.0 %collective-permute-start.3 = (bf16[128,640]{1,0:T(8,128)(2,1)S(1)}, bf16[128,640]{1,0:T(8,128)(2,1)S(1)}, u32[]{:S(2)}, u32[]{:S(2)}) collective-permute-start(bf16[128,640]{1,0:T(8,128)(2,1)S(1)} %constant_dynamic-update-slice_fusion), channel_id=1, source_target_pairs={{464,0},{480,16},{496,32},{0,48},{16,64},{32,80},{48,96},{64,112},... | collective-permute-start | bytes 491528 | tf_op jit(solution)/shard_map/ppermute | solution.py:52
  54.1 17.9 %collective-permute-start.4 = (bf16[128,640]{1,0:T(8,128)(2,1)S(1)}, bf16[128,640]{1,0:T(8,128)(2,1)S(1)}, u32[]{:S(2)}, u32[]{:S(2)}) collective-permute-start(bf16[128,640]{1,0:T(8,128)(2,1)S(1)} %constant_dynamic-update-slice_fusion), channel_id=1, source_target_pairs={{480,0},{496,16},{0,32},{16,48},{32,64},{48,80},{64,96},{80,112},{... | collective-permute-start | bytes 491528 | tf_op jit(solution)/shard_map/ppermute | solution.py:52
  59.7 15.5 %collective-permute-start.5 = (bf16[128,640]{1,0:T(8,128)(2,1)S(1)}, bf16[128,640]{1,0:T(8,128)(2,1)S(1)}, u32[]{:S(2)}, u32[]{:S(2)}) collective-permute-start(bf16[128,640]{1,0:T(8,128)(2,1)S(1)} %constant_dynamic-update-slice_fusion), channel_id=1, source_target_pairs={{496,0},{0,16},{16,32},{32,48},{48,64},{64,80},{80,96},{96,112},{1... | collective-permute-start | bytes 491528 | tf_op jit(solution)/shard_map/ppermute | solution.py:52
  61.6 16.4 %collective-permute-start.6 = (bf16[128,640]{1,0:T(8,128)(2,1)S(1)}, bf16[128,640]{1,0:T(8,128)(2,1)S(1)}, u32[]{:S(2)}, u32[]{:S(2)}) collective-permute-start(bf16[128,640]{1,0:T(8,128)(2,1)S(1)} %constant_dynamic-update-slice_fusion), channel_id=1, source_target_pairs={{16,0},{32,16},{48,32},{64,48},{80,64},{96,80},{112,96},{128,112},... | collective-permute-start | bytes 491528 | tf_op jit(solution)/shard_map/ppermute | solution.py:52
  65.6 12.5 %collective-permute-start.7 = (bf16[128,640]{1,0:T(8,128)(2,1)S(1)}, bf16[128,640]{1,0:T(8,128)(2,1)S(1)}, u32[]{:S(2)}, u32[]{:S(2)}) collective-permute-start(bf16[128,640]{1,0:T(8,128)(2,1)S(1)} %constant_dynamic-update-slice_fusion), channel_id=1, source_target_pairs={{32,0},{48,16},{64,32},{80,48},{96,64},{112,80},{128,96},{144,112}... | collective-permute-start | bytes 491528 | tf_op jit(solution)/shard_map/ppermute | solution.py:52
  67.6 10.5 %collective-permute-start.8 = (bf16[128,640]{1,0:T(8,128)(2,1)S(1)}, bf16[128,640]{1,0:T(8,128)(2,1)S(1)}, u32[]{:S(2)}, u32[]{:S(2)}) collective-permute-start(bf16[128,640]{1,0:T(8,128)(2,1)S(1)} %constant_dynamic-update-slice_fusion), channel_id=1, source_target_pairs={{48,0},{64,16},{80,32},{96,48},{112,64},{128,80},{144,96},{160,112... | collective-permute-start | bytes 491528 | tf_op jit(solution)/shard_map/ppermute | solution.py:52
  72.1 8.3 %collective-permute-start.9 = (bf16[128,640]{1,0:T(8,128)(2,1)S(1)}, bf16[128,640]{1,0:T(8,128)(2,1)S(1)}, u32[]{:S(2)}, u32[]{:S(2)}) collective-permute-start(bf16[128,640]{1,0:T(8,128)(2,1)S(1)} %constant_dynamic-update-slice_fusion), channel_id=1, source_target_pairs={{64,0},{80,16},{96,32},{112,48},{128,64},{144,80},{160,96},{176,11... | collective-permute-start | bytes 491528 | tf_op jit(solution)/shard_map/ppermute | solution.py:52
  75.2 6.8 %collective-permute-start.10 = (bf16[128,640]{1,0:T(8,128)(2,1)S(1)}, bf16[128,640]{1,0:T(8,128)(2,1)S(1)}, u32[]{:S(2)}, u32[]{:S(2)}) collective-permute-start(bf16[128,640]{1,0:T(8,128)(2,1)S(1)} %constant_dynamic-update-slice_fusion), channel_id=1, source_target_pairs={{80,0},{112,32},{144,64},{176,96},{208,128},{240,160},{272,192},{3... | collective-permute-start | bytes 491528 | tf_op jit(solution)/shard_map/ppermute | solution.py:52
  123.4 0.7 copy-start.1
  123.4 2.6 %copy-start = (s32[9]{0:T(128)S(1)}, s32[9]{0:T(128)}, u32[]{:S(2)}) copy-start(s32[9]{0:T(128)} %param.7) | copy-start | bytes 112
Sparse Core Ops, SparseCore 0:
  123.6 62.9 reduce-scatter.1

commit v3 on v2

--- a/solution.py
+++ b/solution.py
@@ -26,6 +26,10 @@
     return lax.ppermute(value, axis, [(i, (i + by) % size) for i in range(size)])
 
 
+def dslice(value, start, size, axis):
+    return lax.dynamic_slice_in_dim(value, start, size, axis, allow_negative_indices=False)
+
+
 def local(anomalies, neighbor_ids, neighbor_counts, lag_set):
     half_rows, days_dev = anomalies.shape
     tm_size = lax.axis_size("tm")
@@ -36,8 +40,8 @@
     margin = shifted(anomalies[:, :LMAX], "tm", -1)
     extended = jnp.concatenate([anomalies, margin], 1)
     lon_index = lax.axis_index("lon")
-    parity = lon_index % 2
-    block_index = lon_index // 2
+    parity = lax.rem(lon_index, 2)
+    block_index = lax.div(lon_index, 2)
     reach = 2 * REACH + 1
     halves = []
     for offset in range(-reach, reach + 1):
@@ -51,13 +55,13 @@
                 pairs.append(((target + offset) % lon_size, target))
         halves.append(lax.ppermute(extended, "lon", pairs))
     halves = jnp.stack(halves, 0)
-    block_ids = lax.dynamic_index_in_dim(neighbor_ids, block_index, 0, keepdims=False)
-    live_count = lax.dynamic_index_in_dim(neighbor_counts, block_index, 0, keepdims=False)
-    positions = (block_ids - block_index + REACH) % blocks
+    block_ids = dslice(neighbor_ids, block_index, 1, 0)[0]
+    live_count = dslice(neighbor_counts, block_index, 1, 0)[0]
+    positions = lax.rem(block_ids - block_index + (REACH + blocks), blocks)
+    firsts = 2 * positions + (reach - 2 * REACH) - parity
     slot_blocks = []
     for slot_index in range(K_SLOTS):
-        first = 2 * (positions[slot_index] - REACH) - parity + reach
-        pair = lax.dynamic_slice_in_dim(halves, first, 2, 0)
+        pair = dslice(halves, firsts[slot_index], 2, 0)
         slot_blocks.append(pair.reshape(block_width, days_dev + LMAX))
     raw = jnp.concatenate([extended] + slot_blocks, 0)
     values = raw.astype(jnp.float32)
@@ -85,14 +89,14 @@
         ],
         1,
     )
+    backs = LMAX - lag_set
     left_rows = []
     for lag_index in range(NLAG):
-        lag_days = lag_set[lag_index]
         left_rows.append(
             jnp.concatenate(
                 [
-                    lax.dynamic_slice_in_dim(padded, LMAX - lag_days, days_dev + LMAX, 1),
-                    lax.dynamic_slice_in_dim(own, lag_days, days_dev, 1),
+                    dslice(padded, backs[lag_index], days_dev + LMAX, 1),
+                    dslice(own, lag_set[lag_index], days_dev, 1),
                 ],
                 1,
             )

time: 197 us -> 181 us (0.919)
  between operations: 44.5 us -> 14.5 us
  local copies, waits for them, and re-layouts: 18.7 us -> 32.3 us
    dynamic_slice x4, local copies, waits for them, and re-layouts: 2.11 us -> 15.1 us  [dslice(): lax.dynamic_slice_in_dim(value, start, size, axis, allow_negative_indices...]
  transfers between devices with their start and end apart: 12 -> 12, of which waited for: 3 -> 3; matrix products, arithmetic and copies ran while one was open for 3% -> 4% of each run, Pallas kernels for 0% -> 0%
where the time goes in v3:
time: 181 us; the launch traced here: 180 us
  waiting for transfers between devices  64.2 us (35%)
  starting transfers between devices  36.2 us (20%)
  local copies, waits for them, and re-layouts  32.3 us (18%)
  blocking collectives  22.7 us (13%)
  between operations  14.5 us (8%)
  matrix products  5.45 us (3%)
  other arithmetic  4.33 us (2%)
    reduce_scatter x1, waiting for transfers between devices, local(): comoment = lax.psum_scatter(product, 'tm', scatter_dimension=0, tiled=True)  60.4 us
    ppermute x10, starting transfers between devices, local(): halves.append(lax.ppermute(extended, 'lon', pairs))  34.9 us
    all_gather x1, blocking collectives, local(): stats = lax.all_gather(jnp.stack([shard_mean, shard_square], 0), 'tm')  22.7 us
    dynamic_slice x4, local copies, waits for them, and re-layouts, dslice(): lax.dynamic_slice_in_dim(value, start, size, axis, allow_negative_indices...  15.1 us
    dot_general x1, matrix products, local(): lax.dot_general(left, right, (((1,), (1,)), ((), ())), preferred_element_...  5.45 us
    reshape x1, local copies, waits for them, and re-layouts, local(): left = jnp.stack(left_rows, 1).reshape(half_rows * NLAG, -1)  4.34 us
    ppermute x10, waiting for transfers between devices, local(): halves.append(lax.ppermute(extended, 'lon', pairs))  3.83 us
    another operation x1, local copies, waits for them, and re-layouts, local(): left = jnp.stack(left_rows, 1).reshape(half_rows * NLAG, -1)  3.78 us
  transfers between devices with their start and end apart: 12, of which 3 were waited for; matrix products, arithmetic and copies ran while one was open for 4% of the time, Pallas kernels for 0%

profile of v3, /device:TPU:6, one launch (start us, length us, event | category | flops | bytes accessed | tf_op | source)
XLA Modules:
  0.0 179.7 jit_solution(12102468052385990805)
XLA Ops:
  6.5 0.8 slice.108
  7.3 1.3 collective-permute-start
  8.6 0.9 constant_dynamic-update-slice_fusion.1
  9.5 0.7 broadcast_subtract_fusion
  10.2 1.7 fusion.35
  11.8 0.9 fusion.26
  12.7 0.6 fusion.36
  13.3 0.0 collective-permute-done
  13.3 1.3 collective-permute-start.1
  14.7 0.7 fusion.34
  15.3 3.5 %collective-permute-start.2 = (bf16[128,640]{1,0:T(8,128)(2,1)S(1)}, bf16[128,640]{1,0:T(8,128)(2,1)S(1)}, u32[]{:S(2)}, u32[]{:S(2)}) collective-permute-start(bf16[128,640]{1,0:T(8,128)(2,1)S(1)} %constant_dynamic-update-slice_fusion), channel_id=1, source_target_pairs={{448,0},{464,16},{480,32},{496,48},{0,64},{16,80},{32,96},{48,112}... | collective-permute-start | bytes 491528 | tf_op jit(solution)/shard_map/ppermute | solution.py:56
  18.8 6.6 %collective-permute-start.3 = (bf16[128,640]{1,0:T(8,128)(2,1)S(1)}, bf16[128,640]{1,0:T(8,128)(2,1)S(1)}, u32[]{:S(2)}, u32[]{:S(2)}) collective-permute-start(bf16[128,640]{1,0:T(8,128)(2,1)S(1)} %constant_dynamic-update-slice_fusion), channel_id=1, source_target_pairs={{464,0},{480,16},{496,32},{0,48},{16,64},{32,80},{48,96},{64,112},... | collective-permute-start | bytes 491528 | tf_op jit(solution)/shard_map/ppermute | solution.py:56
  25.4 5.5 %collective-permute-start.4 = (bf16[128,640]{1,0:T(8,128)(2,1)S(1)}, bf16[128,640]{1,0:T(8,128)(2,1)S(1)}, u32[]{:S(2)}, u32[]{:S(2)}) collective-permute-start(bf16[128,640]{1,0:T(8,128)(2,1)S(1)} %constant_dynamic-update-slice_fusion), channel_id=1, source_target_pairs={{480,0},{496,16},{0,32},{16,48},{32,64},{48,80},{64,96},{80,112},{... | collective-permute-start | bytes 491528 | tf_op jit(solution)/shard_map/ppermute | solution.py:56
  31.0 1.9 %collective-permute-start.5 = (bf16[128,640]{1,0:T(8,128)(2,1)S(1)}, bf16[128,640]{1,0:T(8,128)(2,1)S(1)}, u32[]{:S(2)}, u32[]{:S(2)}) collective-permute-start(bf16[128,640]{1,0:T(8,128)(2,1)S(1)} %constant_dynamic-update-slice_fusion), channel_id=1, source_target_pairs={{496,0},{0,16},{16,32},{32,48},{48,64},{64,80},{80,96},{96,112},{1... | collective-permute-start | bytes 491528 | tf_op jit(solution)/shard_map/ppermute | solution.py:56
  32.9 3.9 %collective-permute-start.6 = (bf16[128,640]{1,0:T(8,128)(2,1)S(1)}, bf16[128,640]{1,0:T(8,128)(2,1)S(1)}, u32[]{:S(2)}, u32[]{:S(2)}) collective-permute-start(bf16[128,640]{1,0:T(8,128)(2,1)S(1)} %constant_dynamic-update-slice_fusion), channel_id=1, source_target_pairs={{16,0},{32,16},{48,32},{64,48},{80,64},{96,80},{112,96},{128,112},... | collective-permute-start | bytes 491528 | tf_op jit(solution)/shard_map/ppermute | solution.py:56
  36.9 0.0 collective-permute-done.2
  36.9 1.9 %collective-permute-start.7 = (bf16[128,640]{1,0:T(8,128)(2,1)S(1)}, bf16[128,640]{1,0:T(8,128)(2,1)S(1)}, u32[]{:S(2)}, u32[]{:S(2)}) collective-permute-start(bf16[128,640]{1,0:T(8,128)(2,1)S(1)} %constant_dynamic-update-slice_fusion), channel_id=1, source_target_pairs={{32,0},{48,16},{64,32},{80,48},{96,64},{112,80},{128,96},{144,112}... | collective-permute-start | bytes 491528 | tf_op jit(solution)/shard_map/ppermute | solution.py:56
  38.8 0.0 collective-permute-done.3
  38.8 4.5 %collective-permute-start.8 = (bf16[128,640]{1,0:T(8,128)(2,1)S(1)}, bf16[128,640]{1,0:T(8,128)(2,1)S(1)}, u32[]{:S(2)}, u32[]{:S(2)}) collective-permute-start(bf16[128,640]{1,0:T(8,128)(2,1)S(1)} %constant_dynamic-update-slice_fusion), channel_id=1, source_target_pairs={{48,0},{64,16},{80,32},{96,48},{112,64},{128,80},{144,96},{160,112... | collective-permute-start | bytes 491528 | tf_op jit(solution)/shard_map/ppermute | solution.py:56
  43.3 3.0 %collective-permute-start.9 = (bf16[128,640]{1,0:T(8,128)(2,1)S(1)}, bf16[128,640]{1,0:T(8,128)(2,1)S(1)}, u32[]{:S(2)}, u32[]{:S(2)}) collective-permute-start(bf16[128,640]{1,0:T(8,128)(2,1)S(1)} %constant_dynamic-update-slice_fusion), channel_id=1, source_target_pairs={{64,0},{80,16},{96,32},{112,48},{128,64},{144,80},{160,96},{176,11... | collective-permute-start | bytes 491528 | tf_op jit(solution)/shard_map/ppermute | solution.py:56
  46.4 2.8 %collective-permute-start.10 = (bf16[128,640]{1,0:T(8,128)(2,1)S(1)}, bf16[128,640]{1,0:T(8,128)(2,1)S(1)}, u32[]{:S(2)}, u32[]{:S(2)}) collective-permute-start(bf16[128,640]{1,0:T(8,128)(2,1)S(1)} %constant_dynamic-update-slice_fusion), channel_id=1, source_target_pairs={{80,0},{112,32},{144,64},{176,96},{208,128},{240,160},{272,192},{3... | collective-permute-start | bytes 491528 | tf_op jit(solution)/shard_map/ppermute | solution.py:56
  49.3 0.0 collective-permute-done.6
  49.3 0.0 collective-permute-done.7
  49.4 2.3 %collective-permute-done.9 = bf16[128,640]{1,0:T(8,128)(2,1)S(1)} collective-permute-done((bf16[128,640]{1,0:T(8,128)(2,1)S(1)}, bf16[128,640]{1,0:T(8,128)(2,1)S(1)}, u32[]{:S(2)}, u32[]{:S(2)}) %collective-permute-start.9) | collective-permute-done | bytes 163872 | tf_op jit(solution)/shard_map/ppermute | solution.py:56
  51.7 1.6 collective-permute-done.10
  53.3 1.9 %constant_dynamic-slice_fusion.20 = (bf16[2,128,640]{2,1,0:T(8,128)(2,1)S(1)}, bf16[2,128,640]{2,1,0:T(8,128)(2,1)S(1)}, bf16[2,128,640]{2,1,0:T(8,128)(2,1)S(1)}) fusion(bf16[11,128,640]{2,1,0:T(8,128)(2,1)S(1)} %bitcast_dynamic-update-slice_fusion, s32[]{:T(128)} %bitcast.12, s32[]{:T(128)} %bitcast.16, s32[]{:T(128)} %bitcast.14), kind=kLoop, calls=%fused_computation.76 | loop fusion | bytes 1966092 | tf_op jit(solution)/shard_map/dynamic_slice | solution.py:30
  55.2 0.2 maximum_convert_fusion
  55.4 0.2 slice_reduce_fusion
  55.6 0.4 multiply_reduce_fusion
  56.0 22.7 %all-gather.1 = f32[16,2,896]{2,1,0:T(2,128)S(1)} all-gather(f32[1,2,896]{2,1,0:T(2,128)S(1)} %maximum_bitcast_fusion.9), channel_id=2, replica_groups=mesh['lon'=32,'tm'=16] {'tm'}, dimensions={0}, use_global_device_ids=true | all-gather | bytes 121856 | tf_op jit(solution)/shard_map/all_gather | solution.py:70
  78.7 0.1 slice_reduce_fusion.2
  78.9 0.4 select_convert_fusion
  79.4 0.8 fusion.32
  80.2 0.9 fusion.33
  81.2 6.4 %constant_dynamic-slice_fusion.1 = (bf16[128,640]{1,0:T(8,128)(2,1)S(1)}, bf16[128,640]{1,0:T(8,128)(2,1)S(1)}, bf16[128,640]{1,0:T(8,128)(2,1)S(1)}, bf16[128,6...) fusion(bf16[128,768]{1,0:T(8,128)(2,1)S(1)} %pad_maximum_fusion, ...), kind=kLoop, calls=%fused_computation.57 | loop fusion | bytes 2949156 | tf_op jit(solution)/shard_map/dynamic_slice | solution.py:30
  87.6 6.2 %constant_dynamic-slice_fusion = (bf16[128,512]{1,0:T(8,128)(2,1)S(1)}, bf16[128,512]{1,0:T(8,128)(2,1)S(1)}, bf16[128,512]{1,0:T(8,128)(2,1)S(1)}, bf16[128,512...) fusion(bf16[128,640]{1,0:T(8,128)(2,1)S(1)} %slice.145, ...), kind=kLoop, calls=%fused_computation.56 | loop fusion | bytes 2359332 | tf_op jit(solution)/shard_map/dynamic_slice | solution.py:30
  94.2 3.8 %copy.16 = bf16[128,9,1152]{2,1,0:T(8,128)(2,1)} copy(bf16[128,9,1152]{2,0,1:T(8,128)(2,1)S(1)} %fusion.20) | data formatting | bytes 5308416 | tf_op jit(solution)/shard_map/stack | solution.py:104
  97.9 4.3 %reshape.69 = bf16[1152,1152]{1,0:T(8,128)(2,1)S(1)} reshape(bf16[128,9,1152]{2,1,0:T(8,128)(2,1)} %copy.16) | data formatting | bytes 5308416 | tf_op jit(solution)/shard_map/reshape | solution.py:104
  102.3 5.4 %fusion = f32[1152,768]{1,0:T(8,128)} fusion(bf16[1152,1152]{1,0:T(8,128)(2,1)S(1)} %reshape.69, bf16[256,512]{1,0:T(8,128)(2,1)} %get-tuple-element.16, bf16[256,640]{1,0:T(8,128)(2,1)S(1)} %get-tuple-element.13, bf16[256,512]{1,0:T(8,128)(2,1)} %get-tuple-element.17, bf16[256,640]{1,0:T(8,128)(2,1)} %get-tuple-element.14, ...), kind=kOutput, calls=%fused_computation.2 | convolution fusion | flops 2049048576 | bytes 7962624 | tf_op jit(solution)/shard_map/dot_general | solution.py:110
  107.7 0.0 reduce-scatter.2.cloned.1.call-update
  107.8 0.6 copy-done.1
  108.4 0.6 dynamic_slice.69
  109.6 0.7 iota_compare_fusion.1
  110.3 60.4 %reduce-scatter.2.cloned.1.call-done = f32[72,768]{1,0:T(8,128)} async-done(((f32[1152,768]{1,0:T(8,128)}), f32[72,768]{1,0:T(8,128)}) %reduce-scatter.2.cloned.1.call-update) | async-done | bytes 221200 | tf_op jit(solution)/shard_map/reduce_scatter | solution.py:115
  170.7 1.0 reshape.70
  171.7 0.3 multiply_reduce_fusion.1
  172.0 0.1 divide_bitcast_fusion
  172.2 0.7 copy.17
  (44 shorter events, 0.7 us)
Async XLA Ops:
  6.5 164.2 %reduce-scatter.2.cloned.1.call-start = ((), (), s32[]{:S(2)}) async-start(), calls=%async_computation.1 | async-start | bytes 3760128 | tf_op jit(solution)/shard_map/reduce_scatter | solution.py:115
  7.3 6.0 %collective-permute-start = (bf16[128,128]{1,0:T(8,128)(2,1)S(1)}, bf16[128,128]{1,0:T(8,128)(2,1)S(1)}, u32[]{:S(2)}, u32[]{:S(2)}) collective-permute-start(bf16[128,128]{1,0:T(8,128)(2,1)S(1)} %slice.108), channel_id=1, source_target_pairs={{1,0},{2,1},{3,2},{4,3},{5,4},{6,5},{7,6},{8,7},{9,8},{10,9},{11,1... | collective-permute-start | bytes 98312 | tf_op jit(solution)/shard_map/ppermute | solution.py:15
  13.3 19.5 %collective-permute-start.1 = (bf16[128,640]{1,0:T(8,128)(2,1)S(1)}, bf16[128,640]{1,0:T(8,128)(2,1)S(1)}, u32[]{:S(2)}, u32[]{:S(2)}) collective-permute-start(bf16[128,640]{1,0:T(8,128)(2,1)S(1)} %constant_dynamic-update-slice_fusion), channel_id=1, source_target_pairs={{448,16},{480,48},{0,80},{32,112},{64,144},{96,176},{128,208},{160... | collective-permute-start | bytes 491528 | tf_op jit(solution)/shard_map/ppermute | solution.py:56
  15.3 21.5 %collective-permute-start.2 = (bf16[128,640]{1,0:T(8,128)(2,1)S(1)}, bf16[128,640]{1,0:T(8,128)(2,1)S(1)}, u32[]{:S(2)}, u32[]{:S(2)}) collective-permute-start(bf16[128,640]{1,0:T(8,128)(2,1)S(1)} %constant_dynamic-update-slice_fusion), channel_id=1, source_target_pairs={{448,0},{464,16},{480,32},{496,48},{0,64},{16,80},{32,96},{48,112}... | collective-permute-start | bytes 491528 | tf_op jit(solution)/shard_map/ppermute | solution.py:56
  18.8 20.0 %collective-permute-start.3 = (bf16[128,640]{1,0:T(8,128)(2,1)S(1)}, bf16[128,640]{1,0:T(8,128)(2,1)S(1)}, u32[]{:S(2)}, u32[]{:S(2)}) collective-permute-start(bf16[128,640]{1,0:T(8,128)(2,1)S(1)} %constant_dynamic-update-slice_fusion), channel_id=1, source_target_pairs={{464,0},{480,16},{496,32},{0,48},{16,64},{32,80},{48,96},{64,112},... | collective-permute-start | bytes 491528 | tf_op jit(solution)/shard_map/ppermute | solution.py:56
  25.4 17.9 %collective-permute-start.4 = (bf16[128,640]{1,0:T(8,128)(2,1)S(1)}, bf16[128,640]{1,0:T(8,128)(2,1)S(1)}, u32[]{:S(2)}, u32[]{:S(2)}) collective-permute-start(bf16[128,640]{1,0:T(8,128)(2,1)S(1)} %constant_dynamic-update-slice_fusion), channel_id=1, source_target_pairs={{480,0},{496,16},{0,32},{16,48},{32,64},{48,80},{64,96},{80,112},{... | collective-permute-start | bytes 491528 | tf_op jit(solution)/shard_map/ppermute | solution.py:56
  31.0 15.5 %collective-permute-start.5 = (bf16[128,640]{1,0:T(8,128)(2,1)S(1)}, bf16[128,640]{1,0:T(8,128)(2,1)S(1)}, u32[]{:S(2)}, u32[]{:S(2)}) collective-permute-start(bf16[128,640]{1,0:T(8,128)(2,1)S(1)} %constant_dynamic-update-slice_fusion), channel_id=1, source_target_pairs={{496,0},{0,16},{16,32},{32,48},{48,64},{64,80},{80,96},{96,112},{1... | collective-permute-start | bytes 491528 | tf_op jit(solution)/shard_map/ppermute | solution.py:56
  32.9 16.4 %collective-permute-start.6 = (bf16[128,640]{1,0:T(8,128)(2,1)S(1)}, bf16[128,640]{1,0:T(8,128)(2,1)S(1)}, u32[]{:S(2)}, u32[]{:S(2)}) collective-permute-start(bf16[128,640]{1,0:T(8,128)(2,1)S(1)} %constant_dynamic-update-slice_fusion), channel_id=1, source_target_pairs={{16,0},{32,16},{48,32},{64,48},{80,64},{96,80},{112,96},{128,112},... | collective-permute-start | bytes 491528 | tf_op jit(solution)/shard_map/ppermute | solution.py:56
  36.9 12.5 %collective-permute-start.7 = (bf16[128,640]{1,0:T(8,128)(2,1)S(1)}, bf16[128,640]{1,0:T(8,128)(2,1)S(1)}, u32[]{:S(2)}, u32[]{:S(2)}) collective-permute-start(bf16[128,640]{1,0:T(8,128)(2,1)S(1)} %constant_dynamic-update-slice_fusion), channel_id=1, source_target_pairs={{32,0},{48,16},{64,32},{80,48},{96,64},{112,80},{128,96},{144,112}... | collective-permute-start | bytes 491528 | tf_op jit(solution)/shard_map/ppermute | solution.py:56
  38.8 10.5 %collective-permute-start.8 = (bf16[128,640]{1,0:T(8,128)(2,1)S(1)}, bf16[128,640]{1,0:T(8,128)(2,1)S(1)}, u32[]{:S(2)}, u32[]{:S(2)}) collective-permute-start(bf16[128,640]{1,0:T(8,128)(2,1)S(1)} %constant_dynamic-update-slice_fusion), channel_id=1, source_target_pairs={{48,0},{64,16},{80,32},{96,48},{112,64},{128,80},{144,96},{160,112... | collective-permute-start | bytes 491528 | tf_op jit(solution)/shard_map/ppermute | solution.py:56
  43.3 8.3 %collective-permute-start.9 = (bf16[128,640]{1,0:T(8,128)(2,1)S(1)}, bf16[128,640]{1,0:T(8,128)(2,1)S(1)}, u32[]{:S(2)}, u32[]{:S(2)}) collective-permute-start(bf16[128,640]{1,0:T(8,128)(2,1)S(1)} %constant_dynamic-update-slice_fusion), channel_id=1, source_target_pairs={{64,0},{80,16},{96,32},{112,48},{128,64},{144,80},{160,96},{176,11... | collective-permute-start | bytes 491528 | tf_op jit(solution)/shard_map/ppermute | solution.py:56
  46.4 6.8 %collective-permute-start.10 = (bf16[128,640]{1,0:T(8,128)(2,1)S(1)}, bf16[128,640]{1,0:T(8,128)(2,1)S(1)}, u32[]{:S(2)}, u32[]{:S(2)}) collective-permute-start(bf16[128,640]{1,0:T(8,128)(2,1)S(1)} %constant_dynamic-update-slice_fusion), channel_id=1, source_target_pairs={{80,0},{112,32},{144,64},{176,96},{208,128},{240,160},{272,192},{3... | collective-permute-start | bytes 491528 | tf_op jit(solution)/shard_map/ppermute | solution.py:56
  107.7 0.7 copy-start.1
  107.7 2.6 %copy-start = (s32[9]{0:T(128)S(1)}, s32[9]{0:T(128)}, u32[]{:S(2)}) copy-start(s32[9]{0:T(128)} %param.7) | copy-start | bytes 112
Sparse Core Ops, SparseCore 0:
  107.9 62.7 reduce-scatter.1

commit v4 on v3

--- a/solution.py
+++ b/solution.py
@@ -89,27 +89,27 @@
         ],
         1,
     )
-    backs = LMAX - lag_set
-    left_rows = []
-    for lag_index in range(NLAG):
-        left_rows.append(
-            jnp.concatenate(
-                [
-                    dslice(padded, backs[lag_index], days_dev + LMAX, 1),
-                    dslice(own, lag_set[lag_index], days_dev, 1),
-                ],
-                1,
-            )
-        )
-    left = jnp.stack(left_rows, 1).reshape(half_rows * NLAG, -1)
     right_rows = []
     for slot_index in range(K_SLOTS):
         columns = standardized[half_rows + slot_index * block_width:][:block_width]
         right_rows.append(jnp.concatenate([columns, columns[:, :days_dev]], 1))
     right = jnp.concatenate(right_rows, 0)
-    product = lax.dot_general(
-        left, right, (((1,), (1,)), ((), ())), preferred_element_type=jnp.float32
-    )
+    pieces = []
+    for lag_index in range(NLAG):
+        lag_days = lax.min(lag_set[lag_index], LMAX)
+        left = jnp.concatenate(
+            [
+                dslice(padded, LMAX - lag_days, days_dev + LMAX, 1),
+                dslice(own, lag_days, days_dev, 1),
+            ],
+            1,
+        )
+        pieces.append(
+            lax.dot_general(
+                left, right, (((1,), (1,)), ((), ())), preferred_element_type=jnp.float32
+            )
+        )
+    product = jnp.concatenate(pieces, 1)
 
     out_rows = half_rows // tm_size
     comoment = lax.psum_scatter(product, "tm", scatter_dimension=0, tiled=True)

time: 181 us -> 166 us (0.917)
  local copies, waits for them, and re-layouts: 32.3 us -> 10.9 us
  between operations: 14.5 us -> 20.2 us
    dynamic_slice x4, local copies, waits for them, and re-layouts: 15.1 us -> 4 us  [dslice(): lax.dynamic_slice_in_dim(value, start, size, axis, allow_negative_indices...]
    reshape x2 -> x0, local copies, waits for them, and re-layouts: 5.39 us -> none  [the longest x1 4.34 us: local(): left = jnp.stack(left_rows, 1).reshape(half_rows * NLAG, -1)]
    another operation x2 -> x1, local copies, waits for them, and re-layouts: 3.78 us -> 0.01 us  [the longest x1 3.78 us: local(): left = jnp.stack(left_rows, 1).reshape(half_rows * NLAG, -1)]
    dot_general x1 -> x9, matrix products: 5.45 us -> 5.69 us  [local(): lax.dot_general(left, right, (((1,), (1,)), ((), ())), preferred_element_...]
  transfers between devices with their start and end apart: 12 -> 12, of which waited for: 3 -> 3; matrix products, arithmetic and copies ran while one was open for 4% -> 3% of each run, Pallas kernels for 0% -> 0%
where the time goes in v4:
time: 166 us
  waiting for transfers between devices  64.8 us (39%)
  starting transfers between devices  36.2 us (22%)
  blocking collectives  22.7 us (14%)
  between operations  20.2 us (12%)
  local copies, waits for them, and re-layouts  10.9 us (7%)
  matrix products  5.69 us (3%)
  other arithmetic  5.18 us (3%)
    reduce_scatter x1, waiting for transfers between devices, local(): comoment = lax.psum_scatter(product, 'tm', scatter_dimension=0, tiled=True)  61 us
    ppermute x10, starting transfers between devices, local(): halves.append(lax.ppermute(extended, 'lon', pairs))  34.9 us
    all_gather x1, blocking collectives, local(): stats = lax.all_gather(jnp.stack([shard_mean, shard_square], 0), 'tm')  22.7 us
    dot_general x9, matrix products, local(): lax.dot_general(left, right, (((1,), (1,)), ((), ())), preferred_element_...  5.69 us
    dynamic_slice x4, local copies, waits for them, and re-layouts, dslice(): lax.dynamic_slice_in_dim(value, start, size, axis, allow_negative_indices...  4 us
    ppermute x10, waiting for transfers between devices, local(): halves.append(lax.ppermute(extended, 'lon', pairs))  3.83 us
  transfers between devices with their start and end apart: 12, of which 3 were waited for; matrix products, arithmetic and copies ran while one was open for 3% of the time, Pallas kernels for 0%

profile of v4, /device:TPU:6, one launch (start us, length us, event | category | flops | bytes accessed | tf_op | source)
XLA Modules:
  0.0 165.6 jit_solution(8355819459598566130)
XLA Ops:
  6.5 0.8 slice.81
  7.3 1.3 collective-permute-start
  8.6 0.9 constant_dynamic-update-slice_fusion.1
  9.5 0.9 fusion.32
  10.4 1.7 %fusion.48 = (s32[1]{0:T(128)}, s32[1]{0:T(128)}, s32[1]{0:T(128)}, s32[1]{0:T(128)}, s32[1]{0:T(128)}, /*index=5*/s32[1]{0:T(128)}, s32[1]{0:T(128)}, s32[1]{0:T(128)}, s32[1]{0:T(128)}) fusion(s32[9]{0:T(128)} %param.7), kind=kLoop, calls=%fused_computation.114 | loop fusion | bytes 72 | tf_op jit(solution)/shard_map/slice | solution.py:99
  12.1 1.3 collective-permute-start.1
  19.0 0.7 fusion.49
  19.7 3.5 %collective-permute-start.2 = (bf16[128,640]{1,0:T(8,128)(2,1)S(1)}, bf16[128,640]{1,0:T(8,128)(2,1)S(1)}, u32[]{:S(2)}, u32[]{:S(2)}) collective-permute-start(bf16[128,640]{1,0:T(8,128)(2,1)S(1)} %constant_dynamic-update-slice_fusion), channel_id=1, source_target_pairs={{448,0},{464,16},{480,32},{496,48},{0,64},{16,80},{32,96},{48,112}... | collective-permute-start | bytes 491528 | tf_op jit(solution)/shard_map/ppermute | solution.py:56
  23.2 6.6 %collective-permute-start.3 = (bf16[128,640]{1,0:T(8,128)(2,1)S(1)}, bf16[128,640]{1,0:T(8,128)(2,1)S(1)}, u32[]{:S(2)}, u32[]{:S(2)}) collective-permute-start(bf16[128,640]{1,0:T(8,128)(2,1)S(1)} %constant_dynamic-update-slice_fusion), channel_id=1, source_target_pairs={{464,0},{480,16},{496,32},{0,48},{16,64},{32,80},{48,96},{64,112},... | collective-permute-start | bytes 491528 | tf_op jit(solution)/shard_map/ppermute | solution.py:56
  29.8 5.6 %collective-permute-start.4 = (bf16[128,640]{1,0:T(8,128)(2,1)S(1)}, bf16[128,640]{1,0:T(8,128)(2,1)S(1)}, u32[]{:S(2)}, u32[]{:S(2)}) collective-permute-start(bf16[128,640]{1,0:T(8,128)(2,1)S(1)} %constant_dynamic-update-slice_fusion), channel_id=1, source_target_pairs={{480,0},{496,16},{0,32},{16,48},{32,64},{48,80},{64,96},{80,112},{... | collective-permute-start | bytes 491528 | tf_op jit(solution)/shard_map/ppermute | solution.py:56
  35.3 1.9 %collective-permute-start.5 = (bf16[128,640]{1,0:T(8,128)(2,1)S(1)}, bf16[128,640]{1,0:T(8,128)(2,1)S(1)}, u32[]{:S(2)}, u32[]{:S(2)}) collective-permute-start(bf16[128,640]{1,0:T(8,128)(2,1)S(1)} %constant_dynamic-update-slice_fusion), channel_id=1, source_target_pairs={{496,0},{0,16},{16,32},{32,48},{48,64},{64,80},{80,96},{96,112},{1... | collective-permute-start | bytes 491528 | tf_op jit(solution)/shard_map/ppermute | solution.py:56
  37.2 3.9 %collective-permute-start.6 = (bf16[128,640]{1,0:T(8,128)(2,1)S(1)}, bf16[128,640]{1,0:T(8,128)(2,1)S(1)}, u32[]{:S(2)}, u32[]{:S(2)}) collective-permute-start(bf16[128,640]{1,0:T(8,128)(2,1)S(1)} %constant_dynamic-update-slice_fusion), channel_id=1, source_target_pairs={{16,0},{32,16},{48,32},{64,48},{80,64},{96,80},{112,96},{128,112},... | collective-permute-start | bytes 491528 | tf_op jit(solution)/shard_map/ppermute | solution.py:56
  41.2 1.9 %collective-permute-start.7 = (bf16[128,640]{1,0:T(8,128)(2,1)S(1)}, bf16[128,640]{1,0:T(8,128)(2,1)S(1)}, u32[]{:S(2)}, u32[]{:S(2)}) collective-permute-start(bf16[128,640]{1,0:T(8,128)(2,1)S(1)} %constant_dynamic-update-slice_fusion), channel_id=1, source_target_pairs={{32,0},{48,16},{64,32},{80,48},{96,64},{112,80},{128,96},{144,112}... | collective-permute-start | bytes 491528 | tf_op jit(solution)/shard_map/ppermute | solution.py:56
  43.2 4.5 %collective-permute-start.8 = (bf16[128,640]{1,0:T(8,128)(2,1)S(1)}, bf16[128,640]{1,0:T(8,128)(2,1)S(1)}, u32[]{:S(2)}, u32[]{:S(2)}) collective-permute-start(bf16[128,640]{1,0:T(8,128)(2,1)S(1)} %constant_dynamic-update-slice_fusion), channel_id=1, source_target_pairs={{48,0},{64,16},{80,32},{96,48},{112,64},{128,80},{144,96},{160,112... | collective-permute-start | bytes 491528 | tf_op jit(solution)/shard_map/ppermute | solution.py:56
  47.7 3.0 %collective-permute-start.9 = (bf16[128,640]{1,0:T(8,128)(2,1)S(1)}, bf16[128,640]{1,0:T(8,128)(2,1)S(1)}, u32[]{:S(2)}, u32[]{:S(2)}) collective-permute-start(bf16[128,640]{1,0:T(8,128)(2,1)S(1)} %constant_dynamic-update-slice_fusion), channel_id=1, source_target_pairs={{64,0},{80,16},{96,32},{112,48},{128,64},{144,80},{160,96},{176,11... | collective-permute-start | bytes 491528 | tf_op jit(solution)/shard_map/ppermute | solution.py:56
  50.8 2.8 %collective-permute-start.10 = (bf16[128,640]{1,0:T(8,128)(2,1)S(1)}, bf16[128,640]{1,0:T(8,128)(2,1)S(1)}, u32[]{:S(2)}, u32[]{:S(2)}) collective-permute-start(bf16[128,640]{1,0:T(8,128)(2,1)S(1)} %constant_dynamic-update-slice_fusion), channel_id=1, source_target_pairs={{80,0},{112,32},{144,64},{176,96},{208,128},{240,160},{272,192},{3... | collective-permute-start | bytes 491528 | tf_op jit(solution)/shard_map/ppermute | solution.py:56
  53.7 2.3 %collective-permute-done.9 = bf16[128,640]{1,0:T(8,128)(2,1)S(1)} collective-permute-done((bf16[128,640]{1,0:T(8,128)(2,1)S(1)}, bf16[128,640]{1,0:T(8,128)(2,1)S(1)}, u32[]{:S(2)}, u32[]{:S(2)}) %collective-permute-start.9) | collective-permute-done | bytes 163872 | tf_op jit(solution)/shard_map/ppermute | solution.py:56
  56.1 1.5 collective-permute-done.10
  57.6 2.0 %constant_dynamic-slice_fusion.20 = (bf16[2,128,640]{2,1,0:T(8,128)(2,1)S(1)}, bf16[2,128,640]{2,1,0:T(8,128)(2,1)S(1)}, bf16[2,128,640]{2,1,0:T(8,128)(2,1)S(1)}) fusion(bf16[11,128,640]{2,1,0:T(8,128)(2,1)S(1)} %bitcast_dynamic-update-slice_fusion, s32[]{:T(128)} %bitcast.12, s32[]{:T(128)} %bitcast.16, s32[]{:T(128)} %bitcast.14), kind=kLoop, calls=%fused_computation.83 | loop fusion | bytes 1966092 | tf_op jit(solution)/shard_map/dynamic_slice | solution.py:30
  59.6 0.2 maximum_convert_fusion
  59.8 0.2 slice_reduce_fusion
  60.0 0.4 multiply_reduce_fusion
  60.4 22.7 %all-gather.1 = f32[16,2,896]{2,1,0:T(2,128)S(1)} all-gather(f32[1,2,896]{2,1,0:T(2,128)S(1)} %maximum_bitcast_fusion), channel_id=2, replica_groups=mesh['lon'=32,'tm'=16] {'tm'}, dimensions={0}, use_global_device_ids=true | all-gather | bytes 121856 | tf_op jit(solution)/shard_map/all_gather | solution.py:70
  83.1 0.1 slice_reduce_fusion.2
  83.3 0.4 select_convert_fusion
  83.8 0.1 fusion.46
  83.9 0.1 fusion.47
  84.0 0.6 constant_dynamic-slice_fusion
  84.6 0.8 constant_dynamic-slice_fusion.1
  85.4 0.6 convolution_dynamic-update-slice_fusion.8
  86.1 0.6 convolution_dynamic-update-slice_fusion.7
  86.7 0.6 convolution_dynamic-update-slice_fusion.6
  87.3 0.6 convolution_dynamic-update-slice_fusion.5
  88.0 0.6 convolution_dynamic-update-slice_fusion.4
  88.6 0.6 convolution_dynamic-update-slice_fusion.3
  89.3 0.6 convolution_dynamic-update-slice_fusion.2
  89.9 0.6 convolution_dynamic-update-slice_fusion.1
  90.5 0.6 convolution_dynamic-update-slice_fusion
  91.2 0.0 copy-start.2
  91.2 0.0 copy-start.1
  91.2 1.7 %copy-done = f32[128,6912]{1,0:T(8,128)} copy-done((f32[128,6912]{1,0:T(8,128)}, f32[128,6912]{1,0:T(8,128)S(1)}, u32[]{:S(2)}) %copy-start) | copy-done | bytes 3538968
  92.9 0.0 reduce-scatter.2.cloned.1.call-update
  93.0 0.6 dynamic_slice.69
  94.2 0.7 iota_compare_fusion.1
  94.9 61.0 %reduce-scatter.2.cloned.1.call-done = f32[8,6912]{1,0:T(8,128)} async-done(((f32[128,6912]{1,0:T(8,128)}), f32[8,6912]{1,0:T(8,128)}) %reduce-scatter.2.cloned.1.call-update) | async-done | bytes 221200 | tf_op jit(solution)/shard_map/reduce_scatter | solution.py:115
  155.9 1.2 multiply_reduce_fusion.1
  157.0 1.0 divide_bitcast_fusion
  158.1 0.7 copy.6
  (40 shorter events, 0.4 us)
Async XLA Ops:
  6.5 149.3 %reduce-scatter.2.cloned.1.call-start = ((), (), s32[]{:S(2)}) async-start(), calls=%async_computation.1 | async-start | bytes 3760128 | tf_op jit(solution)/shard_map/reduce_scatter | solution.py:115
  7.3 4.8 %collective-permute-start = (bf16[128,128]{1,0:T(8,128)(2,1)S(1)}, bf16[128,128]{1,0:T(8,128)(2,1)S(1)}, u32[]{:S(2)}, u32[]{:S(2)}) collective-permute-start(bf16[128,128]{1,0:T(8,128)(2,1)S(1)} %slice.81), channel_id=1, source_target_pairs={{1,0},{2,1},{3,2},{4,3},{5,4},{6,5},{7,6},{8,7},{9,8},{10,9},{11,1... | collective-permute-start | bytes 98312 | tf_op jit(solution)/shard_map/ppermute | solution.py:15
  12.1 25.2 %collective-permute-start.1 = (bf16[128,640]{1,0:T(8,128)(2,1)S(1)}, bf16[128,640]{1,0:T(8,128)(2,1)S(1)}, u32[]{:S(2)}, u32[]{:S(2)}) collective-permute-start(bf16[128,640]{1,0:T(8,128)(2,1)S(1)} %constant_dynamic-update-slice_fusion), channel_id=1, source_target_pairs={{448,16},{480,48},{0,80},{32,112},{64,144},{96,176},{128,208},{160... | collective-permute-start | bytes 491528 | tf_op jit(solution)/shard_map/ppermute | solution.py:56
  19.7 21.5 %collective-permute-start.2 = (bf16[128,640]{1,0:T(8,128)(2,1)S(1)}, bf16[128,640]{1,0:T(8,128)(2,1)S(1)}, u32[]{:S(2)}, u32[]{:S(2)}) collective-permute-start(bf16[128,640]{1,0:T(8,128)(2,1)S(1)} %constant_dynamic-update-slice_fusion), channel_id=1, source_target_pairs={{448,0},{464,16},{480,32},{496,48},{0,64},{16,80},{32,96},{48,112}... | collective-permute-start | bytes 491528 | tf_op jit(solution)/shard_map/ppermute | solution.py:56
  23.2 20.0 %collective-permute-start.3 = (bf16[128,640]{1,0:T(8,128)(2,1)S(1)}, bf16[128,640]{1,0:T(8,128)(2,1)S(1)}, u32[]{:S(2)}, u32[]{:S(2)}) collective-permute-start(bf16[128,640]{1,0:T(8,128)(2,1)S(1)} %constant_dynamic-update-slice_fusion), channel_id=1, source_target_pairs={{464,0},{480,16},{496,32},{0,48},{16,64},{32,80},{48,96},{64,112},... | collective-permute-start | bytes 491528 | tf_op jit(solution)/shard_map/ppermute | solution.py:56
  29.8 17.9 %collective-permute-start.4 = (bf16[128,640]{1,0:T(8,128)(2,1)S(1)}, bf16[128,640]{1,0:T(8,128)(2,1)S(1)}, u32[]{:S(2)}, u32[]{:S(2)}) collective-permute-start(bf16[128,640]{1,0:T(8,128)(2,1)S(1)} %constant_dynamic-update-slice_fusion), channel_id=1, source_target_pairs={{480,0},{496,16},{0,32},{16,48},{32,64},{48,80},{64,96},{80,112},{... | collective-permute-start | bytes 491528 | tf_op jit(solution)/shard_map/ppermute | solution.py:56
  35.3 15.5 %collective-permute-start.5 = (bf16[128,640]{1,0:T(8,128)(2,1)S(1)}, bf16[128,640]{1,0:T(8,128)(2,1)S(1)}, u32[]{:S(2)}, u32[]{:S(2)}) collective-permute-start(bf16[128,640]{1,0:T(8,128)(2,1)S(1)} %constant_dynamic-update-slice_fusion), channel_id=1, source_target_pairs={{496,0},{0,16},{16,32},{32,48},{48,64},{64,80},{80,96},{96,112},{1... | collective-permute-start | bytes 491528 | tf_op jit(solution)/shard_map/ppermute | solution.py:56
  37.2 16.4 %collective-permute-start.6 = (bf16[128,640]{1,0:T(8,128)(2,1)S(1)}, bf16[128,640]{1,0:T(8,128)(2,1)S(1)}, u32[]{:S(2)}, u32[]{:S(2)}) collective-permute-start(bf16[128,640]{1,0:T(8,128)(2,1)S(1)} %constant_dynamic-update-slice_fusion), channel_id=1, source_target_pairs={{16,0},{32,16},{48,32},{64,48},{80,64},{96,80},{112,96},{128,112},... | collective-permute-start | bytes 491528 | tf_op jit(solution)/shard_map/ppermute | solution.py:56
  41.2 12.4 %collective-permute-start.7 = (bf16[128,640]{1,0:T(8,128)(2,1)S(1)}, bf16[128,640]{1,0:T(8,128)(2,1)S(1)}, u32[]{:S(2)}, u32[]{:S(2)}) collective-permute-start(bf16[128,640]{1,0:T(8,128)(2,1)S(1)} %constant_dynamic-update-slice_fusion), channel_id=1, source_target_pairs={{32,0},{48,16},{64,32},{80,48},{96,64},{112,80},{128,96},{144,112}... | collective-permute-start | bytes 491528 | tf_op jit(solution)/shard_map/ppermute | solution.py:56
  43.2 10.5 %collective-permute-start.8 = (bf16[128,640]{1,0:T(8,128)(2,1)S(1)}, bf16[128,640]{1,0:T(8,128)(2,1)S(1)}, u32[]{:S(2)}, u32[]{:S(2)}) collective-permute-start(bf16[128,640]{1,0:T(8,128)(2,1)S(1)} %constant_dynamic-update-slice_fusion), channel_id=1, source_target_pairs={{48,0},{64,16},{80,32},{96,48},{112,64},{128,80},{144,96},{160,112... | collective-permute-start | bytes 491528 | tf_op jit(solution)/shard_map/ppermute | solution.py:56
  47.7 8.4 %collective-permute-start.9 = (bf16[128,640]{1,0:T(8,128)(2,1)S(1)}, bf16[128,640]{1,0:T(8,128)(2,1)S(1)}, u32[]{:S(2)}, u32[]{:S(2)}) collective-permute-start(bf16[128,640]{1,0:T(8,128)(2,1)S(1)} %constant_dynamic-update-slice_fusion), channel_id=1, source_target_pairs={{64,0},{80,16},{96,32},{112,48},{128,64},{144,80},{160,96},{176,11... | collective-permute-start | bytes 491528 | tf_op jit(solution)/shard_map/ppermute | solution.py:56
  50.8 6.8 %collective-permute-start.10 = (bf16[128,640]{1,0:T(8,128)(2,1)S(1)}, bf16[128,640]{1,0:T(8,128)(2,1)S(1)}, u32[]{:S(2)}, u32[]{:S(2)}) collective-permute-start(bf16[128,640]{1,0:T(8,128)(2,1)S(1)} %constant_dynamic-update-slice_fusion), channel_id=1, source_target_pairs={{80,0},{112,32},{144,64},{176,96},{208,128},{240,160},{272,192},{3... | collective-permute-start | bytes 491528 | tf_op jit(solution)/shard_map/ppermute | solution.py:56
  91.2 1.7 %copy-start = (f32[128,6912]{1,0:T(8,128)}, f32[128,6912]{1,0:T(8,128)S(1)}, u32[]{:S(2)}) copy-start(f32[128,6912]{1,0:T(8,128)S(1)} %convolution_dynamic-update-slice_fusion) | copy-start | bytes 10616836
  91.2 1.8 %copy-start.2 = (s32[16]{0:T(128)S(1)}, s32[16]{0:T(128)}, u32[]{:S(2)}) copy-start(s32[16]{0:T(128)} %param.6) | copy-start | bytes 196
  91.2 3.7 %copy-start.1 = (s32[9]{0:T(128)S(1)}, s32[9]{0:T(128)}, u32[]{:S(2)}) copy-start(s32[9]{0:T(128)} %param.7) | copy-start | bytes 112
Sparse Core Ops, SparseCore 0:
  93.1 62.7 reduce-scatter.1

commit v5 on v4

v5 whole, which is shorter than its diff:
```python
import jax
import jax.numpy as jnp
from jax import lax
from jax.sharding import Mesh, PartitionSpec as P

LMAX = 128
NLAG = 9
K_SLOTS = 3
REACH = 2
TIME = ("tz", "tc")


def dslice(value, start, size, axis):
    return lax.dynamic_slice_in_dim(value, start, size, axis, allow_negative_indices=False)


def local(anomalies, neighbor_ids, neighbor_counts, lag_set):
    half_rows, days_dev = anomalies.shape
    tz_size = lax.axis_size("tz")
    tm_size = tz_size * lax.axis_size("tc")
    lon_size = lax.axis_size("lon")
    blocks = lon_size // 2
    block_width = 2 * half_rows
    total_days = days_dev * tm_size
    tm_index = lax.axis_index("tz") * 2 + lax.axis_index("tc")
    core = lax.axis_index("tc")
    margin = lax.ppermute(
        anomalies[:, :LMAX], TIME, [(i, i - 1) for i in range(1, tm_size)]
    )
    extended = jnp.concatenate([anomalies, margin], 1)
    lon_index = lax.axis_index("lon")
    parity = lax.rem(lon_index, 2)
    block_index = lax.div(lon_index, 2)
    reach = 2 * REACH + 1
    halves = []
    for offset in range(-reach, reach + 1):
        if offset == 0:
            halves.append(extended)
            continue
        pairs = []
        for target in range(lon_size):
            low = -2 * REACH - target % 2
            if low <= offset <= low + 2 * (2 * REACH + 1) - 1:
                pairs.append(((target + offset) % lon_size, target))
        halves.append(lax.ppermute(extended, "lon", pairs))
    halves = jnp.stack(halves, 0)
    block_ids = dslice(neighbor_ids, block_index, 1, 0)[0]
    live_count = dslice(neighbor_counts, block_index, 1, 0)[0]
    positions = lax.rem(block_ids - block_index + (REACH + blocks), blocks)
    firsts = 2 * positions + (reach - 2 * REACH) - parity
    slot_blocks = []
    for slot_index in range(K_SLOTS):
        pair = dslice(halves, firsts[slot_index], 2, 0)
        slot_blocks.append(pair.reshape(block_width, days_dev + LMAX))
    raw = jnp.concatenate([extended] + slot_blocks, 0)
    values = raw.astype(jnp.float32)
    shard_mean = jnp.mean(values[:, :days_dev], axis=1)
    shard_square = jnp.sum(jnp.square(values[:, :days_dev] - shard_mean[:, None]), axis=1)
    stats = lax.all_gather(jnp.stack([shard_mean, shard_square], 0), TIME)
    means, squares = stats[:, 0], stats[:, 1]
    point_mean = jnp.mean(means, axis=0)
    point_m2 = jnp.sum(squares, axis=0) + days_dev * jnp.sum(
        jnp.square(means - point_mean[None, :]), axis=0
    )
    spread = jnp.sqrt(point_m2 / total_days + 1e-06)
    day = lax.broadcasted_iota(jnp.int32, (1, days_dev + LMAX), 1)
    inside = (day < days_dev) | (tm_index < tm_size - 1)
    standardized = jnp.where(
        inside, (values - point_mean[:, None]) / spread[:, None], 0.0
    ).astype(jnp.bfloat16)

    other = lax.ppermute(standardized, "tc", [(0, 1), (1, 0)])
    first = core == 0
    window = jnp.concatenate(
        [
            jnp.where(first, standardized[:, :days_dev], other[:, :days_dev]),
            jnp.where(first, other, standardized),
        ],
        1,
    )
    span = 2 * days_dev
    out_rows = half_rows // tm_size
    own = window[:half_rows].reshape(tz_size, 2, out_rows, span + LMAX)
    own = dslice(own, core, 1, 1).reshape(half_rows // 2, span + LMAX)
    columns_all = window[half_rows:]

    padded = jnp.concatenate(
        [
            jnp.zeros((half_rows // 2, LMAX), jnp.bfloat16),
            own[:, :span],
            jnp.zeros((half_rows // 2, LMAX), jnp.bfloat16),
        ],
        1,
    )
    right_rows = []
    for slot_index in range(K_SLOTS):
        columns = columns_all[slot_index * block_width:][:block_width]
        right_rows.append(jnp.concatenate([columns, columns[:, :span]], 1))
    right = jnp.concatenate(right_rows, 0)
    pieces = []
    for lag_index in range(NLAG):
        lag_days = lax.min(lag_set[lag_index], LMAX)
        left = jnp.concatenate(
            [
                dslice(padded, LMAX - lag_days, span + LMAX, 1),
                dslice(own, lag_days, span, 1),
            ],
            1,
        )
        pieces.append(
            lax.dot_general(
                left, right, (((1,), (1,)), ((), ())), preferred_element_type=jnp.float32
            )
        )
    product = jnp.concatenate(pieces, 1)

    comoment = lax.psum_scatter(product, "tz", scatter_dimension=0, tiled=True)
    comoment = comoment.reshape(out_rows, NLAG, K_SLOTS, block_width).transpose(0, 2, 1, 3)
    denominator = 2.0 * (total_days - lag_set).astype(jnp.float32)
    is_live = jnp.arange(K_SLOTS, dtype=jnp.int32) < live_count
    linked = jnp.where(
        is_live[None, :, None, None], comoment / denominator[None, None, :, None], 0.0
    )
    squares = jnp.sum(jnp.square(linked), axis=(1, 2, 3))
    row_scale = jnp.sqrt(squares / (live_count * NLAG * block_width).astype(jnp.float32) + 1e-06)
    return (linked / row_scale[:, None, None, None]).reshape(out_rows, -1)


def solution(mesh):
    lon_size, tm_size = mesh.devices.shape
    split = Mesh(mesh.devices.reshape(lon_size, tm_size // 2, 2), ("lon", "tz", "tc"))
    return jax.shard_map(
        local,
        mesh=split,
        in_specs=(P("lon", TIME), P(), P(), P()),
        out_specs=P(("lon",) + TIME, None),
        check_vma=False,
    )
```

time: 166 us -> 169 us (1.018)
  waiting for transfers between devices: 64.8 us -> 44.9 us
  other arithmetic: 5.18 us -> 23.5 us
  matrix products: 5.69 us -> 9.76 us
  starting transfers between devices: 36.2 us -> 38.6 us
    reduce_scatter x1, waiting for transfers between devices: 61 us -> 40.6 us  [local(): comoment = lax.psum_scatter(product, 'tz', scatter_dimension=0, tiled=True)]
    concatenate x1 -> x5, other arithmetic: 0.02 us -> 18.2 us  [the longest x1 17.9 us: local(): right = jnp.concatenate(right_rows, 0)]
    dot_general x9, matrix products: 5.69 us -> 9.76 us  [local(): lax.dot_general(left, right, (((1,), (1,)), ((), ())), preferred_element_...]
    ppermute x1 -> x2, starting transfers between devices: 1.28 us -> 3.71 us  [the longest x1 2.43 us: local(): other = lax.ppermute(standardized, 'tc', [(0, 1), (1, 0)])]
  transfers between devices with their start and end apart: 12 -> 13, of which waited for: 3 -> 3; matrix products, arithmetic and copies ran while one was open for 3% -> 3% of each run, Pallas kernels for 0% -> 0%
where the time goes in v5:
time: 169 us
  waiting for transfers between devices  44.9 us (27%)
  starting transfers between devices  38.6 us (23%)
  other arithmetic  23.5 us (14%)
  blocking collectives  22.2 us (13%)
  between operations  20.2 us (12%)
  matrix products  9.76 us (6%)
  local copies, waits for them, and re-layouts  9.26 us (5%)
    reduce_scatter x1, waiting for transfers between devices, local(): comoment = lax.psum_scatter(product, 'tz', scatter_dimension=0, tiled=True)  40.6 us
    ppermute x10, starting transfers between devices, local(): halves.append(lax.ppermute(extended, 'lon', pairs))  34.9 us
    all_gather x1, blocking collectives, local(): stats = lax.all_gather(jnp.stack([shard_mean, shard_square], 0), TIME)  22.2 us
    concatenate x1, other arithmetic, local(): right = jnp.concatenate(right_rows, 0)  17.9 us
    dot_general x9, matrix products, local(): lax.dot_general(left, right, (((1,), (1,)), ((), ())), preferred_element_...  9.76 us
    ppermute x10, waiting for transfers between devices, local(): halves.append(lax.ppermute(extended, 'lon', pairs))  4.31 us
    dynamic_slice x4, local copies, waits for them, and re-layouts, dslice(): lax.dynamic_slice_in_dim(value, start, size, axis, allow_negative_indices...  4 us
  transfers between devices with their start and end apart: 13, of which 3 were waited for; matrix products, arithmetic and copies ran while one was open for 3% of the time, Pallas kernels for 0%

profile of v5, /device:TPU:6, one launch (start us, length us, event | category | flops | bytes accessed | tf_op | source)
XLA Modules:
  0.0 168.5 jit_solution(17672307372097177984)
XLA Ops:
  6.5 0.8 slice.88
  7.3 1.3 collective-permute-start
  8.6 0.9 fusion.46
  9.5 0.9 constant_dynamic-update-slice_fusion.1
  10.4 1.3 collective-permute-start.1
  11.7 0.6 fusion.61
  12.4 3.5 %collective-permute-start.2 = (bf16[128,640]{1,0:T(8,128)(2,1)S(1)}, bf16[128,640]{1,0:T(8,128)(2,1)S(1)}, u32[]{:S(2)}, u32[]{:S(2)}) collective-permute-start(bf16[128,640]{1,0:T(8,128)(2,1)S(1)} %constant_dynamic-update-slice_fusion), channel_id=1, source_target_pairs={{448,0},{464,16},{480,32},{496,48},{0,64},{16,80},{32,96},{48,112}... | collective-permute-start | bytes 491528 | tf_op jit(solution)/shard_map/ppermute | solution.py:45
  15.9 6.6 %collective-permute-start.3 = (bf16[128,640]{1,0:T(8,128)(2,1)S(1)}, bf16[128,640]{1,0:T(8,128)(2,1)S(1)}, u32[]{:S(2)}, u32[]{:S(2)}) collective-permute-start(bf16[128,640]{1,0:T(8,128)(2,1)S(1)} %constant_dynamic-update-slice_fusion), channel_id=1, source_target_pairs={{464,0},{480,16},{496,32},{0,48},{16,64},{32,80},{48,96},{64,112},... | collective-permute-start | bytes 491528 | tf_op jit(solution)/shard_map/ppermute | solution.py:45
  22.5 5.5 %collective-permute-start.4 = (bf16[128,640]{1,0:T(8,128)(2,1)S(1)}, bf16[128,640]{1,0:T(8,128)(2,1)S(1)}, u32[]{:S(2)}, u32[]{:S(2)}) collective-permute-start(bf16[128,640]{1,0:T(8,128)(2,1)S(1)} %constant_dynamic-update-slice_fusion), channel_id=1, source_target_pairs={{480,0},{496,16},{0,32},{16,48},{32,64},{48,80},{64,96},{80,112},{... | collective-permute-start | bytes 491528 | tf_op jit(solution)/shard_map/ppermute | solution.py:45
  28.0 1.9 %collective-permute-start.5 = (bf16[128,640]{1,0:T(8,128)(2,1)S(1)}, bf16[128,640]{1,0:T(8,128)(2,1)S(1)}, u32[]{:S(2)}, u32[]{:S(2)}) collective-permute-start(bf16[128,640]{1,0:T(8,128)(2,1)S(1)} %constant_dynamic-update-slice_fusion), channel_id=1, source_target_pairs={{496,0},{0,16},{16,32},{32,48},{48,64},{64,80},{80,96},{96,112},{1... | collective-permute-start | bytes 491528 | tf_op jit(solution)/shard_map/ppermute | solution.py:45
  29.9 3.9 %collective-permute-start.6 = (bf16[128,640]{1,0:T(8,128)(2,1)S(1)}, bf16[128,640]{1,0:T(8,128)(2,1)S(1)}, u32[]{:S(2)}, u32[]{:S(2)}) collective-permute-start(bf16[128,640]{1,0:T(8,128)(2,1)S(1)} %constant_dynamic-update-slice_fusion), channel_id=1, source_target_pairs={{16,0},{32,16},{48,32},{64,48},{80,64},{96,80},{112,96},{128,112},... | collective-permute-start | bytes 491528 | tf_op jit(solution)/shard_map/ppermute | solution.py:45
  33.9 1.9 %collective-permute-start.7 = (bf16[128,640]{1,0:T(8,128)(2,1)S(1)}, bf16[128,640]{1,0:T(8,128)(2,1)S(1)}, u32[]{:S(2)}, u32[]{:S(2)}) collective-permute-start(bf16[128,640]{1,0:T(8,128)(2,1)S(1)} %constant_dynamic-update-slice_fusion), channel_id=1, source_target_pairs={{32,0},{48,16},{64,32},{80,48},{96,64},{112,80},{128,96},{144,112}... | collective-permute-start | bytes 491528 | tf_op jit(solution)/shard_map/ppermute | solution.py:45
  35.9 4.5 %collective-permute-start.8 = (bf16[128,640]{1,0:T(8,128)(2,1)S(1)}, bf16[128,640]{1,0:T(8,128)(2,1)S(1)}, u32[]{:S(2)}, u32[]{:S(2)}) collective-permute-start(bf16[128,640]{1,0:T(8,128)(2,1)S(1)} %constant_dynamic-update-slice_fusion), channel_id=1, source_target_pairs={{48,0},{64,16},{80,32},{96,48},{112,64},{128,80},{144,96},{160,112... | collective-permute-start | bytes 491528 | tf_op jit(solution)/shard_map/ppermute | solution.py:45
  40.4 3.0 %collective-permute-start.9 = (bf16[128,640]{1,0:T(8,128)(2,1)S(1)}, bf16[128,640]{1,0:T(8,128)(2,1)S(1)}, u32[]{:S(2)}, u32[]{:S(2)}) collective-permute-start(bf16[128,640]{1,0:T(8,128)(2,1)S(1)} %constant_dynamic-update-slice_fusion), channel_id=1, source_target_pairs={{64,0},{80,16},{96,32},{112,48},{128,64},{144,80},{160,96},{176,11... | collective-permute-start | bytes 491528 | tf_op jit(solution)/shard_map/ppermute | solution.py:45
  43.5 2.8 %collective-permute-start.10 = (bf16[128,640]{1,0:T(8,128)(2,1)S(1)}, bf16[128,640]{1,0:T(8,128)(2,1)S(1)}, u32[]{:S(2)}, u32[]{:S(2)}) collective-permute-start(bf16[128,640]{1,0:T(8,128)(2,1)S(1)} %constant_dynamic-update-slice_fusion), channel_id=1, source_target_pairs={{80,0},{112,32},{144,64},{176,96},{208,128},{240,160},{272,192},{3... | collective-permute-start | bytes 491528 | tf_op jit(solution)/shard_map/ppermute | solution.py:45
  46.5 2.9 %collective-permute-done.9 = bf16[128,640]{1,0:T(8,128)(2,1)S(1)} collective-permute-done((bf16[128,640]{1,0:T(8,128)(2,1)S(1)}, bf16[128,640]{1,0:T(8,128)(2,1)S(1)}, u32[]{:S(2)}, u32[]{:S(2)}) %collective-permute-start.9) | collective-permute-done | bytes 163872 | tf_op jit(solution)/shard_map/ppermute | solution.py:45
  49.4 1.4 collective-permute-done.10
  50.8 2.0 %constant_dynamic-slice_fusion.20 = (bf16[2,128,640]{2,1,0:T(8,128)(2,1)S(1)}, bf16[2,128,640]{2,1,0:T(8,128)(2,1)S(1)}, bf16[2,128,640]{2,1,0:T(8,128)(2,1)S(1)}) fusion(bf16[11,128,640]{2,1,0:T(8,128)(2,1)S(1)} %bitcast_dynamic-update-slice_fusion, s32[]{:T(128)} %bitcast.12, s32[]{:T(128)} %bitcast.16, s32[]{:T(128)} %bitcast.14), kind=kLoop, calls=%fused_computation.113 | loop fusion | bytes 1966092 | tf_op jit(solution)/shard_map/dynamic_slice | solution.py:14
  52.8 0.2 maximum_convert_fusion
  52.9 0.2 slice_reduce_fusion
  53.2 0.4 multiply_reduce_fusion
  53.6 22.2 %all-gather.1 = f32[16,2,896]{2,1,0:T(2,128)S(1)} all-gather(f32[1,2,896]{2,1,0:T(2,128)S(1)} %maximum_bitcast_fusion), channel_id=2, replica_groups=mesh['lon'=32,'tz'=8,'tc'=2] {'tz','tc'}, dimensions={0}, use_global_device_ids=true | all-gather | bytes 121856 | tf_op jit(solution)/shard_map/all_gather | solution.py:59
  75.8 0.1 slice_reduce_fusion.2
  76.0 0.4 select_convert_fusion
  76.5 2.4 %collective-permute-start.11 = (bf16[896,640]{1,0:T(8,128)(2,1)S(1)}, bf16[896,640]{1,0:T(8,128)(2,1)S(1)}, u32[]{:S(2)}, u32[]{:S(2)}) collective-permute-start(bf16[896,640]{1,0:T(8,128)(2,1)S(1)} %select_convert_fusion), channel_id=1, source_target_pairs={{0,1},{1,0},{2,3},{3,2},{4,5},{5,4},{6,7},{7,6},{8,9},{9,8},{10,11... | collective-permute-start | bytes 3440648 | tf_op jit(solution)/shard_map/ppermute | solution.py:72
  78.9 0.7 fusion.60
  85.3 0.1 broadcast_select_fusion
  85.5 0.1 fusion.9
  85.7 0.1 fusion.11
  85.9 0.7 constant_dynamic-slice_fusion
  86.6 17.9 %fusion.7 = bf16[768,2176]{1,0:T(8,128)(2,1)S(1)} fusion(bf16[896,640]{1,0:T(8,128)(2,1)S(1)} %broadcast_select_fusion, bf16[896,512]{1,0:T(8,128)(2,1)S(1)} %slice_select_fusion, bf16[256,1152]{1,0:T(8,128)(2,1)S(1)} %get-tuple-element.9, bf16[256,1024]{1,0:T(8,128)(2,1)S(1)} %get-tuple-element.11, bf16[256,1152]{1,0:T(8,128)(2,1)S(1)} %get-tuple-element.8, ...), kind=kLoop, calls=%fused_computation.15 | loop fusion | flops 35094528 | bytes 8224768 | tf_op jit(solution)/shard_map/concatenate | solution.py:99
  104.5 0.8 constant_dynamic-slice_fusion.1
  105.2 1.1 convolution_dynamic-update-slice_fusion.8
  106.3 1.1 convolution_dynamic-update-slice_fusion.7
  107.4 1.1 convolution_dynamic-update-slice_fusion.6
  108.5 1.1 convolution_dynamic-update-slice_fusion.5
  109.6 1.1 convolution_dynamic-update-slice_fusion.4
  110.6 1.1 convolution_dynamic-update-slice_fusion.3
  111.7 1.1 convolution_dynamic-update-slice_fusion.2
  112.8 1.1 convolution_dynamic-update-slice_fusion.1
  113.9 1.1 convolution_dynamic-update-slice_fusion
  115.0 1.2 copy-done
  116.3 0.6 dynamic_slice.72
  117.5 0.7 iota_compare_fusion.3
  118.2 40.6 %reduce-scatter.2.cloned.1.call-done = f32[8,6912]{1,0:T(8,128)} async-done(((f32[64,6912]{1,0:T(8,128)}), f32[8,6912]{1,0:T(8,128)}) %reduce-scatter.2.cloned.1.call-update) | async-done | bytes 221200 | tf_op jit(solution)/shard_map/reduce_scatter | solution.py:117
  158.8 1.2 multiply_reduce_fusion.1
  159.9 1.0 divide_bitcast_fusion
  161.0 0.7 copy.6
  (45 shorter events, 0.6 us)
Async XLA Ops:
  6.5 152.2 %reduce-scatter.2.cloned.1.call-start = ((), (), s32[]{:S(2)}) async-start(), calls=%async_computation.1 | async-start | bytes 1990656 | tf_op jit(solution)/shard_map/reduce_scatter | solution.py:117
  7.3 3.1 %collective-permute-start = (bf16[128,128]{1,0:T(8,128)(2,1)S(1)}, bf16[128,128]{1,0:T(8,128)(2,1)S(1)}, u32[]{:S(2)}, u32[]{:S(2)}) collective-permute-start(bf16[128,128]{1,0:T(8,128)(2,1)S(1)} %slice.88), channel_id=1, source_target_pairs={{1,0},{2,1},{3,2},{4,3},{5,4},{6,5},{7,6},{8,7},{9,8},{10,9},{11,1... | collective-permute-start | bytes 98312 | tf_op jit(solution)/shard_map/ppermute | solution.py:27
  10.4 19.5 %collective-permute-start.1 = (bf16[128,640]{1,0:T(8,128)(2,1)S(1)}, bf16[128,640]{1,0:T(8,128)(2,1)S(1)}, u32[]{:S(2)}, u32[]{:S(2)}) collective-permute-start(bf16[128,640]{1,0:T(8,128)(2,1)S(1)} %constant_dynamic-update-slice_fusion), channel_id=1, source_target_pairs={{448,16},{480,48},{0,80},{32,112},{64,144},{96,176},{128,208},{160... | collective-permute-start | bytes 491528 | tf_op jit(solution)/shard_map/ppermute | solution.py:45
  12.4 21.5 %collective-permute-start.2 = (bf16[128,640]{1,0:T(8,128)(2,1)S(1)}, bf16[128,640]{1,0:T(8,128)(2,1)S(1)}, u32[]{:S(2)}, u32[]{:S(2)}) collective-permute-start(bf16[128,640]{1,0:T(8,128)(2,1)S(1)} %constant_dynamic-update-slice_fusion), channel_id=1, source_target_pairs={{448,0},{464,16},{480,32},{496,48},{0,64},{16,80},{32,96},{48,112}... | collective-permute-start | bytes 491528 | tf_op jit(solution)/shard_map/ppermute | solution.py:45
  15.9 20.0 %collective-permute-start.3 = (bf16[128,640]{1,0:T(8,128)(2,1)S(1)}, bf16[128,640]{1,0:T(8,128)(2,1)S(1)}, u32[]{:S(2)}, u32[]{:S(2)}) collective-permute-start(bf16[128,640]{1,0:T(8,128)(2,1)S(1)} %constant_dynamic-update-slice_fusion), channel_id=1, source_target_pairs={{464,0},{480,16},{496,32},{0,48},{16,64},{32,80},{48,96},{64,112},... | collective-permute-start | bytes 491528 | tf_op jit(solution)/shard_map/ppermute | solution.py:45
  22.5 17.9 %collective-permute-start.4 = (bf16[128,640]{1,0:T(8,128)(2,1)S(1)}, bf16[128,640]{1,0:T(8,128)(2,1)S(1)}, u32[]{:S(2)}, u32[]{:S(2)}) collective-permute-start(bf16[128,640]{1,0:T(8,128)(2,1)S(1)} %constant_dynamic-update-slice_fusion), channel_id=1, source_target_pairs={{480,0},{496,16},{0,32},{16,48},{32,64},{48,80},{64,96},{80,112},{... | collective-permute-start | bytes 491528 | tf_op jit(solution)/shard_map/ppermute | solution.py:45
  28.0 15.5 %collective-permute-start.5 = (bf16[128,640]{1,0:T(8,128)(2,1)S(1)}, bf16[128,640]{1,0:T(8,128)(2,1)S(1)}, u32[]{:S(2)}, u32[]{:S(2)}) collective-permute-start(bf16[128,640]{1,0:T(8,128)(2,1)S(1)} %constant_dynamic-update-slice_fusion), channel_id=1, source_target_pairs={{496,0},{0,16},{16,32},{32,48},{48,64},{64,80},{80,96},{96,112},{1... | collective-permute-start | bytes 491528 | tf_op jit(solution)/shard_map/ppermute | solution.py:45
  29.9 16.4 %collective-permute-start.6 = (bf16[128,640]{1,0:T(8,128)(2,1)S(1)}, bf16[128,640]{1,0:T(8,128)(2,1)S(1)}, u32[]{:S(2)}, u32[]{:S(2)}) collective-permute-start(bf16[128,640]{1,0:T(8,128)(2,1)S(1)} %constant_dynamic-update-slice_fusion), channel_id=1, source_target_pairs={{16,0},{32,16},{48,32},{64,48},{80,64},{96,80},{112,96},{128,112},... | collective-permute-start | bytes 491528 | tf_op jit(solution)/shard_map/ppermute | solution.py:45
  33.9 12.5 %collective-permute-start.7 = (bf16[128,640]{1,0:T(8,128)(2,1)S(1)}, bf16[128,640]{1,0:T(8,128)(2,1)S(1)}, u32[]{:S(2)}, u32[]{:S(2)}) collective-permute-start(bf16[128,640]{1,0:T(8,128)(2,1)S(1)} %constant_dynamic-update-slice_fusion), channel_id=1, source_target_pairs={{32,0},{48,16},{64,32},{80,48},{96,64},{112,80},{128,96},{144,112}... | collective-permute-start | bytes 491528 | tf_op jit(solution)/shard_map/ppermute | solution.py:45
  35.9 10.5 %collective-permute-start.8 = (bf16[128,640]{1,0:T(8,128)(2,1)S(1)}, bf16[128,640]{1,0:T(8,128)(2,1)S(1)}, u32[]{:S(2)}, u32[]{:S(2)}) collective-permute-start(bf16[128,640]{1,0:T(8,128)(2,1)S(1)} %constant_dynamic-update-slice_fusion), channel_id=1, source_target_pairs={{48,0},{64,16},{80,32},{96,48},{112,64},{128,80},{144,96},{160,112... | collective-permute-start | bytes 491528 | tf_op jit(solution)/shard_map/ppermute | solution.py:45
  40.4 9.0 %collective-permute-start.9 = (bf16[128,640]{1,0:T(8,128)(2,1)S(1)}, bf16[128,640]{1,0:T(8,128)(2,1)S(1)}, u32[]{:S(2)}, u32[]{:S(2)}) collective-permute-start(bf16[128,640]{1,0:T(8,128)(2,1)S(1)} %constant_dynamic-update-slice_fusion), channel_id=1, source_target_pairs={{64,0},{80,16},{96,32},{112,48},{128,64},{144,80},{160,96},{176,11... | collective-permute-start | bytes 491528 | tf_op jit(solution)/shard_map/ppermute | solution.py:45
  43.5 7.3 %collective-permute-start.10 = (bf16[128,640]{1,0:T(8,128)(2,1)S(1)}, bf16[128,640]{1,0:T(8,128)(2,1)S(1)}, u32[]{:S(2)}, u32[]{:S(2)}) collective-permute-start(bf16[128,640]{1,0:T(8,128)(2,1)S(1)} %constant_dynamic-update-slice_fusion), channel_id=1, source_target_pairs={{80,0},{112,32},{144,64},{176,96},{208,128},{240,160},{272,192},{3... | collective-permute-start | bytes 491528 | tf_op jit(solution)/shard_map/ppermute | solution.py:45
  53.2 25.8 %copy-start.1 = (s32[9]{0:T(128)S(1)}, s32[9]{0:T(128)}, u32[]{:S(2)}) copy-start(s32[9]{0:T(128)} %param.7) | copy-start | bytes 112
  76.5 8.8 %collective-permute-start.11 = (bf16[896,640]{1,0:T(8,128)(2,1)S(1)}, bf16[896,640]{1,0:T(8,128)(2,1)S(1)}, u32[]{:S(2)}, u32[]{:S(2)}) collective-permute-start(bf16[896,640]{1,0:T(8,128)(2,1)S(1)} %select_convert_fusion), channel_id=1, source_target_pairs={{0,1},{1,0},{2,3},{3,2},{4,5},{5,4},{6,7},{7,6},{8,9},{9,8},{10,11... | collective-permute-start | bytes 3440648 | tf_op jit(solution)/shard_map/ppermute | solution.py:72
  113.9 2.4 %copy-start.2 = (s32[16]{0:T(128)S(1)}, s32[16]{0:T(128)}, u32[]{:S(2)}) copy-start(s32[16]{0:T(128)} %param.6) | copy-start | bytes 196
  115.0 1.2 copy-start
Sparse Core Ops, SparseCore 0:
  116.4 42.3 reduce-scatter.1

commit v6 on v5

--- a/solution.py
+++ b/solution.py
@@ -70,19 +70,14 @@
     ).astype(jnp.bfloat16)
 
     other = lax.ppermute(standardized, "tc", [(0, 1), (1, 0)])
-    first = core == 0
-    window = jnp.concatenate(
-        [
-            jnp.where(first, standardized[:, :days_dev], other[:, :days_dev]),
-            jnp.where(first, other, standardized),
-        ],
-        1,
-    )
+    pair = jnp.stack([standardized, other], 0)
+    earlier = dslice(pair, core, 1, 0)[0]
+    later = dslice(pair, 1 - core, 1, 0)[0]
     span = 2 * days_dev
     out_rows = half_rows // tm_size
-    own = window[:half_rows].reshape(tz_size, 2, out_rows, span + LMAX)
+    own = jnp.concatenate([earlier[:half_rows, :days_dev], later[:half_rows]], 1)
+    own = own.reshape(tz_size, 2, out_rows, span + LMAX)
     own = dslice(own, core, 1, 1).reshape(half_rows // 2, span + LMAX)
-    columns_all = window[half_rows:]
 
     padded = jnp.concatenate(
         [
@@ -92,11 +87,11 @@
         ],
         1,
     )
-    right_rows = []
-    for slot_index in range(K_SLOTS):
-        columns = columns_all[slot_index * block_width:][:block_width]
-        right_rows.append(jnp.concatenate([columns, columns[:, :span]], 1))
-    right = jnp.concatenate(right_rows, 0)
+    early_columns = earlier[half_rows:, :days_dev]
+    late_columns = later[half_rows:]
+    right = jnp.concatenate(
+        [early_columns, late_columns, early_columns, late_columns[:, :days_dev]], 1
+    )
     pieces = []
     for lag_index in range(NLAG):
         lag_days = lax.min(lag_set[lag_index], LMAX)

time: 169 us -> 152 us (0.90)
  other arithmetic: 23.5 us -> 6.57 us
    concatenate x4 -> x0, other arithmetic: 18.2 us -> none  [the longest x1 17.9 us: local(): right = jnp.concatenate(right_rows, 0)]
where the time goes in v6:
time: 152 us
  waiting for transfers between devices  44.9 us (30%)
  starting transfers between devices  38.5 us (25%)
  blocking collectives  22.2 us (15%)
  between operations  20.2 us (13%)
  matrix products  9.8 us (6%)
  local copies, waits for them, and re-layouts  9.46 us (6%)
  other arithmetic  6.57 us (4%)
    reduce_scatter x1, waiting for transfers between devices, local(): comoment = lax.psum_scatter(product, 'tz', scatter_dimension=0, tiled=True)  40.6 us
    ppermute x10, starting transfers between devices, local(): halves.append(lax.ppermute(extended, 'lon', pairs))  34.9 us
    all_gather x1, blocking collectives, local(): stats = lax.all_gather(jnp.stack([shard_mean, shard_square], 0), TIME)  22.2 us
    dot_general x9, matrix products, local(): lax.dot_general(left, right, (((1,), (1,)), ((), ())), preferred_element_...  9.8 us
    ppermute x10, waiting for transfers between devices, local(): halves.append(lax.ppermute(extended, 'lon', pairs))  4.31 us
    dynamic_slice x4, local copies, waits for them, and re-layouts, dslice(): lax.dynamic_slice_in_dim(value, start, size, axis, allow_negative_indices...  4.01 us
  transfers between devices with their start and end apart: 13, of which 3 were waited for; matrix products, arithmetic and copies ran while one was open for 3% of the time, Pallas kernels for 0%

profile of v6, /device:TPU:6, one launch (start us, length us, event | category | flops | bytes accessed | tf_op | source)
XLA Modules:
  0.0 151.6 jit_solution(6545609814434203)
XLA Ops:
  6.5 0.8 slice.71
  7.3 1.3 collective-permute-start
  8.6 0.9 fusion.37
  9.5 0.9 constant_dynamic-update-slice_fusion.1
  10.4 1.3 collective-permute-start.1
  11.7 0.7 fusion.52
  12.4 3.5 %collective-permute-start.2 = (bf16[128,640]{1,0:T(8,128)(2,1)S(1)}, bf16[128,640]{1,0:T(8,128)(2,1)S(1)}, u32[]{:S(2)}, u32[]{:S(2)}) collective-permute-start(bf16[128,640]{1,0:T(8,128)(2,1)S(1)} %constant_dynamic-update-slice_fusion), channel_id=1, source_target_pairs={{448,0},{464,16},{480,32},{496,48},{0,64},{16,80},{32,96},{48,112}... | collective-permute-start | bytes 491528 | tf_op jit(solution)/shard_map/ppermute | solution.py:45
  15.9 6.6 %collective-permute-start.3 = (bf16[128,640]{1,0:T(8,128)(2,1)S(1)}, bf16[128,640]{1,0:T(8,128)(2,1)S(1)}, u32[]{:S(2)}, u32[]{:S(2)}) collective-permute-start(bf16[128,640]{1,0:T(8,128)(2,1)S(1)} %constant_dynamic-update-slice_fusion), channel_id=1, source_target_pairs={{464,0},{480,16},{496,32},{0,48},{16,64},{32,80},{48,96},{64,112},... | collective-permute-start | bytes 491528 | tf_op jit(solution)/shard_map/ppermute | solution.py:45
  22.5 5.5 %collective-permute-start.4 = (bf16[128,640]{1,0:T(8,128)(2,1)S(1)}, bf16[128,640]{1,0:T(8,128)(2,1)S(1)}, u32[]{:S(2)}, u32[]{:S(2)}) collective-permute-start(bf16[128,640]{1,0:T(8,128)(2,1)S(1)} %constant_dynamic-update-slice_fusion), channel_id=1, source_target_pairs={{480,0},{496,16},{0,32},{16,48},{32,64},{48,80},{64,96},{80,112},{... | collective-permute-start | bytes 491528 | tf_op jit(solution)/shard_map/ppermute | solution.py:45
  28.0 1.9 %collective-permute-start.5 = (bf16[128,640]{1,0:T(8,128)(2,1)S(1)}, bf16[128,640]{1,0:T(8,128)(2,1)S(1)}, u32[]{:S(2)}, u32[]{:S(2)}) collective-permute-start(bf16[128,640]{1,0:T(8,128)(2,1)S(1)} %constant_dynamic-update-slice_fusion), channel_id=1, source_target_pairs={{496,0},{0,16},{16,32},{32,48},{48,64},{64,80},{80,96},{96,112},{1... | collective-permute-start | bytes 491528 | tf_op jit(solution)/shard_map/ppermute | solution.py:45
  29.9 3.9 %collective-permute-start.6 = (bf16[128,640]{1,0:T(8,128)(2,1)S(1)}, bf16[128,640]{1,0:T(8,128)(2,1)S(1)}, u32[]{:S(2)}, u32[]{:S(2)}) collective-permute-start(bf16[128,640]{1,0:T(8,128)(2,1)S(1)} %constant_dynamic-update-slice_fusion), channel_id=1, source_target_pairs={{16,0},{32,16},{48,32},{64,48},{80,64},{96,80},{112,96},{128,112},... | collective-permute-start | bytes 491528 | tf_op jit(solution)/shard_map/ppermute | solution.py:45
  33.9 1.9 %collective-permute-start.7 = (bf16[128,640]{1,0:T(8,128)(2,1)S(1)}, bf16[128,640]{1,0:T(8,128)(2,1)S(1)}, u32[]{:S(2)}, u32[]{:S(2)}) collective-permute-start(bf16[128,640]{1,0:T(8,128)(2,1)S(1)} %constant_dynamic-update-slice_fusion), channel_id=1, source_target_pairs={{32,0},{48,16},{64,32},{80,48},{96,64},{112,80},{128,96},{144,112}... | collective-permute-start | bytes 491528 | tf_op jit(solution)/shard_map/ppermute | solution.py:45
  35.9 4.5 %collective-permute-start.8 = (bf16[128,640]{1,0:T(8,128)(2,1)S(1)}, bf16[128,640]{1,0:T(8,128)(2,1)S(1)}, u32[]{:S(2)}, u32[]{:S(2)}) collective-permute-start(bf16[128,640]{1,0:T(8,128)(2,1)S(1)} %constant_dynamic-update-slice_fusion), channel_id=1, source_target_pairs={{48,0},{64,16},{80,32},{96,48},{112,64},{128,80},{144,96},{160,112... | collective-permute-start | bytes 491528 | tf_op jit(solution)/shard_map/ppermute | solution.py:45
  40.4 3.0 %collective-permute-start.9 = (bf16[128,640]{1,0:T(8,128)(2,1)S(1)}, bf16[128,640]{1,0:T(8,128)(2,1)S(1)}, u32[]{:S(2)}, u32[]{:S(2)}) collective-permute-start(bf16[128,640]{1,0:T(8,128)(2,1)S(1)} %constant_dynamic-update-slice_fusion), channel_id=1, source_target_pairs={{64,0},{80,16},{96,32},{112,48},{128,64},{144,80},{160,96},{176,11... | collective-permute-start | bytes 491528 | tf_op jit(solution)/shard_map/ppermute | solution.py:45
  43.5 2.8 %collective-permute-start.10 = (bf16[128,640]{1,0:T(8,128)(2,1)S(1)}, bf16[128,640]{1,0:T(8,128)(2,1)S(1)}, u32[]{:S(2)}, u32[]{:S(2)}) collective-permute-start(bf16[128,640]{1,0:T(8,128)(2,1)S(1)} %constant_dynamic-update-slice_fusion), channel_id=1, source_target_pairs={{80,0},{112,32},{144,64},{176,96},{208,128},{240,160},{272,192},{3... | collective-permute-start | bytes 491528 | tf_op jit(solution)/shard_map/ppermute | solution.py:45
  46.5 2.9 %collective-permute-done.9 = bf16[128,640]{1,0:T(8,128)(2,1)S(1)} collective-permute-done((bf16[128,640]{1,0:T(8,128)(2,1)S(1)}, bf16[128,640]{1,0:T(8,128)(2,1)S(1)}, u32[]{:S(2)}, u32[]{:S(2)}) %collective-permute-start.9) | collective-permute-done | bytes 163872 | tf_op jit(solution)/shard_map/ppermute | solution.py:45
  49.4 1.4 collective-permute-done.10
  50.8 2.0 %constant_dynamic-slice_fusion.20 = (bf16[2,128,640]{2,1,0:T(8,128)(2,1)S(1)}, bf16[2,128,640]{2,1,0:T(8,128)(2,1)S(1)}, bf16[2,128,640]{2,1,0:T(8,128)(2,1)S(1)}) fusion(bf16[11,128,640]{2,1,0:T(8,128)(2,1)S(1)} %bitcast_dynamic-update-slice_fusion, s32[]{:T(128)} %bitcast.12, s32[]{:T(128)} %bitcast.16, s32[]{:T(128)} %bitcast.14), kind=kLoop, calls=%fused_computation.96 | loop fusion | bytes 1966092 | tf_op jit(solution)/shard_map/dynamic_slice | solution.py:14
  52.8 0.2 maximum_convert_fusion
  53.0 0.2 slice_reduce_fusion
  53.2 0.4 multiply_reduce_fusion
  53.6 22.2 %all-gather.1 = f32[16,2,896]{2,1,0:T(2,128)S(1)} all-gather(f32[1,2,896]{2,1,0:T(2,128)S(1)} %maximum_bitcast_fusion), channel_id=2, replica_groups=mesh['lon'=32,'tz'=8,'tc'=2] {'tz','tc'}, dimensions={0}, use_global_device_ids=true | all-gather | bytes 121856 | tf_op jit(solution)/shard_map/all_gather | solution.py:59
  75.9 0.1 slice_reduce_fusion.2
  76.1 0.4 select_convert_fusion
  76.5 2.3 %collective-permute-start.11 = (bf16[896,640]{1,0:T(8,128)(2,1)S(1)}, bf16[896,640]{1,0:T(8,128)(2,1)S(1)}, u32[]{:S(2)}, u32[]{:S(2)}) collective-permute-start(bf16[896,640]{1,0:T(8,128)(2,1)S(1)} %select_convert_fusion), channel_id=1, source_target_pairs={{0,1},{1,0},{2,3},{3,2},{4,5},{5,4},{6,7},{7,6},{8,9},{9,8},{10,11... | collective-permute-start | bytes 3440648 | tf_op jit(solution)/shard_map/ppermute | solution.py:72
  78.8 0.7 fusion.51
  85.1 0.4 select_convert_fusion.1
  85.5 1.0 fusion
  86.5 0.1 slice_bitcast_fusion
  86.7 0.7 constant_dynamic-slice_fusion
  87.4 0.1 slice.102
  87.5 0.7 constant_dynamic-slice_fusion.1
  88.2 1.1 convolution_dynamic-update-slice_fusion.8
  89.3 1.1 convolution_dynamic-update-slice_fusion.7
  90.4 1.1 convolution_dynamic-update-slice_fusion.6
  91.5 1.1 convolution_dynamic-update-slice_fusion.5
  92.6 1.1 convolution_dynamic-update-slice_fusion.4
  93.7 1.1 convolution_dynamic-update-slice_fusion.3
  94.8 1.1 convolution_dynamic-update-slice_fusion.2
  95.9 1.1 convolution_dynamic-update-slice_fusion.1
  97.0 1.1 convolution_dynamic-update-slice_fusion
  98.1 1.2 copy-done
  99.3 0.6 dynamic_slice.78
  100.6 0.7 iota_compare_fusion.1
  101.2 40.6 %reduce-scatter.2.cloned.1.call-done = f32[8,6912]{1,0:T(8,128)} async-done(((f32[64,6912]{1,0:T(8,128)}), f32[8,6912]{1,0:T(8,128)}) %reduce-scatter.2.cloned.1.call-update) | async-done | bytes 221200 | tf_op jit(solution)/shard_map/reduce_scatter | solution.py:112
  141.8 1.2 multiply_reduce_fusion.1
  143.0 1.0 divide_bitcast_fusion
  144.1 0.7 copy.6
  (46 shorter events, 0.5 us)
Async XLA Ops:
  6.5 135.3 %reduce-scatter.2.cloned.1.call-start = ((), (), s32[]{:S(2)}) async-start(), calls=%async_computation.1 | async-start | bytes 1990656 | tf_op jit(solution)/shard_map/reduce_scatter | solution.py:112
  7.3 3.1 %collective-permute-start = (bf16[128,128]{1,0:T(8,128)(2,1)S(1)}, bf16[128,128]{1,0:T(8,128)(2,1)S(1)}, u32[]{:S(2)}, u32[]{:S(2)}) collective-permute-start(bf16[128,128]{1,0:T(8,128)(2,1)S(1)} %slice.71), channel_id=1, source_target_pairs={{1,0},{2,1},{3,2},{4,3},{5,4},{6,5},{7,6},{8,7},{9,8},{10,9},{11,1... | collective-permute-start | bytes 98312 | tf_op jit(solution)/shard_map/ppermute | solution.py:27
  10.4 19.5 %collective-permute-start.1 = (bf16[128,640]{1,0:T(8,128)(2,1)S(1)}, bf16[128,640]{1,0:T(8,128)(2,1)S(1)}, u32[]{:S(2)}, u32[]{:S(2)}) collective-permute-start(bf16[128,640]{1,0:T(8,128)(2,1)S(1)} %constant_dynamic-update-slice_fusion), channel_id=1, source_target_pairs={{448,16},{480,48},{0,80},{32,112},{64,144},{96,176},{128,208},{160... | collective-permute-start | bytes 491528 | tf_op jit(solution)/shard_map/ppermute | solution.py:45
  12.4 21.5 %collective-permute-start.2 = (bf16[128,640]{1,0:T(8,128)(2,1)S(1)}, bf16[128,640]{1,0:T(8,128)(2,1)S(1)}, u32[]{:S(2)}, u32[]{:S(2)}) collective-permute-start(bf16[128,640]{1,0:T(8,128)(2,1)S(1)} %constant_dynamic-update-slice_fusion), channel_id=1, source_target_pairs={{448,0},{464,16},{480,32},{496,48},{0,64},{16,80},{32,96},{48,112}... | collective-permute-start | bytes 491528 | tf_op jit(solution)/shard_map/ppermute | solution.py:45
  15.9 20.0 %collective-permute-start.3 = (bf16[128,640]{1,0:T(8,128)(2,1)S(1)}, bf16[128,640]{1,0:T(8,128)(2,1)S(1)}, u32[]{:S(2)}, u32[]{:S(2)}) collective-permute-start(bf16[128,640]{1,0:T(8,128)(2,1)S(1)} %constant_dynamic-update-slice_fusion), channel_id=1, source_target_pairs={{464,0},{480,16},{496,32},{0,48},{16,64},{32,80},{48,96},{64,112},... | collective-permute-start | bytes 491528 | tf_op jit(solution)/shard_map/ppermute | solution.py:45
  22.5 17.9 %collective-permute-start.4 = (bf16[128,640]{1,0:T(8,128)(2,1)S(1)}, bf16[128,640]{1,0:T(8,128)(2,1)S(1)}, u32[]{:S(2)}, u32[]{:S(2)}) collective-permute-start(bf16[128,640]{1,0:T(8,128)(2,1)S(1)} %constant_dynamic-update-slice_fusion), channel_id=1, source_target_pairs={{480,0},{496,16},{0,32},{16,48},{32,64},{48,80},{64,96},{80,112},{... | collective-permute-start | bytes 491528 | tf_op jit(solution)/shard_map/ppermute | solution.py:45
  28.0 15.5 %collective-permute-start.5 = (bf16[128,640]{1,0:T(8,128)(2,1)S(1)}, bf16[128,640]{1,0:T(8,128)(2,1)S(1)}, u32[]{:S(2)}, u32[]{:S(2)}) collective-permute-start(bf16[128,640]{1,0:T(8,128)(2,1)S(1)} %constant_dynamic-update-slice_fusion), channel_id=1, source_target_pairs={{496,0},{0,16},{16,32},{32,48},{48,64},{64,80},{80,96},{96,112},{1... | collective-permute-start | bytes 491528 | tf_op jit(solution)/shard_map/ppermute | solution.py:45
  29.9 16.4 %collective-permute-start.6 = (bf16[128,640]{1,0:T(8,128)(2,1)S(1)}, bf16[128,640]{1,0:T(8,128)(2,1)S(1)}, u32[]{:S(2)}, u32[]{:S(2)}) collective-permute-start(bf16[128,640]{1,0:T(8,128)(2,1)S(1)} %constant_dynamic-update-slice_fusion), channel_id=1, source_target_pairs={{16,0},{32,16},{48,32},{64,48},{80,64},{96,80},{112,96},{128,112},... | collective-permute-start | bytes 491528 | tf_op jit(solution)/shard_map/ppermute | solution.py:45
  33.9 12.5 %collective-permute-start.7 = (bf16[128,640]{1,0:T(8,128)(2,1)S(1)}, bf16[128,640]{1,0:T(8,128)(2,1)S(1)}, u32[]{:S(2)}, u32[]{:S(2)}) collective-permute-start(bf16[128,640]{1,0:T(8,128)(2,1)S(1)} %constant_dynamic-update-slice_fusion), channel_id=1, source_target_pairs={{32,0},{48,16},{64,32},{80,48},{96,64},{112,80},{128,96},{144,112}... | collective-permute-start | bytes 491528 | tf_op jit(solution)/shard_map/ppermute | solution.py:45
  35.9 10.5 %collective-permute-start.8 = (bf16[128,640]{1,0:T(8,128)(2,1)S(1)}, bf16[128,640]{1,0:T(8,128)(2,1)S(1)}, u32[]{:S(2)}, u32[]{:S(2)}) collective-permute-start(bf16[128,640]{1,0:T(8,128)(2,1)S(1)} %constant_dynamic-update-slice_fusion), channel_id=1, source_target_pairs={{48,0},{64,16},{80,32},{96,48},{112,64},{128,80},{144,96},{160,112... | collective-permute-start | bytes 491528 | tf_op jit(solution)/shard_map/ppermute | solution.py:45
  40.4 9.0 %collective-permute-start.9 = (bf16[128,640]{1,0:T(8,128)(2,1)S(1)}, bf16[128,640]{1,0:T(8,128)(2,1)S(1)}, u32[]{:S(2)}, u32[]{:S(2)}) collective-permute-start(bf16[128,640]{1,0:T(8,128)(2,1)S(1)} %constant_dynamic-update-slice_fusion), channel_id=1, source_target_pairs={{64,0},{80,16},{96,32},{112,48},{128,64},{144,80},{160,96},{176,11... | collective-permute-start | bytes 491528 | tf_op jit(solution)/shard_map/ppermute | solution.py:45
  43.5 7.3 %collective-permute-start.10 = (bf16[128,640]{1,0:T(8,128)(2,1)S(1)}, bf16[128,640]{1,0:T(8,128)(2,1)S(1)}, u32[]{:S(2)}, u32[]{:S(2)}) collective-permute-start(bf16[128,640]{1,0:T(8,128)(2,1)S(1)} %constant_dynamic-update-slice_fusion), channel_id=1, source_target_pairs={{80,0},{112,32},{144,64},{176,96},{208,128},{240,160},{272,192},{3... | collective-permute-start | bytes 491528 | tf_op jit(solution)/shard_map/ppermute | solution.py:45
  53.2 25.6 %copy-start.1 = (s32[9]{0:T(128)S(1)}, s32[9]{0:T(128)}, u32[]{:S(2)}) copy-start(s32[9]{0:T(128)} %param.7) | copy-start | bytes 112
  76.5 9.0 %collective-permute-start.11 = (bf16[896,640]{1,0:T(8,128)(2,1)S(1)}, bf16[896,640]{1,0:T(8,128)(2,1)S(1)}, u32[]{:S(2)}, u32[]{:S(2)}) collective-permute-start(bf16[896,640]{1,0:T(8,128)(2,1)S(1)} %select_convert_fusion), channel_id=1, source_target_pairs={{0,1},{1,0},{2,3},{3,2},{4,5},{5,4},{6,7},{7,6},{8,9},{9,8},{10,11... | collective-permute-start | bytes 3440648 | tf_op jit(solution)/shard_map/ppermute | solution.py:72
  97.0 2.4 %copy-start.2 = (s32[16]{0:T(128)S(1)}, s32[16]{0:T(128)}, u32[]{:S(2)}) copy-start(s32[16]{0:T(128)} %param.6) | copy-start | bytes 196
  98.1 1.2 copy-start
Sparse Core Ops, SparseCore 0:
  99.4 42.3 reduce-scatter.1

commit v7 on v6

--- a/solution.py
+++ b/solution.py
@@ -22,7 +22,6 @@
     blocks = lon_size // 2
     block_width = 2 * half_rows
     total_days = days_dev * tm_size
-    tm_index = lax.axis_index("tz") * 2 + lax.axis_index("tc")
     core = lax.axis_index("tc")
     margin = lax.ppermute(
         anomalies[:, :LMAX], TIME, [(i, i - 1) for i in range(1, tm_size)]
@@ -53,9 +52,10 @@
         pair = dslice(halves, firsts[slot_index], 2, 0)
         slot_blocks.append(pair.reshape(block_width, days_dev + LMAX))
     raw = jnp.concatenate([extended] + slot_blocks, 0)
-    values = raw.astype(jnp.float32)
-    shard_mean = jnp.mean(values[:, :days_dev], axis=1)
-    shard_square = jnp.sum(jnp.square(values[:, :days_dev] - shard_mean[:, None]), axis=1)
+    other = lax.ppermute(raw, "tc", [(0, 1), (1, 0)])
+    values = raw[:, :days_dev].astype(jnp.float32)
+    shard_mean = jnp.mean(values, axis=1)
+    shard_square = jnp.sum(jnp.square(values - shard_mean[:, None]), axis=1)
     stats = lax.all_gather(jnp.stack([shard_mean, shard_square], 0), TIME)
     means, squares = stats[:, 0], stats[:, 1]
     point_mean = jnp.mean(means, axis=0)
@@ -63,21 +63,21 @@
         jnp.square(means - point_mean[None, :]), axis=0
     )
     spread = jnp.sqrt(point_m2 / total_days + 1e-06)
-    day = lax.broadcasted_iota(jnp.int32, (1, days_dev + LMAX), 1)
-    inside = (day < days_dev) | (tm_index < tm_size - 1)
-    standardized = jnp.where(
-        inside, (values - point_mean[:, None]) / spread[:, None], 0.0
-    ).astype(jnp.bfloat16)
 
-    other = lax.ppermute(standardized, "tc", [(0, 1), (1, 0)])
-    pair = jnp.stack([standardized, other], 0)
+    pair = jnp.stack([raw, other], 0)
     earlier = dslice(pair, core, 1, 0)[0]
     later = dslice(pair, 1 - core, 1, 0)[0]
     span = 2 * days_dev
+    window = jnp.concatenate([earlier[:, :days_dev], later], 1).astype(jnp.float32)
+    day = lax.broadcasted_iota(jnp.int32, (1, span + LMAX), 1)
+    inside = (day < span) | (lax.axis_index("tz") < tz_size - 1)
+    standardized = jnp.where(
+        inside, (window - point_mean[:, None]) / spread[:, None], 0.0
+    ).astype(jnp.bfloat16)
     out_rows = half_rows // tm_size
-    own = jnp.concatenate([earlier[:half_rows, :days_dev], later[:half_rows]], 1)
-    own = own.reshape(tz_size, 2, out_rows, span + LMAX)
+    own = standardized[:half_rows].reshape(tz_size, 2, out_rows, span + LMAX)
     own = dslice(own, core, 1, 1).reshape(half_rows // 2, span + LMAX)
+    columns = standardized[half_rows:]
 
     padded = jnp.concatenate(
         [
@@ -87,11 +87,7 @@
         ],
         1,
     )
-    early_columns = earlier[half_rows:, :days_dev]
-    late_columns = later[half_rows:]
-    right = jnp.concatenate(
-        [early_columns, late_columns, early_columns, late_columns[:, :days_dev]], 1
-    )
+    right = jnp.concatenate([columns, columns[:, :span]], 1)
     pieces = []
     for lag_index in range(NLAG):
         lag_days = lax.min(lag_set[lag_index], LMAX)

time: 152 us -> 154 us (1.013)
  transfers between devices with their start and end apart: 13 -> 13, of which waited for: 3 -> 3; matrix products, arithmetic and copies ran while one was open for 3% -> 4% of each run, Pallas kernels for 0% -> 0%
where the time goes in v7:
time: 154 us; the launch traced here: 153 us
  waiting for transfers between devices  44.3 us (29%)
  starting transfers between devices  38.1 us (25%)
  blocking collectives  22.9 us (15%)
  between operations  20.1 us (13%)
  local copies, waits for them, and re-layouts  10.7 us (7%)
  matrix products  9.83 us (6%)
  other arithmetic  6.97 us (5%)
    reduce_scatter x1, waiting for transfers between devices, local(): comoment = lax.psum_scatter(product, 'tz', scatter_dimension=0, tiled=True)  40.4 us
    ppermute x10, starting transfers between devices, local(): halves.append(lax.ppermute(extended, 'lon', pairs))  34.9 us
    all_gather x1, blocking collectives, local(): stats = lax.all_gather(jnp.stack([shard_mean, shard_square], 0), TIME)  22.9 us
    dot_general x9, matrix products, local(): lax.dot_general(left, right, (((1,), (1,)), ((), ())), preferred_element_...  9.83 us
    dynamic_slice x4, local copies, waits for them, and re-layouts, dslice(): lax.dynamic_slice_in_dim(value, start, size, axis, allow_negative_indices...  4.01 us
    ppermute x10, waiting for transfers between devices, local(): halves.append(lax.ppermute(extended, 'lon', pairs))  3.83 us
  transfers between devices with their start and end apart: 13, of which 3 were waited for; matrix products, arithmetic and copies ran while one was open for 4% of the time, Pallas kernels for 0%

profile of v7, /device:TPU:6, one launch (start us, length us, event | category | flops | bytes accessed | tf_op | source)
XLA Modules:
  0.0 152.9 jit_solution(8493081304935037064)
XLA Ops:
  6.5 0.8 slice.64
  7.3 1.3 collective-permute-start
  8.6 0.9 constant_dynamic-update-slice_fusion.1
  9.5 0.9 fusion.38
  10.4 1.7 %fusion.53 = (s32[1]{0:T(128)}, s32[1]{0:T(128)}, s32[1]{0:T(128)}, s32[1]{0:T(128)}, s32[1]{0:T(128)}, /*index=5*/s32[1]{0:T(128)}, s32[1]{0:T(128)}, s32[1]{0:T(128)}, s32[1]{0:T(128)}) fusion(s32[9]{0:T(128)} %param.7), kind=kLoop, calls=%fused_computation.124 | loop fusion | bytes 72 | tf_op jit(solution)/shard_map/slice | solution.py:93
  12.1 1.3 collective-permute-start.1
  19.0 0.6 fusion.54
  19.7 3.5 %collective-permute-start.2 = (bf16[128,640]{1,0:T(8,128)(2,1)S(1)}, bf16[128,640]{1,0:T(8,128)(2,1)S(1)}, u32[]{:S(2)}, u32[]{:S(2)}) collective-permute-start(bf16[128,640]{1,0:T(8,128)(2,1)S(1)} %constant_dynamic-update-slice_fusion), channel_id=1, source_target_pairs={{448,0},{464,16},{480,32},{496,48},{0,64},{16,80},{32,96},{48,112}... | collective-permute-start | bytes 491528 | tf_op jit(solution)/shard_map/ppermute | solution.py:44
  23.2 6.6 %collective-permute-start.3 = (bf16[128,640]{1,0:T(8,128)(2,1)S(1)}, bf16[128,640]{1,0:T(8,128)(2,1)S(1)}, u32[]{:S(2)}, u32[]{:S(2)}) collective-permute-start(bf16[128,640]{1,0:T(8,128)(2,1)S(1)} %constant_dynamic-update-slice_fusion), channel_id=1, source_target_pairs={{464,0},{480,16},{496,32},{0,48},{16,64},{32,80},{48,96},{64,112},... | collective-permute-start | bytes 491528 | tf_op jit(solution)/shard_map/ppermute | solution.py:44
  29.7 5.6 %collective-permute-start.4 = (bf16[128,640]{1,0:T(8,128)(2,1)S(1)}, bf16[128,640]{1,0:T(8,128)(2,1)S(1)}, u32[]{:S(2)}, u32[]{:S(2)}) collective-permute-start(bf16[128,640]{1,0:T(8,128)(2,1)S(1)} %constant_dynamic-update-slice_fusion), channel_id=1, source_target_pairs={{480,0},{496,16},{0,32},{16,48},{32,64},{48,80},{64,96},{80,112},{... | collective-permute-start | bytes 491528 | tf_op jit(solution)/shard_map/ppermute | solution.py:44
  35.3 1.9 %collective-permute-start.5 = (bf16[128,640]{1,0:T(8,128)(2,1)S(1)}, bf16[128,640]{1,0:T(8,128)(2,1)S(1)}, u32[]{:S(2)}, u32[]{:S(2)}) collective-permute-start(bf16[128,640]{1,0:T(8,128)(2,1)S(1)} %constant_dynamic-update-slice_fusion), channel_id=1, source_target_pairs={{496,0},{0,16},{16,32},{32,48},{48,64},{64,80},{80,96},{96,112},{1... | collective-permute-start | bytes 491528 | tf_op jit(solution)/shard_map/ppermute | solution.py:44
  37.2 3.9 %collective-permute-start.6 = (bf16[128,640]{1,0:T(8,128)(2,1)S(1)}, bf16[128,640]{1,0:T(8,128)(2,1)S(1)}, u32[]{:S(2)}, u32[]{:S(2)}) collective-permute-start(bf16[128,640]{1,0:T(8,128)(2,1)S(1)} %constant_dynamic-update-slice_fusion), channel_id=1, source_target_pairs={{16,0},{32,16},{48,32},{64,48},{80,64},{96,80},{112,96},{128,112},... | collective-permute-start | bytes 491528 | tf_op jit(solution)/shard_map/ppermute | solution.py:44
  41.2 1.9 %collective-permute-start.7 = (bf16[128,640]{1,0:T(8,128)(2,1)S(1)}, bf16[128,640]{1,0:T(8,128)(2,1)S(1)}, u32[]{:S(2)}, u32[]{:S(2)}) collective-permute-start(bf16[128,640]{1,0:T(8,128)(2,1)S(1)} %constant_dynamic-update-slice_fusion), channel_id=1, source_target_pairs={{32,0},{48,16},{64,32},{80,48},{96,64},{112,80},{128,96},{144,112}... | collective-permute-start | bytes 491528 | tf_op jit(solution)/shard_map/ppermute | solution.py:44
  43.2 4.5 %collective-permute-start.8 = (bf16[128,640]{1,0:T(8,128)(2,1)S(1)}, bf16[128,640]{1,0:T(8,128)(2,1)S(1)}, u32[]{:S(2)}, u32[]{:S(2)}) collective-permute-start(bf16[128,640]{1,0:T(8,128)(2,1)S(1)} %constant_dynamic-update-slice_fusion), channel_id=1, source_target_pairs={{48,0},{64,16},{80,32},{96,48},{112,64},{128,80},{144,96},{160,112... | collective-permute-start | bytes 491528 | tf_op jit(solution)/shard_map/ppermute | solution.py:44
  47.7 3.0 %collective-permute-start.9 = (bf16[128,640]{1,0:T(8,128)(2,1)S(1)}, bf16[128,640]{1,0:T(8,128)(2,1)S(1)}, u32[]{:S(2)}, u32[]{:S(2)}) collective-permute-start(bf16[128,640]{1,0:T(8,128)(2,1)S(1)} %constant_dynamic-update-slice_fusion), channel_id=1, source_target_pairs={{64,0},{80,16},{96,32},{112,48},{128,64},{144,80},{160,96},{176,11... | collective-permute-start | bytes 491528 | tf_op jit(solution)/shard_map/ppermute | solution.py:44
  50.8 2.8 %collective-permute-start.10 = (bf16[128,640]{1,0:T(8,128)(2,1)S(1)}, bf16[128,640]{1,0:T(8,128)(2,1)S(1)}, u32[]{:S(2)}, u32[]{:S(2)}) collective-permute-start(bf16[128,640]{1,0:T(8,128)(2,1)S(1)} %constant_dynamic-update-slice_fusion), channel_id=1, source_target_pairs={{80,0},{112,32},{144,64},{176,96},{208,128},{240,160},{272,192},{3... | collective-permute-start | bytes 491528 | tf_op jit(solution)/shard_map/ppermute | solution.py:44
  53.7 2.3 %collective-permute-done.9 = bf16[128,640]{1,0:T(8,128)(2,1)S(1)} collective-permute-done((bf16[128,640]{1,0:T(8,128)(2,1)S(1)}, bf16[128,640]{1,0:T(8,128)(2,1)S(1)}, u32[]{:S(2)}, u32[]{:S(2)}) %collective-permute-start.9) | collective-permute-done | bytes 163872 | tf_op jit(solution)/shard_map/ppermute | solution.py:44
  56.1 1.5 collective-permute-done.10
  57.6 2.0 %constant_dynamic-slice_fusion.20 = (bf16[2,128,640]{2,1,0:T(8,128)(2,1)S(1)}, bf16[2,128,640]{2,1,0:T(8,128)(2,1)S(1)}, bf16[2,128,640]{2,1,0:T(8,128)(2,1)S(1)}) fusion(bf16[11,128,640]{2,1,0:T(8,128)(2,1)S(1)} %bitcast_dynamic-update-slice_fusion, s32[]{:T(128)} %bitcast.12, s32[]{:T(128)} %bitcast.16, s32[]{:T(128)} %bitcast.14), kind=kLoop, calls=%fused_computation.96 | loop fusion | bytes 1966092 | tf_op jit(solution)/shard_map/dynamic_slice | solution.py:14
  59.6 0.2 pad_maximum_fusion.1
  59.8 0.2 convert_reduce_fusion
  60.0 1.9 %collective-permute-start.11 = (bf16[896,640]{1,0:T(8,128)(2,1)S(1)}, bf16[896,640]{1,0:T(8,128)(2,1)S(1)}, u32[]{:S(2)}, u32[]{:S(2)}) collective-permute-start(bf16[896,640]{1,0:T(8,128)(2,1)S(1)} %get-tuple-element.12), channel_id=1, source_target_pairs={{0,1},{1,0},{2,3},{3,2},{4,5},{5,4},{6,7},{7,6},{8,9},{9,8},{10,11... | collective-permute-start | bytes 3440648 | tf_op jit(solution)/shard_map/ppermute | solution.py:55
  62.0 0.5 fusion.1
  62.5 22.9 %all-gather.1 = f32[16,2,896]{2,1,0:T(2,128)S(1)} all-gather(f32[1,2,896]{2,1,0:T(2,128)S(1)} %maximum_bitcast_fusion), channel_id=2, replica_groups=mesh['lon'=32,'tz'=8,'tc'=2] {'tz','tc'}, dimensions={0}, use_global_device_ids=true | all-gather | bytes 121856 | tf_op jit(solution)/shard_map/all_gather | solution.py:59
  85.3 0.1 slice_reduce_fusion.1
  85.5 1.0 fusion.5
  86.5 0.1 slice.85
  86.6 1.2 select_convert_fusion
  87.8 0.1 slice.91
  87.9 0.2 slice.92
  88.2 0.7 constant_dynamic-slice_fusion
  88.9 0.7 constant_dynamic-slice_fusion.1
  89.6 1.1 convolution_dynamic-update-slice_fusion.8
  90.7 1.1 convolution_dynamic-update-slice_fusion.7
  91.8 1.1 convolution_dynamic-update-slice_fusion.6
  92.9 1.1 convolution_dynamic-update-slice_fusion.5
  94.0 1.1 convolution_dynamic-update-slice_fusion.4
  95.1 1.1 convolution_dynamic-update-slice_fusion.3
  96.2 1.1 convolution_dynamic-update-slice_fusion.2
  97.3 1.1 convolution_dynamic-update-slice_fusion.1
  98.4 1.1 convolution_dynamic-update-slice_fusion
  99.5 1.2 copy-done
  100.8 0.6 dynamic_slice.78
  102.0 0.7 iota_compare_fusion.1
  102.7 40.4 %reduce-scatter.2.cloned.1.call-done = f32[8,6912]{1,0:T(8,128)} async-done(((f32[64,6912]{1,0:T(8,128)}), f32[8,6912]{1,0:T(8,128)}) %reduce-scatter.2.cloned.1.call-update) | async-done | bytes 221200 | tf_op jit(solution)/shard_map/reduce_scatter | solution.py:108
  143.1 1.2 multiply_reduce_fusion
  144.3 1.0 divide_bitcast_fusion
  145.4 0.7 copy.6
  (44 shorter events, 0.5 us)
Async XLA Ops:
  6.5 136.6 %reduce-scatter.2.cloned.1.call-start = ((), (), s32[]{:S(2)}) async-start(), calls=%async_computation.1 | async-start | bytes 1990656 | tf_op jit(solution)/shard_map/reduce_scatter | solution.py:108
  7.3 4.8 %collective-permute-start = (bf16[128,128]{1,0:T(8,128)(2,1)S(1)}, bf16[128,128]{1,0:T(8,128)(2,1)S(1)}, u32[]{:S(2)}, u32[]{:S(2)}) collective-permute-start(bf16[128,128]{1,0:T(8,128)(2,1)S(1)} %slice.64), channel_id=1, source_target_pairs={{1,0},{2,1},{3,2},{4,3},{5,4},{6,5},{7,6},{8,7},{9,8},{10,9},{11,1... | collective-permute-start | bytes 98312 | tf_op jit(solution)/shard_map/ppermute | solution.py:26
  12.1 25.2 %collective-permute-start.1 = (bf16[128,640]{1,0:T(8,128)(2,1)S(1)}, bf16[128,640]{1,0:T(8,128)(2,1)S(1)}, u32[]{:S(2)}, u32[]{:S(2)}) collective-permute-start(bf16[128,640]{1,0:T(8,128)(2,1)S(1)} %constant_dynamic-update-slice_fusion), channel_id=1, source_target_pairs={{448,16},{480,48},{0,80},{32,112},{64,144},{96,176},{128,208},{160... | collective-permute-start | bytes 491528 | tf_op jit(solution)/shard_map/ppermute | solution.py:44
  19.7 21.5 %collective-permute-start.2 = (bf16[128,640]{1,0:T(8,128)(2,1)S(1)}, bf16[128,640]{1,0:T(8,128)(2,1)S(1)}, u32[]{:S(2)}, u32[]{:S(2)}) collective-permute-start(bf16[128,640]{1,0:T(8,128)(2,1)S(1)} %constant_dynamic-update-slice_fusion), channel_id=1, source_target_pairs={{448,0},{464,16},{480,32},{496,48},{0,64},{16,80},{32,96},{48,112}... | collective-permute-start | bytes 491528 | tf_op jit(solution)/shard_map/ppermute | solution.py:44
  23.2 20.0 %collective-permute-start.3 = (bf16[128,640]{1,0:T(8,128)(2,1)S(1)}, bf16[128,640]{1,0:T(8,128)(2,1)S(1)}, u32[]{:S(2)}, u32[]{:S(2)}) collective-permute-start(bf16[128,640]{1,0:T(8,128)(2,1)S(1)} %constant_dynamic-update-slice_fusion), channel_id=1, source_target_pairs={{464,0},{480,16},{496,32},{0,48},{16,64},{32,80},{48,96},{64,112},... | collective-permute-start | bytes 491528 | tf_op jit(solution)/shard_map/ppermute | solution.py:44
  29.7 17.9 %collective-permute-start.4 = (bf16[128,640]{1,0:T(8,128)(2,1)S(1)}, bf16[128,640]{1,0:T(8,128)(2,1)S(1)}, u32[]{:S(2)}, u32[]{:S(2)}) collective-permute-start(bf16[128,640]{1,0:T(8,128)(2,1)S(1)} %constant_dynamic-update-slice_fusion), channel_id=1, source_target_pairs={{480,0},{496,16},{0,32},{16,48},{32,64},{48,80},{64,96},{80,112},{... | collective-permute-start | bytes 491528 | tf_op jit(solution)/shard_map/ppermute | solution.py:44
  35.3 15.5 %collective-permute-start.5 = (bf16[128,640]{1,0:T(8,128)(2,1)S(1)}, bf16[128,640]{1,0:T(8,128)(2,1)S(1)}, u32[]{:S(2)}, u32[]{:S(2)}) collective-permute-start(bf16[128,640]{1,0:T(8,128)(2,1)S(1)} %constant_dynamic-update-slice_fusion), channel_id=1, source_target_pairs={{496,0},{0,16},{16,32},{32,48},{48,64},{64,80},{80,96},{96,112},{1... | collective-permute-start | bytes 491528 | tf_op jit(solution)/shard_map/ppermute | solution.py:44
  37.2 16.4 %collective-permute-start.6 = (bf16[128,640]{1,0:T(8,128)(2,1)S(1)}, bf16[128,640]{1,0:T(8,128)(2,1)S(1)}, u32[]{:S(2)}, u32[]{:S(2)}) collective-permute-start(bf16[128,640]{1,0:T(8,128)(2,1)S(1)} %constant_dynamic-update-slice_fusion), channel_id=1, source_target_pairs={{16,0},{32,16},{48,32},{64,48},{80,64},{96,80},{112,96},{128,112},... | collective-permute-start | bytes 491528 | tf_op jit(solution)/shard_map/ppermute | solution.py:44
  41.2 12.4 %collective-permute-start.7 = (bf16[128,640]{1,0:T(8,128)(2,1)S(1)}, bf16[128,640]{1,0:T(8,128)(2,1)S(1)}, u32[]{:S(2)}, u32[]{:S(2)}) collective-permute-start(bf16[128,640]{1,0:T(8,128)(2,1)S(1)} %constant_dynamic-update-slice_fusion), channel_id=1, source_target_pairs={{32,0},{48,16},{64,32},{80,48},{96,64},{112,80},{128,96},{144,112}... | collective-permute-start | bytes 491528 | tf_op jit(solution)/shard_map/ppermute | solution.py:44
  43.2 10.5 %collective-permute-start.8 = (bf16[128,640]{1,0:T(8,128)(2,1)S(1)}, bf16[128,640]{1,0:T(8,128)(2,1)S(1)}, u32[]{:S(2)}, u32[]{:S(2)}) collective-permute-start(bf16[128,640]{1,0:T(8,128)(2,1)S(1)} %constant_dynamic-update-slice_fusion), channel_id=1, source_target_pairs={{48,0},{64,16},{80,32},{96,48},{112,64},{128,80},{144,96},{160,112... | collective-permute-start | bytes 491528 | tf_op jit(solution)/shard_map/ppermute | solution.py:44
  47.7 8.4 %collective-permute-start.9 = (bf16[128,640]{1,0:T(8,128)(2,1)S(1)}, bf16[128,640]{1,0:T(8,128)(2,1)S(1)}, u32[]{:S(2)}, u32[]{:S(2)}) collective-permute-start(bf16[128,640]{1,0:T(8,128)(2,1)S(1)} %constant_dynamic-update-slice_fusion), channel_id=1, source_target_pairs={{64,0},{80,16},{96,32},{112,48},{128,64},{144,80},{160,96},{176,11... | collective-permute-start | bytes 491528 | tf_op jit(solution)/shard_map/ppermute | solution.py:44
  50.8 6.8 %collective-permute-start.10 = (bf16[128,640]{1,0:T(8,128)(2,1)S(1)}, bf16[128,640]{1,0:T(8,128)(2,1)S(1)}, u32[]{:S(2)}, u32[]{:S(2)}) collective-permute-start(bf16[128,640]{1,0:T(8,128)(2,1)S(1)} %constant_dynamic-update-slice_fusion), channel_id=1, source_target_pairs={{80,0},{112,32},{144,64},{176,96},{208,128},{240,160},{272,192},{3... | collective-permute-start | bytes 491528 | tf_op jit(solution)/shard_map/ppermute | solution.py:44
  60.0 25.5 %collective-permute-start.11 = (bf16[896,640]{1,0:T(8,128)(2,1)S(1)}, bf16[896,640]{1,0:T(8,128)(2,1)S(1)}, u32[]{:S(2)}, u32[]{:S(2)}) collective-permute-start(bf16[896,640]{1,0:T(8,128)(2,1)S(1)} %get-tuple-element.12), channel_id=1, source_target_pairs={{0,1},{1,0},{2,3},{3,2},{4,5},{5,4},{6,7},{7,6},{8,9},{9,8},{10,11... | collective-permute-start | bytes 3440648 | tf_op jit(solution)/shard_map/ppermute | solution.py:55
  98.4 2.4 %copy-start.2 = (s32[16]{0:T(128)S(1)}, s32[16]{0:T(128)}, u32[]{:S(2)}) copy-start(s32[16]{0:T(128)} %param.6) | copy-start | bytes 196
  98.4 4.3 %copy-start.1 = (s32[9]{0:T(128)S(1)}, s32[9]{0:T(128)}, u32[]{:S(2)}) copy-start(s32[9]{0:T(128)} %param.7) | copy-start | bytes 112
  99.5 1.2 copy-start
Sparse Core Ops, SparseCore 0:
  100.9 42.2 reduce-scatter.1

commit v8 on v7

--- a/solution.py
+++ b/solution.py
@@ -18,8 +18,7 @@
     half_rows, days_dev = anomalies.shape
     tz_size = lax.axis_size("tz")
     tm_size = tz_size * lax.axis_size("tc")
-    lon_size = lax.axis_size("lon")
-    blocks = lon_size // 2
+    blocks = lax.axis_size("ly") * lax.axis_size("lx") // 2
     block_width = 2 * half_rows
     total_days = days_dev * tm_size
     core = lax.axis_index("tc")
@@ -27,26 +26,19 @@
         anomalies[:, :LMAX], TIME, [(i, i - 1) for i in range(1, tm_size)]
     )
     extended = jnp.concatenate([anomalies, margin], 1)
-    lon_index = lax.axis_index("lon")
-    parity = lax.rem(lon_index, 2)
-    block_index = lax.div(lon_index, 2)
-    reach = 2 * REACH + 1
-    halves = []
-    for offset in range(-reach, reach + 1):
-        if offset == 0:
-            halves.append(extended)
-            continue
-        pairs = []
-        for target in range(lon_size):
-            low = -2 * REACH - target % 2
-            if low <= offset <= low + 2 * (2 * REACH + 1) - 1:
-                pairs.append(((target + offset) % lon_size, target))
-        halves.append(lax.ppermute(extended, "lon", pairs))
-    halves = jnp.stack(halves, 0)
+    row_size = lax.axis_size("lx")
+    lx_index = lax.axis_index("lx")
+    parity = lax.rem(lx_index, 2)
+    block_index = lax.axis_index("ly") * (row_size // 2) + lax.div(lx_index, 2)
+    row = lax.all_gather(extended, "lx")
+    rows_size = lax.axis_size("ly")
+    before = lax.ppermute(row, "ly", [(i, (i + 1) % rows_size) for i in range(rows_size)])
+    after = lax.ppermute(row, "ly", [(i, (i - 1) % rows_size) for i in range(rows_size)])
+    halves = jnp.concatenate([before, row, after], 0)
     block_ids = dslice(neighbor_ids, block_index, 1, 0)[0]
     live_count = dslice(neighbor_counts, block_index, 1, 0)[0]
     positions = lax.rem(block_ids - block_index + (REACH + blocks), blocks)
-    firsts = 2 * positions + (reach - 2 * REACH) - parity
+    firsts = 2 * (positions + lax.div(lx_index, 2) + (row_size // 2 - REACH))
     slot_blocks = []
     for slot_index in range(K_SLOTS):
         pair = dslice(halves, firsts[slot_index], 2, 0)
@@ -119,11 +111,13 @@
 
 def solution(mesh):
     lon_size, tm_size = mesh.devices.shape
-    split = Mesh(mesh.devices.reshape(lon_size, tm_size // 2, 2), ("lon", "tz", "tc"))
+    split = Mesh(
+        mesh.devices.reshape(lon_size // 4, 4, tm_size // 2, 2), ("ly", "lx", "tz", "tc")
+    )
     return jax.shard_map(
         local,
         mesh=split,
-        in_specs=(P("lon", TIME), P(), P(), P()),
-        out_specs=P(("lon",) + TIME, None),
+        in_specs=(P(("ly", "lx"), TIME), P(), P(), P()),
+        out_specs=P(("ly", "lx") + TIME, None),
         check_vma=False,
     )

time: 154 us -> 142 us (0.922)
  starting transfers between devices: 38.1 us -> 10.2 us
  blocking collectives: 22.9 us -> 37.9 us
  waiting for transfers between devices: 44.3 us -> 46.4 us
    ppermute x10 -> x2, starting transfers between devices: 34.9 us -> 7.04 us  [the longest x1 5.13 us: local(): lax.ppermute(row, 'ly', [(i, (i - 1) % rows_size) for i in range(rows_siz...]
    all_gather x0 -> x1, blocking collectives: none -> 16.3 us  [local(): row = lax.all_gather(extended, 'lx')]
    ppermute x10 -> x2, waiting for transfers between devices: 3.83 us -> 3.72 us  [the longest x1 2.54 us: local(): lax.ppermute(row, 'ly', [(i, (i + 1) % rows_size) for i in range(rows_siz...]
  transfers between devices with their start and end apart: 13 -> 5, of which waited for: 3 -> 4; matrix products, arithmetic and copies ran while one was open for 4% -> 4% of each run, Pallas kernels for 0% -> 0%
where the time goes in v8:
time: 142 us
  waiting for transfers between devices  46.4 us (33%)
  blocking collectives  37.9 us (27%)
  between operations  19.9 us (14%)
  local copies, waits for them, and re-layouts  10.5 us (7%)
  starting transfers between devices  10.2 us (7%)
  matrix products  9.83 us (7%)
  other arithmetic  7.21 us (5%)
    reduce_scatter x1, waiting for transfers between devices, local(): comoment = lax.psum_scatter(product, 'tz', scatter_dimension=0, tiled=True)  41.8 us
    all_gather x1, blocking collectives, local(): stats = lax.all_gather(jnp.stack([shard_mean, shard_square], 0), TIME)  21.6 us
    all_gather x1, blocking collectives, local(): row = lax.all_gather(extended, 'lx')  16.3 us
    dot_general x9, matrix products, local(): lax.dot_general(left, right, (((1,), (1,)), ((), ())), preferred_element_...  9.83 us
    ppermute x1, starting transfers between devices, local(): lax.ppermute(row, 'ly', [(i, (i - 1) % rows_size) for i in range(rows_siz...  5.13 us
    dynamic_slice x4, local copies, waits for them, and re-layouts, dslice(): lax.dynamic_slice_in_dim(value, start, size, axis, allow_negative_indices...  4.05 us
  transfers between devices with their start and end apart: 5, of which 4 were waited for; matrix products, arithmetic and copies ran while one was open for 4% of the time, Pallas kernels for 0%

profile of v8, /device:TPU:6, one launch (start us, length us, event | category | flops | bytes accessed | tf_op | source)
XLA Modules:
  0.0 141.9 jit_solution(3528024184017862449)
XLA Ops:
  6.5 0.0 reduce-scatter.2.cloned.1.call-start
  6.5 0.8 slice.64
  7.3 1.3 collective-permute-start
  8.6 0.9 constant_dynamic-update-slice_fusion.1
  9.5 0.9 collective-permute-done
  10.4 16.3 %all-gather = bf16[512,640]{1,0:T(8,128)(2,1)S(1)} all-gather(bf16[128,640]{1,0:T(8,128)(2,1)S(1)} %constant_dynamic-update-slice_fusion), channel_id=2, replica_groups=mesh['ly'=8,'lx'=4,'tz'=8,'tc'=2] {'lx'}, dimensions={0}, use_global_device_ids=true | all-gather | bytes 819200 | tf_op jit(solution)/shard_map/all_gather | solution.py:33
  26.7 1.9 %collective-permute-start.1 = (bf16[4,128,640]{2,1,0:T(8,128)(2,1)S(1)}, bf16[4,128,640]{2,1,0:T(8,128)(2,1)S(1)}, u32[]{:S(2)}, u32[]{:S(2)}) collective-permute-start(bf16[4,128,640]{2,1,0:T(8,128)(2,1)S(1)} %bitcast.39), channel_id=1, source_target_pairs={{0,64},{64,128},{128,192},{192,256},{256,320},{320,384},{384,448},... | collective-permute-start | bytes 1966088 | tf_op jit(solution)/shard_map/ppermute | solution.py:35
  28.6 5.1 %collective-permute-start.2 = (bf16[4,128,640]{2,1,0:T(8,128)(2,1)S(1)}, bf16[4,128,640]{2,1,0:T(8,128)(2,1)S(1)}, u32[]{:S(2)}, u32[]{:S(2)}) collective-permute-start(bf16[4,128,640]{2,1,0:T(8,128)(2,1)S(1)} %bitcast.40), channel_id=1, source_target_pairs={{0,448},{64,0},{128,64},{192,128},{256,192},{320,256},{384,320},{4... | collective-permute-start | bytes 1966088 | tf_op jit(solution)/shard_map/ppermute | solution.py:36
  33.8 1.7 %fusion.52 = (s32[1]{0:T(128)}, s32[1]{0:T(128)}, s32[1]{0:T(128)}, s32[1]{0:T(128)}, s32[1]{0:T(128)}, /*index=5*/s32[1]{0:T(128)}, s32[1]{0:T(128)}, s32[1]{0:T(128)}, s32[1]{0:T(128)}) fusion(s32[9]{0:T(128)} %param.7), kind=kLoop, calls=%fused_computation.113 | loop fusion | bytes 72 | tf_op jit(solution)/shard_map/slice | solution.py:85
  41.0 0.9 fusion.38
  41.9 0.7 fusion.53
  42.5 2.5 %collective-permute-done.1 = bf16[4,128,640]{2,1,0:T(8,128)(2,1)S(1)} collective-permute-done((bf16[4,128,640]{2,1,0:T(8,128)(2,1)S(1)}, bf16[4,128,640]{2,1,0:T(8,128)(2,1)S(1)}, u32[]{:S(2)}, u32[]{:S(2)}) %collective-permute-start.1) | collective-permute-done | bytes 655392 | tf_op jit(solution)/shard_map/ppermute | solution.py:35
  45.1 1.2 collective-permute-done.2
  46.3 0.2 pad_maximum_fusion.1
  46.5 2.0 %constant_dynamic-slice_fusion.20 = (bf16[2,128,640]{2,1,0:T(8,128)(2,1)S(1)}, bf16[2,128,640]{2,1,0:T(8,128)(2,1)S(1)}, bf16[2,128,640]{2,1,0:T(8,128)(2,1)S(1)}) fusion(bf16[12,128,640]{2,1,0:T(8,128)(2,1)S(1)} %pad_maximum_fusion.1, s32[]{:T(128)} %bitcast.2, s32[]{:T(128)} %bitcast.6, s32[]{:T(128)} %bitcast.4), kind=kLoop, calls=%fused_computation.86 | loop fusion | bytes 1966092 | tf_op jit(solution)/shard_map/dynamic_slice | solution.py:14
  48.6 0.2 pad_maximum_fusion.2
  48.7 0.2 convert_reduce_fusion
  49.0 1.9 %collective-permute-start.3 = (bf16[896,640]{1,0:T(8,128)(2,1)S(1)}, bf16[896,640]{1,0:T(8,128)(2,1)S(1)}, u32[]{:S(2)}, u32[]{:S(2)}) collective-permute-start(bf16[896,640]{1,0:T(8,128)(2,1)S(1)} %get-tuple-element.12), channel_id=1, source_target_pairs={{0,1},{1,0},{2,3},{3,2},{4,5},{5,4},{6,7},{7,6},{8,9},{9,8},{10,11... | collective-permute-start | bytes 3440648 | tf_op jit(solution)/shard_map/ppermute | solution.py:47
  50.9 0.5 fusion.1
  51.4 21.6 %all-gather.2 = f32[16,2,896]{2,1,0:T(2,128)S(1)} all-gather(f32[1,2,896]{2,1,0:T(2,128)S(1)} %maximum_bitcast_fusion), channel_id=3, replica_groups=mesh['ly'=8,'lx'=4,'tz'=8,'tc'=2] {'tz','tc'}, dimensions={0}, use_global_device_ids=true | all-gather | bytes 121856 | tf_op jit(solution)/shard_map/all_gather | solution.py:51
  73.0 0.1 slice_reduce_fusion.1
  73.2 0.0 collective-permute-done.3
  73.2 1.0 fusion.5
  74.1 0.1 slice.85
  74.2 1.2 select_convert_fusion
  75.4 0.1 slice.91
  75.6 0.2 slice.92
  75.8 0.7 constant_dynamic-slice_fusion
  76.5 0.7 constant_dynamic-slice_fusion.1
  77.3 1.1 convolution_dynamic-update-slice_fusion.8
  78.4 1.1 convolution_dynamic-update-slice_fusion.7
  79.5 1.1 convolution_dynamic-update-slice_fusion.6
  80.5 1.1 convolution_dynamic-update-slice_fusion.5
  81.7 1.1 convolution_dynamic-update-slice_fusion.4
  82.7 1.1 convolution_dynamic-update-slice_fusion.3
  83.8 1.1 convolution_dynamic-update-slice_fusion.2
  84.9 1.1 convolution_dynamic-update-slice_fusion.1
  86.0 0.0 copy-start.1
  86.0 1.1 convolution_dynamic-update-slice_fusion
  87.1 1.2 copy-done
  88.4 0.0 reduce-scatter.2.cloned.1.call-update
  88.4 0.0 copy-done.2
  88.4 0.6 dynamic_slice.78
  89.6 0.7 iota_compare_fusion.1
  90.3 41.8 %reduce-scatter.2.cloned.1.call-done = f32[8,6912]{1,0:T(8,128)} async-done(((f32[64,6912]{1,0:T(8,128)}), f32[8,6912]{1,0:T(8,128)}) %reduce-scatter.2.cloned.1.call-update) | async-done | bytes 221200 | tf_op jit(solution)/shard_map/reduce_scatter | solution.py:100
  132.1 1.2 multiply_reduce_fusion
  133.3 1.0 divide_bitcast_fusion
  134.4 0.7 copy.6
  (19 shorter events, 0.2 us)
Async XLA Ops:
  6.5 125.6 %reduce-scatter.2.cloned.1.call-start = ((), (), s32[]{:S(2)}) async-start(), calls=%async_computation.1 | async-start | bytes 1990656 | tf_op jit(solution)/shard_map/reduce_scatter | solution.py:100
  7.3 3.1 %collective-permute-start = (bf16[128,128]{1,0:T(8,128)(2,1)S(1)}, bf16[128,128]{1,0:T(8,128)(2,1)S(1)}, u32[]{:S(2)}, u32[]{:S(2)}) collective-permute-start(bf16[128,128]{1,0:T(8,128)(2,1)S(1)} %slice.64), channel_id=1, source_target_pairs={{1,0},{2,1},{3,2},{4,3},{5,4},{6,5},{7,6},{8,7},{9,8},{10,9},{11,1... | collective-permute-start | bytes 98312 | tf_op jit(solution)/shard_map/ppermute | solution.py:25
  26.7 18.4 %collective-permute-start.1 = (bf16[4,128,640]{2,1,0:T(8,128)(2,1)S(1)}, bf16[4,128,640]{2,1,0:T(8,128)(2,1)S(1)}, u32[]{:S(2)}, u32[]{:S(2)}) collective-permute-start(bf16[4,128,640]{2,1,0:T(8,128)(2,1)S(1)} %bitcast.39), channel_id=1, source_target_pairs={{0,64},{64,128},{128,192},{192,256},{256,320},{320,384},{384,448},... | collective-permute-start | bytes 1966088 | tf_op jit(solution)/shard_map/ppermute | solution.py:35
  28.6 17.6 %collective-permute-start.2 = (bf16[4,128,640]{2,1,0:T(8,128)(2,1)S(1)}, bf16[4,128,640]{2,1,0:T(8,128)(2,1)S(1)}, u32[]{:S(2)}, u32[]{:S(2)}) collective-permute-start(bf16[4,128,640]{2,1,0:T(8,128)(2,1)S(1)} %bitcast.40), channel_id=1, source_target_pairs={{0,448},{64,0},{128,64},{192,128},{256,192},{320,256},{384,320},{4... | collective-permute-start | bytes 1966088 | tf_op jit(solution)/shard_map/ppermute | solution.py:36
  49.0 24.2 %collective-permute-start.3 = (bf16[896,640]{1,0:T(8,128)(2,1)S(1)}, bf16[896,640]{1,0:T(8,128)(2,1)S(1)}, u32[]{:S(2)}, u32[]{:S(2)}) collective-permute-start(bf16[896,640]{1,0:T(8,128)(2,1)S(1)} %get-tuple-element.12), channel_id=1, source_target_pairs={{0,1},{1,0},{2,3},{3,2},{4,5},{5,4},{6,7},{7,6},{8,9},{9,8},{10,11... | collective-permute-start | bytes 3440648 | tf_op jit(solution)/shard_map/ppermute | solution.py:47
  86.0 2.4 %copy-start.2 = (s32[16]{0:T(128)S(1)}, s32[16]{0:T(128)}, u32[]{:S(2)}) copy-start(s32[16]{0:T(128)} %param.6) | copy-start | bytes 196
  86.0 4.3 %copy-start.1 = (s32[9]{0:T(128)S(1)}, s32[9]{0:T(128)}, u32[]{:S(2)}) copy-start(s32[9]{0:T(128)} %param.7) | copy-start | bytes 112
  87.1 1.2 copy-start
Sparse Core Ops, SparseCore 0:
  88.5 43.5 reduce-scatter.1

commit v9 on v8

--- a/solution.py
+++ b/solution.py
@@ -48,12 +48,18 @@
     values = raw[:, :days_dev].astype(jnp.float32)
     shard_mean = jnp.mean(values, axis=1)
     shard_square = jnp.sum(jnp.square(values - shard_mean[:, None]), axis=1)
-    stats = lax.all_gather(jnp.stack([shard_mean, shard_square], 0), TIME)
-    means, squares = stats[:, 0], stats[:, 1]
-    point_mean = jnp.mean(means, axis=0)
-    point_m2 = jnp.sum(squares, axis=0) + days_dev * jnp.sum(
-        jnp.square(means - point_mean[None, :]), axis=0
-    )
+    point_mean, point_m2 = shard_mean, shard_square
+    count = days_dev
+    steps = [("tc", 1)] + [("tz", 1 << bit) for bit in range(tz_size.bit_length() - 1)]
+    for axis, stride in steps:
+        size = lax.axis_size(axis)
+        pairs = [(i, i ^ stride) for i in range(size)]
+        theirs = lax.ppermute(jnp.stack([point_mean, point_m2], 0), axis, pairs)
+        their_mean, their_m2 = theirs[0], theirs[1]
+        delta = their_mean - point_mean
+        point_mean = (point_mean + their_mean) * 0.5
+        point_m2 = (point_m2 + their_m2) + delta * delta * (count * 0.5)
+        count = 2 * count
     spread = jnp.sqrt(point_m2 / total_days + 1e-06)
 
     pair = jnp.stack([raw, other], 0)

time: 142 us -> 150 us (1.056)
  blocking collectives: 37.9 us -> 16.3 us
  starting transfers between devices: 10.2 us -> 31.7 us
  waiting for transfers between devices: 46.4 us -> 54.5 us
    all_gather x1 -> x0, blocking collectives: 21.6 us -> none  [local(): stats = lax.all_gather(jnp.stack([shard_mean, shard_square], 0), TIME)]
    ppermute x0 -> x4, starting transfers between devices: none -> 21.5 us  [local(): theirs = lax.ppermute(jnp.stack([point_mean, point_m2], 0), axis, pairs)]
    ppermute x1, waiting for transfers between devices: 2.54 us -> 9.75 us  [local(): lax.ppermute(row, 'ly', [(i, (i + 1) % rows_size) for i in range(rows_siz...]
    ppermute x0 -> x4, waiting for transfers between devices: none -> 2.04 us  [local(): theirs = lax.ppermute(jnp.stack([point_mean, point_m2], 0), axis, pairs)]
  transfers between devices with their start and end apart: 5 -> 9, of which waited for: 4 -> 6; matrix products, arithmetic and copies ran while one was open for 4% -> 3% of each run, Pallas kernels for 0% -> 0%
where the time goes in v9:
time: 150 us; the launch traced here: 149 us
  waiting for transfers between devices  54.5 us (36%)
  starting transfers between devices  31.7 us (21%)
  between operations  20 us (13%)
  blocking collectives  16.3 us (11%)
  matrix products  9.84 us (7%)
  local copies, waits for them, and re-layouts  9.47 us (6%)
  other arithmetic  7.19 us (5%)
    reduce_scatter x1, waiting for transfers between devices, local(): comoment = lax.psum_scatter(product, 'tz', scatter_dimension=0, tiled=True)  40.6 us
    ppermute x4, starting transfers between devices, local(): theirs = lax.ppermute(jnp.stack([point_mean, point_m2], 0), axis, pairs)  21.5 us
    all_gather x1, blocking collectives, local(): row = lax.all_gather(extended, 'lx')  16.3 us
    dot_general x9, matrix products, local(): lax.dot_general(left, right, (((1,), (1,)), ((), ())), preferred_element_...  9.84 us
    ppermute x1, waiting for transfers between devices, local(): lax.ppermute(row, 'ly', [(i, (i + 1) % rows_size) for i in range(rows_siz...  9.75 us
    ppermute x1, starting transfers between devices, local(): lax.ppermute(row, 'ly', [(i, (i - 1) % rows_size) for i in range(rows_siz...  5.13 us
    dynamic_slice x4, local copies, waits for them, and re-layouts, dslice(): lax.dynamic_slice_in_dim(value, start, size, axis, allow_negative_indices...  3.99 us
  transfers between devices with their start and end apart: 9, of which 6 were waited for; matrix products, arithmetic and copies ran while one was open for 3% of the time, Pallas kernels for 0%

profile of v9, /device:TPU:6, one launch (start us, length us, event | category | flops | bytes accessed | tf_op | source)
XLA Modules:
  0.0 149.0 jit_solution(1008639119805891219)
XLA Ops:
  6.5 0.8 slice.82
  7.3 1.3 collective-permute-start
  8.6 0.9 constant_dynamic-update-slice_fusion.1
  9.5 0.9 collective-permute-done
  10.4 16.3 %all-gather = bf16[512,640]{1,0:T(8,128)(2,1)S(1)} all-gather(bf16[128,640]{1,0:T(8,128)(2,1)S(1)} %constant_dynamic-update-slice_fusion), channel_id=2, replica_groups=mesh['ly'=8,'lx'=4,'tz'=8,'tc'=2] {'lx'}, dimensions={0}, use_global_device_ids=true | all-gather | bytes 819200 | tf_op jit(solution)/shard_map/all_gather | solution.py:33
  26.7 1.9 %collective-permute-start.1 = (bf16[4,128,640]{2,1,0:T(8,128)(2,1)S(1)}, bf16[4,128,640]{2,1,0:T(8,128)(2,1)S(1)}, u32[]{:S(2)}, u32[]{:S(2)}) collective-permute-start(bf16[4,128,640]{2,1,0:T(8,128)(2,1)S(1)} %bitcast.31), channel_id=1, source_target_pairs={{0,64},{64,128},{128,192},{192,256},{256,320},{320,384},{384,448},... | collective-permute-start | bytes 1966088 | tf_op jit(solution)/shard_map/ppermute | solution.py:35
  28.6 5.1 %collective-permute-start.2 = (bf16[4,128,640]{2,1,0:T(8,128)(2,1)S(1)}, bf16[4,128,640]{2,1,0:T(8,128)(2,1)S(1)}, u32[]{:S(2)}, u32[]{:S(2)}) collective-permute-start(bf16[4,128,640]{2,1,0:T(8,128)(2,1)S(1)} %bitcast.32), channel_id=1, source_target_pairs={{0,448},{64,0},{128,64},{192,128},{256,192},{320,256},{384,320},{4... | collective-permute-start | bytes 1966088 | tf_op jit(solution)/shard_map/ppermute | solution.py:36
  33.8 0.9 fusion.36
  34.7 0.7 fusion.51
  35.3 9.7 %collective-permute-done.1 = bf16[4,128,640]{2,1,0:T(8,128)(2,1)S(1)} collective-permute-done((bf16[4,128,640]{2,1,0:T(8,128)(2,1)S(1)}, bf16[4,128,640]{2,1,0:T(8,128)(2,1)S(1)}, u32[]{:S(2)}, u32[]{:S(2)}) %collective-permute-start.1) | collective-permute-done | bytes 655392 | tf_op jit(solution)/shard_map/ppermute | solution.py:35
  45.1 1.2 collective-permute-done.2
  46.3 0.2 pad_maximum_fusion.1
  46.5 2.0 %constant_dynamic-slice_fusion.20 = (bf16[2,128,640]{2,1,0:T(8,128)(2,1)S(1)}, bf16[2,128,640]{2,1,0:T(8,128)(2,1)S(1)}, bf16[2,128,640]{2,1,0:T(8,128)(2,1)S(1)}) fusion(bf16[12,128,640]{2,1,0:T(8,128)(2,1)S(1)} %pad_maximum_fusion.1, s32[]{:T(128)} %bitcast.2, s32[]{:T(128)} %bitcast.6, s32[]{:T(128)} %bitcast.4), kind=kLoop, calls=%fused_computation.85 | loop fusion | bytes 1966092 | tf_op jit(solution)/shard_map/dynamic_slice | solution.py:14
  48.5 0.2 pad_maximum_fusion.2
  48.7 0.2 convert_reduce_fusion
  48.9 0.5 fusion.1
  49.4 1.9 %collective-permute-start.4 = (f32[2,896]{1,0:T(2,128)S(1)}, f32[2,896]{1,0:T(2,128)S(1)}, u32[]{:S(2)}, u32[]{:S(2)}) collective-permute-start(f32[2,896]{1,0:T(2,128)S(1)} %pad_maximum_fusion.4), channel_id=1, source_target_pairs={{0,1},{1,0},{2,3},{3,2},{4,5},{5,4},{6,7},{7,6},{8,9},{9,8},{10,11... | collective-permute-start | bytes 21512 | tf_op jit(solution)/shard_map/ppermute | solution.py:57
  51.4 1.1 collective-permute-done.4
  52.5 4.3 %collective-permute-start.5 = (f32[2,896]{1,0:T(2,128)S(1)}, f32[2,896]{1,0:T(2,128)S(1)}, u32[]{:S(2)}, u32[]{:S(2)}) collective-permute-start(f32[2,896]{1,0:T(2,128)S(1)} %pad_maximum_fusion.5), channel_id=1, source_target_pairs={{0,2},{2,0},{4,6},{6,4},{8,10},{10,8},{12,14},{14,12},{1,3},{3,1},... | collective-permute-start | bytes 21512 | tf_op jit(solution)/shard_map/ppermute | solution.py:57
  56.9 1.9 %collective-permute-start.3 = (bf16[896,640]{1,0:T(8,128)(2,1)S(1)}, bf16[896,640]{1,0:T(8,128)(2,1)S(1)}, u32[]{:S(2)}, u32[]{:S(2)}) collective-permute-start(bf16[896,640]{1,0:T(8,128)(2,1)S(1)} %get-tuple-element.18), channel_id=1, source_target_pairs={{0,1},{1,0},{2,3},{3,2},{4,5},{5,4},{6,7},{7,6},{8,9},{9,8},{10,11... | collective-permute-start | bytes 3440648 | tf_op jit(solution)/shard_map/ppermute | solution.py:47
  58.9 6.2 %collective-permute-start.6 = (f32[2,896]{1,0:T(2,128)S(1)}, f32[2,896]{1,0:T(2,128)S(1)}, u32[]{:S(2)}, u32[]{:S(2)}) collective-permute-start(f32[2,896]{1,0:T(2,128)S(1)} %pad_maximum_fusion.6), channel_id=1, source_target_pairs={{0,4},{2,6},{4,0},{6,2},{8,12},{10,14},{12,8},{14,10},{1,5},{3,7},... | collective-permute-start | bytes 21512 | tf_op jit(solution)/shard_map/ppermute | solution.py:57
  65.0 0.7 fusion.50
  65.7 0.9 collective-permute-done.6
  66.7 9.1 %collective-permute-start.7 = (f32[2,896]{1,0:T(2,128)S(1)}, f32[2,896]{1,0:T(2,128)S(1)}, u32[]{:S(2)}, u32[]{:S(2)}) collective-permute-start(f32[2,896]{1,0:T(2,128)S(1)} %pad_maximum_fusion.7), channel_id=1, source_target_pairs={{0,8},{2,10},{4,12},{6,14},{8,0},{10,2},{12,4},{14,6},{1,9},{3,11}... | collective-permute-start | bytes 21512 | tf_op jit(solution)/shard_map/ppermute | solution.py:57
  81.5 1.0 fusion.5
  82.5 0.1 slice.109
  82.6 1.2 select_convert_fusion
  83.8 0.1 slice.121
  83.9 0.2 slice.122
  84.1 0.7 constant_dynamic-slice_fusion
  84.9 0.7 constant_dynamic-slice_fusion.1
  85.6 1.1 convolution_dynamic-update-slice_fusion.8
  86.7 1.1 convolution_dynamic-update-slice_fusion.7
  87.8 1.1 convolution_dynamic-update-slice_fusion.6
  88.9 1.1 convolution_dynamic-update-slice_fusion.5
  90.0 1.1 convolution_dynamic-update-slice_fusion.4
  91.1 1.1 convolution_dynamic-update-slice_fusion.3
  92.2 1.1 convolution_dynamic-update-slice_fusion.2
  93.3 1.1 convolution_dynamic-update-slice_fusion.1
  94.4 1.1 convolution_dynamic-update-slice_fusion
  95.5 1.2 copy-done
  96.7 0.0 reduce-scatter.2.cloned.1.call-update
  96.7 0.6 dynamic_slice.78
  98.0 0.7 iota_compare_fusion.1
  98.6 40.6 %reduce-scatter.2.cloned.1.call-done = f32[8,6912]{1,0:T(8,128)} async-done(((f32[64,6912]{1,0:T(8,128)}), f32[8,6912]{1,0:T(8,128)}) %reduce-scatter.2.cloned.1.call-update) | async-done | bytes 221200 | tf_op jit(solution)/shard_map/reduce_scatter | solution.py:106
  139.2 1.2 multiply_reduce_fusion
  140.4 1.0 divide_bitcast_fusion
  141.5 0.7 copy.5
  (30 shorter events, 0.3 us)
Async XLA Ops:
  6.5 132.7 %reduce-scatter.2.cloned.1.call-start = ((), (), s32[]{:S(2)}) async-start(), calls=%async_computation.1 | async-start | bytes 1990656 | tf_op jit(solution)/shard_map/reduce_scatter | solution.py:106
  7.3 3.1 %collective-permute-start = (bf16[128,128]{1,0:T(8,128)(2,1)S(1)}, bf16[128,128]{1,0:T(8,128)(2,1)S(1)}, u32[]{:S(2)}, u32[]{:S(2)}) collective-permute-start(bf16[128,128]{1,0:T(8,128)(2,1)S(1)} %slice.82), channel_id=1, source_target_pairs={{1,0},{2,1},{3,2},{4,3},{5,4},{6,5},{7,6},{8,7},{9,8},{10,9},{11,1... | collective-permute-start | bytes 98312 | tf_op jit(solution)/shard_map/ppermute | solution.py:25
  26.7 18.4 %collective-permute-start.1 = (bf16[4,128,640]{2,1,0:T(8,128)(2,1)S(1)}, bf16[4,128,640]{2,1,0:T(8,128)(2,1)S(1)}, u32[]{:S(2)}, u32[]{:S(2)}) collective-permute-start(bf16[4,128,640]{2,1,0:T(8,128)(2,1)S(1)} %bitcast.31), channel_id=1, source_target_pairs={{0,64},{64,128},{128,192},{192,256},{256,320},{320,384},{384,448},... | collective-permute-start | bytes 1966088 | tf_op jit(solution)/shard_map/ppermute | solution.py:35
  28.6 17.6 %collective-permute-start.2 = (bf16[4,128,640]{2,1,0:T(8,128)(2,1)S(1)}, bf16[4,128,640]{2,1,0:T(8,128)(2,1)S(1)}, u32[]{:S(2)}, u32[]{:S(2)}) collective-permute-start(bf16[4,128,640]{2,1,0:T(8,128)(2,1)S(1)} %bitcast.32), channel_id=1, source_target_pairs={{0,448},{64,0},{128,64},{192,128},{256,192},{320,256},{384,320},{4... | collective-permute-start | bytes 1966088 | tf_op jit(solution)/shard_map/ppermute | solution.py:36
  48.5 16.5 %copy-start.1 = (s32[9]{0:T(128)S(1)}, s32[9]{0:T(128)}, u32[]{:S(2)}) copy-start(s32[9]{0:T(128)} %param.7) | copy-start | bytes 112
  49.4 3.1 %collective-permute-start.4 = (f32[2,896]{1,0:T(2,128)S(1)}, f32[2,896]{1,0:T(2,128)S(1)}, u32[]{:S(2)}, u32[]{:S(2)}) collective-permute-start(f32[2,896]{1,0:T(2,128)S(1)} %pad_maximum_fusion.4), channel_id=1, source_target_pairs={{0,1},{1,0},{2,3},{3,2},{4,5},{5,4},{6,7},{7,6},{8,9},{9,8},{10,11... | collective-permute-start | bytes 21512 | tf_op jit(solution)/shard_map/ppermute | solution.py:57
  52.5 6.3 %collective-permute-start.5 = (f32[2,896]{1,0:T(2,128)S(1)}, f32[2,896]{1,0:T(2,128)S(1)}, u32[]{:S(2)}, u32[]{:S(2)}) collective-permute-start(f32[2,896]{1,0:T(2,128)S(1)} %pad_maximum_fusion.5), channel_id=1, source_target_pairs={{0,2},{2,0},{4,6},{6,4},{8,10},{10,8},{12,14},{14,12},{1,3},{3,1},... | collective-permute-start | bytes 21512 | tf_op jit(solution)/shard_map/ppermute | solution.py:57
  56.9 24.6 %collective-permute-start.3 = (bf16[896,640]{1,0:T(8,128)(2,1)S(1)}, bf16[896,640]{1,0:T(8,128)(2,1)S(1)}, u32[]{:S(2)}, u32[]{:S(2)}) collective-permute-start(bf16[896,640]{1,0:T(8,128)(2,1)S(1)} %get-tuple-element.18), channel_id=1, source_target_pairs={{0,1},{1,0},{2,3},{3,2},{4,5},{5,4},{6,7},{7,6},{8,9},{9,8},{10,11... | collective-permute-start | bytes 3440648 | tf_op jit(solution)/shard_map/ppermute | solution.py:47
  58.9 7.8 %collective-permute-start.6 = (f32[2,896]{1,0:T(2,128)S(1)}, f32[2,896]{1,0:T(2,128)S(1)}, u32[]{:S(2)}, u32[]{:S(2)}) collective-permute-start(f32[2,896]{1,0:T(2,128)S(1)} %pad_maximum_fusion.6), channel_id=1, source_target_pairs={{0,4},{2,6},{4,0},{6,2},{8,12},{10,14},{12,8},{14,10},{1,5},{3,7},... | collective-permute-start | bytes 21512 | tf_op jit(solution)/shard_map/ppermute | solution.py:57
  66.7 14.8 %collective-permute-start.7 = (f32[2,896]{1,0:T(2,128)S(1)}, f32[2,896]{1,0:T(2,128)S(1)}, u32[]{:S(2)}, u32[]{:S(2)}) collective-permute-start(f32[2,896]{1,0:T(2,128)S(1)} %pad_maximum_fusion.7), channel_id=1, source_target_pairs={{0,8},{2,10},{4,12},{6,14},{8,0},{10,2},{12,4},{14,6},{1,9},{3,11}... | collective-permute-start | bytes 21512 | tf_op jit(solution)/shard_map/ppermute | solution.py:57
  94.4 2.3 %copy-start.2 = (s32[16]{0:T(128)S(1)}, s32[16]{0:T(128)}, u32[]{:S(2)}) copy-start(s32[16]{0:T(128)} %param.6) | copy-start | bytes 196
  95.5 1.2 copy-start
Sparse Core Ops, SparseCore 0:
  96.8 42.3 reduce-scatter.1

commit v10 on v8

--- a/solution.py
+++ b/solution.py
@@ -95,9 +95,13 @@
                 left, right, (((1,), (1,)), ((), ())), preferred_element_type=jnp.float32
             )
         )
-    product = jnp.concatenate(pieces, 1)
-
-    comoment = lax.psum_scatter(product, "tz", scatter_dimension=0, tiled=True)
+    parts = [
+        lax.psum_scatter(
+            jnp.concatenate(pieces[first:first + 3], 1), "tz", scatter_dimension=0, tiled=True
+        )
+        for first in range(0, NLAG, 3)
+    ]
+    comoment = jnp.concatenate(parts, 1)
     comoment = comoment.reshape(out_rows, NLAG, K_SLOTS, block_width).transpose(0, 2, 1, 3)
     denominator = 2.0 * (total_days - lag_set).astype(jnp.float32)
     is_live = jnp.arange(K_SLOTS, dtype=jnp.int32) < live_count

time: 142 us -> 216 us (1.52)
  waiting for transfers between devices: 46.4 us -> 116 us
    reduce_scatter x1 -> x3, waiting for transfers between devices: 41.8 us -> 111 us  [local(): lax.psum_scatter(jnp.concatenate(pieces[first:first + 3], 1), 'tz', scatt...]
    concatenate x0 -> x4, other arithmetic: none -> 3.58 us  [the longest x3 2.61 us: local(): jnp.concatenate(pieces[first:first + 3], 1)]
  transfers between devices with their start and end apart: 5 -> 7, of which waited for: 4 -> 6; matrix products, arithmetic and copies ran while one was open for 4% -> 8% of each run, Pallas kernels for 0% -> 0%
where the time goes in v10:
time: 216 us; the launch traced here: 215 us
  waiting for transfers between devices  116 us (54%)
  blocking collectives  37.7 us (17%)
  between operations  19.7 us (9%)
  matrix products  11.9 us (6%)
  local copies, waits for them, and re-layouts  10.9 us (5%)
  starting transfers between devices  10.3 us (5%)
  other arithmetic  8.93 us (4%)
    reduce_scatter x3, waiting for transfers between devices, local(): lax.psum_scatter(jnp.concatenate(pieces[first:first + 3], 1), 'tz', scatt...  111 us
    all_gather x1, blocking collectives, local(): stats = lax.all_gather(jnp.stack([shard_mean, shard_square], 0), TIME)  21.4 us
    all_gather x1, blocking collectives, local(): row = lax.all_gather(extended, 'lx')  16.3 us
    dot_general x9, matrix products, local(): lax.dot_general(left, right, (((1,), (1,)), ((), ())), preferred_element_...  11.9 us
    dynamic_slice x4, local copies, waits for them, and re-layouts, dslice(): lax.dynamic_slice_in_dim(value, start, size, axis, allow_negative_indices...  5.67 us
    ppermute x1, starting transfers between devices, local(): lax.ppermute(row, 'ly', [(i, (i - 1) % rows_size) for i in range(rows_siz...  5.13 us
  transfers between devices with their start and end apart: 7, of which 6 were waited for; matrix products, arithmetic and copies ran while one was open for 8% of the time, Pallas kernels for 0%

profile of v10, /device:TPU:6, one launch (start us, length us, event | category | flops | bytes accessed | tf_op | source)
XLA Modules:
  0.0 215.4 jit_solution(7395389257152989362)
XLA Ops:
  6.5 0.8 slice.64
  7.3 1.3 collective-permute-start
  8.6 0.9 constant_dynamic-update-slice_fusion.1
  9.5 0.9 collective-permute-done
  10.4 16.3 %all-gather = bf16[512,640]{1,0:T(8,128)(2,1)S(1)} all-gather(bf16[128,640]{1,0:T(8,128)(2,1)S(1)} %constant_dynamic-update-slice_fusion), channel_id=2, replica_groups=mesh['ly'=8,'lx'=4,'tz'=8,'tc'=2] {'lx'}, dimensions={0}, use_global_device_ids=true | all-gather | bytes 819200 | tf_op jit(solution)/shard_map/all_gather | solution.py:33
  26.7 1.9 collective-permute-start.1
  28.6 5.1 %collective-permute-start.2 = (bf16[4,128,640]{2,1,0:T(8,128)(2,1)S(1)}, bf16[4,128,640]{2,1,0:T(8,128)(2,1)S(1)}, u32[]{:S(2)}, u32[]{:S(2)}) collective-permute-start(bf16[4,128,640]{2,1,0:T(8,128)(2,1)S(1)} %bitcast.40), channel_id=1, source_target_pairs={{0,448},{64,0},{128,64},{192,128},{256,192},{320,256},{384,320},{4... | collective-permute-start | bytes 1966088 | tf_op jit(solution)/shard_map/ppermute | solution.py:36
  33.8 1.7 fusion.61
  41.0 0.9 fusion.47
  41.9 0.6 fusion.62
  42.5 2.6 %collective-permute-done.1 = bf16[4,128,640]{2,1,0:T(8,128)(2,1)S(1)} collective-permute-done((bf16[4,128,640]{2,1,0:T(8,128)(2,1)S(1)}, bf16[4,128,640]{2,1,0:T(8,128)(2,1)S(1)}, u32[]{:S(2)}, u32[]{:S(2)}) %collective-permute-start.1) | collective-permute-done | bytes 655392 | tf_op jit(solution)/shard_map/ppermute | solution.py:35
  45.1 1.2 collective-permute-done.2
  46.3 0.2 pad_maximum_fusion.1
  46.5 1.9 constant_dynamic-slice_fusion.20
  48.4 0.2 pad_maximum_fusion.2
  48.6 0.2 convert_reduce_fusion
  48.8 1.9 collective-permute-start.3
  50.8 0.5 fusion.1
  51.3 21.4 %all-gather.2 = f32[16,2,896]{2,1,0:T(2,128)S(1)} all-gather(f32[1,2,896]{2,1,0:T(2,128)S(1)} %maximum_bitcast_fusion), channel_id=3, replica_groups=mesh['ly'=8,'lx'=4,'tz'=8,'tc'=2] {'tz','tc'}, dimensions={0}, use_global_device_ids=true | all-gather | bytes 121856 | tf_op jit(solution)/shard_map/all_gather | solution.py:51
  72.7 0.1 slice_reduce_fusion.1
  72.9 1.0 fusion.5
  73.8 0.1 slice.85
  73.9 1.2 select_convert_fusion
  75.1 0.1 slice.91
  75.3 0.2 slice.92
  75.5 1.6 constant_dynamic-slice_fusion.16
  77.1 1.6 constant_dynamic-slice_fusion.17
  78.7 1.1 fusion.6
  79.8 1.1 fusion.10
  80.9 1.1 fusion.14
  82.0 0.9 pad_maximum_fusion.3
  82.9 2.1 fusion.18
  85.1 1.1 fusion.22
  86.2 1.1 fusion.26
  87.3 0.9 pad_maximum_fusion.4
  88.3 2.1 fusion.30
  90.4 1.1 fusion.34
  91.5 1.1 fusion.38
  92.6 0.9 pad_maximum_fusion.5
  93.5 0.6 dynamic_slice.78
  94.8 0.7 iota_compare_fusion.1
  95.5 27.6 %reduce-scatter.4.cloned.1.call-done = f32[8,2304]{1,0:T(8,128)} async-done(((f32[64,2304]{1,0:T(8,128)}), f32[8,2304]{1,0:T(8,128)}) %reduce-scatter.4.cloned.1.call-update) | async-done | bytes 73744 | tf_op jit(solution)/shard_map/reduce_scatter | solution.py:99
  123.0 41.9 %reduce-scatter.6.cloned.1.call-done = f32[8,2304]{1,0:T(8,128)} async-done(((f32[64,2304]{1,0:T(8,128)}), f32[8,2304]{1,0:T(8,128)}) %reduce-scatter.6.cloned.1.call-update) | async-done | bytes 73744 | tf_op jit(solution)/shard_map/reduce_scatter | solution.py:99
  164.9 41.9 %reduce-scatter.8.cloned.1.call-done = f32[8,2304]{1,0:T(8,128)} async-done(((f32[64,2304]{1,0:T(8,128)}), f32[8,2304]{1,0:T(8,128)}) %reduce-scatter.8.cloned.1.call-update) | async-done | bytes 73744 | tf_op jit(solution)/shard_map/reduce_scatter | solution.py:99
  206.8 1.0 pad_maximum_fusion.6
  207.8 0.2 multiply_reduce_fusion
  208.1 0.1 divide_bitcast_fusion
  208.2 0.7 copy.6
  (41 shorter events, 0.4 us)
Async XLA Ops:
  6.5 116.5 %reduce-scatter.4.cloned.1.call-start = ((), (), s32[]{:S(2)}) async-start(), calls=%async_computation.3 | async-start | bytes 663552 | tf_op jit(solution)/shard_map/reduce_scatter | solution.py:99
  7.3 3.1 %collective-permute-start = (bf16[128,128]{1,0:T(8,128)(2,1)S(1)}, bf16[128,128]{1,0:T(8,128)(2,1)S(1)}, u32[]{:S(2)}, u32[]{:S(2)}) collective-permute-start(bf16[128,128]{1,0:T(8,128)(2,1)S(1)} %slice.64), channel_id=1, source_target_pairs={{1,0},{2,1},{3,2},{4,3},{5,4},{6,5},{7,6},{8,7},{9,8},{10,9},{11,1... | collective-permute-start | bytes 98312 | tf_op jit(solution)/shard_map/ppermute | solution.py:25
  26.7 18.4 %collective-permute-start.1 = (bf16[4,128,640]{2,1,0:T(8,128)(2,1)S(1)}, bf16[4,128,640]{2,1,0:T(8,128)(2,1)S(1)}, u32[]{:S(2)}, u32[]{:S(2)}) collective-permute-start(bf16[4,128,640]{2,1,0:T(8,128)(2,1)S(1)} %bitcast.39), channel_id=1, source_target_pairs={{0,64},{64,128},{128,192},{192,256},{256,320},{320,384},{384,448},... | collective-permute-start | bytes 1966088 | tf_op jit(solution)/shard_map/ppermute | solution.py:35
  28.6 17.6 %collective-permute-start.2 = (bf16[4,128,640]{2,1,0:T(8,128)(2,1)S(1)}, bf16[4,128,640]{2,1,0:T(8,128)(2,1)S(1)}, u32[]{:S(2)}, u32[]{:S(2)}) collective-permute-start(bf16[4,128,640]{2,1,0:T(8,128)(2,1)S(1)} %bitcast.40), channel_id=1, source_target_pairs={{0,448},{64,0},{128,64},{192,128},{256,192},{320,256},{384,320},{4... | collective-permute-start | bytes 1966088 | tf_op jit(solution)/shard_map/ppermute | solution.py:36
  48.8 24.0 %collective-permute-start.3 = (bf16[896,640]{1,0:T(8,128)(2,1)S(1)}, bf16[896,640]{1,0:T(8,128)(2,1)S(1)}, u32[]{:S(2)}, u32[]{:S(2)}) collective-permute-start(bf16[896,640]{1,0:T(8,128)(2,1)S(1)} %get-tuple-element.12), channel_id=1, source_target_pairs={{0,1},{1,0},{2,3},{3,2},{4,5},{5,4},{6,7},{7,6},{8,9},{9,8},{10,11... | collective-permute-start | bytes 3440648 | tf_op jit(solution)/shard_map/ppermute | solution.py:47
  82.9 82.1 %reduce-scatter.6.cloned.1.call-start = ((), (), s32[]{:S(2)}) async-start(), calls=%async_computation.4 | async-start | bytes 663552 | tf_op jit(solution)/shard_map/reduce_scatter | solution.py:99
  82.9 2.1 copy-start.2
  82.9 2.1 copy-start.6
  85.1 1.1 copy-start.1
  85.1 1.1 copy-start.5
  88.2 118.6 %reduce-scatter.8.cloned.1.call-start = ((), (), s32[]{:S(2)}) async-start(), calls=%async_computation.5 | async-start | bytes 663552 | tf_op jit(solution)/shard_map/reduce_scatter | solution.py:99
  88.2 2.1 copy-start
  88.2 2.1 copy-start.4
  90.4 1.1 copy-start.3
  91.5 2.0 copy-start.8
  91.5 3.9 %copy-start.7 = (s32[9]{0:T(128)S(1)}, s32[9]{0:T(128)}, u32[]{:S(2)}) copy-start(s32[9]{0:T(128)} %param.7) | copy-start | bytes 112
Sparse Core Ops, SparseCore 0:
  83.0 39.9 reduce-scatter.3
  125.8 39.0 reduce-scatter.5
  167.8 39.0 reduce-scatter.7

commit v11 on v8

--- a/solution.py
+++ b/solution.py
@@ -97,7 +97,8 @@
         )
     product = jnp.concatenate(pieces, 1)
 
-    comoment = lax.psum_scatter(product, "tz", scatter_dimension=0, tiled=True)
+    received = lax.all_to_all(product, "tz", 0, 0, tiled=True)
+    comoment = jnp.sum(received.reshape(tz_size, out_rows, -1), axis=0)
     comoment = comoment.reshape(out_rows, NLAG, K_SLOTS, block_width).transpose(0, 2, 1, 3)
     denominator = 2.0 * (total_days - lag_set).astype(jnp.float32)
     is_live = jnp.arange(K_SLOTS, dtype=jnp.int32) < live_count

time: 142 us -> 141 us (level)
  the two profiles are of different devices: /device:TPU:6 before, /device:TPU:24 now
where the time goes in v11:
time: 141 us; the launch traced here: 140 us
  waiting for transfers between devices  52.5 us (37%)
  blocking collectives  35.8 us (25%)
  matrix products  16.1 us (11%)
  starting transfers between devices  14.8 us (10%)
  local copies, waits for them, and re-layouts  9.39 us (7%)
  between operations  6.46 us (5%)
  other arithmetic  5.49 us (4%)
    all_to_all x1, waiting for transfers between devices, local(): received = lax.all_to_all(product, 'tz', 0, 0, tiled=True)  42.8 us
    all_gather x1, blocking collectives, local(): stats = lax.all_gather(jnp.stack([shard_mean, shard_square], 0), TIME)  21.5 us
    dot_general x9, matrix products, local(): lax.dot_general(left, right, (((1,), (1,)), ((), ())), preferred_element_...  16.1 us
    all_gather x1, blocking collectives, local(): row = lax.all_gather(extended, 'lx')  14.3 us
    ppermute x1, waiting for transfers between devices, local(): lax.ppermute(row, 'ly', [(i, (i - 1) % rows_size) for i in range(rows_siz...  5.33 us
    all_to_all x1, starting transfers between devices, local(): received = lax.all_to_all(product, 'tz', 0, 0, tiled=True)  4.98 us
    ppermute x1, starting transfers between devices, local(): lax.ppermute(row, 'ly', [(i, (i + 1) % rows_size) for i in range(rows_siz...  4.68 us
    dynamic_slice x4, local copies, waits for them, and re-layouts, dslice(): lax.dynamic_slice_in_dim(value, start, size, axis, allow_negative_indices...  4.05 us
  transfers between devices with their start and end apart: 5, of which 4 were waited for; matrix products, arithmetic and copies ran while one was open for 4% of the time, Pallas kernels for 0%

profile of v11, /device:TPU:24, one launch (start us, length us, event | category | flops | bytes accessed | tf_op | source)
XLA Modules:
  0.0 140.5 jit_solution(7625747954278512029)
XLA Ops:
  0.0 0.8 slice.64
  0.8 1.3 collective-permute-start
  2.0 0.9 constant_dynamic-update-slice_fusion.1
  3.0 0.9 collective-permute-done
  3.9 14.3 %all-gather = bf16[512,640]{1,0:T(8,128)(2,1)S(1)} all-gather(bf16[128,640]{1,0:T(8,128)(2,1)S(1)} %constant_dynamic-update-slice_fusion), channel_id=2, replica_groups=mesh['ly'=8,'lx'=4,'tz'=8,'tc'=2] {'lx'}, dimensions={0}, use_global_device_ids=true | all-gather | bytes 819200 | tf_op jit(solution)/shard_map/all_gather | solution.py:33
  18.1 4.7 %collective-permute-start.1 = (bf16[4,128,640]{2,1,0:T(8,128)(2,1)S(1)}, bf16[4,128,640]{2,1,0:T(8,128)(2,1)S(1)}, u32[]{:S(2)}, u32[]{:S(2)}) collective-permute-start(bf16[4,128,640]{2,1,0:T(8,128)(2,1)S(1)} %bitcast.39), channel_id=1, source_target_pairs={{0,64},{64,128},{128,192},{192,256},{256,320},{320,384},{384,448},... | collective-permute-start | bytes 1966088 | tf_op jit(solution)/shard_map/ppermute | solution.py:35
  22.8 1.9 %collective-permute-start.2 = (bf16[4,128,640]{2,1,0:T(8,128)(2,1)S(1)}, bf16[4,128,640]{2,1,0:T(8,128)(2,1)S(1)}, u32[]{:S(2)}, u32[]{:S(2)}) collective-permute-start(bf16[4,128,640]{2,1,0:T(8,128)(2,1)S(1)} %bitcast.40), channel_id=1, source_target_pairs={{0,448},{64,0},{128,64},{192,128},{256,192},{320,256},{384,320},{4... | collective-permute-start | bytes 1966088 | tf_op jit(solution)/shard_map/ppermute | solution.py:36
  24.8 1.7 %fusion.52 = (s32[1]{0:T(128)}, s32[1]{0:T(128)}, s32[1]{0:T(128)}, s32[1]{0:T(128)}, s32[1]{0:T(128)}, /*index=5*/s32[1]{0:T(128)}, s32[1]{0:T(128)}, s32[1]{0:T(128)}, s32[1]{0:T(128)}) fusion(s32[9]{0:T(128)} %param.7), kind=kLoop, calls=%fused_computation.113 | loop fusion | bytes 72 | tf_op jit(solution)/shard_map/slice | solution.py:85
  32.0 0.9 fusion.38
  32.9 0.7 fusion.53
  33.5 3.6 %collective-permute-done.1 = bf16[4,128,640]{2,1,0:T(8,128)(2,1)S(1)} collective-permute-done((bf16[4,128,640]{2,1,0:T(8,128)(2,1)S(1)}, bf16[4,128,640]{2,1,0:T(8,128)(2,1)S(1)}, u32[]{:S(2)}, u32[]{:S(2)}) %collective-permute-start.1) | collective-permute-done | bytes 655392 | tf_op jit(solution)/shard_map/ppermute | solution.py:35
  37.1 5.3 %collective-permute-done.2 = bf16[4,128,640]{2,1,0:T(8,128)(2,1)S(1)} collective-permute-done((bf16[4,128,640]{2,1,0:T(8,128)(2,1)S(1)}, bf16[4,128,640]{2,1,0:T(8,128)(2,1)S(1)}, u32[]{:S(2)}, u32[]{:S(2)}) %collective-permute-start.2) | collective-permute-done | bytes 655392 | tf_op jit(solution)/shard_map/ppermute | solution.py:36
  42.4 0.2 pad_maximum_fusion.1
  42.7 2.0 %constant_dynamic-slice_fusion.20 = (bf16[2,128,640]{2,1,0:T(8,128)(2,1)S(1)}, bf16[2,128,640]{2,1,0:T(8,128)(2,1)S(1)}, bf16[2,128,640]{2,1,0:T(8,128)(2,1)S(1)}) fusion(bf16[12,128,640]{2,1,0:T(8,128)(2,1)S(1)} %pad_maximum_fusion.1, s32[]{:T(128)} %bitcast.2, s32[]{:T(128)} %bitcast.6, s32[]{:T(128)} %bitcast.4), kind=kLoop, calls=%fused_computation.86 | loop fusion | bytes 1966092 | tf_op jit(solution)/shard_map/dynamic_slice | solution.py:14
  44.7 0.2 pad_maximum_fusion.2
  44.9 0.2 convert_reduce_fusion
  45.1 1.9 %collective-permute-start.3 = (bf16[896,640]{1,0:T(8,128)(2,1)S(1)}, bf16[896,640]{1,0:T(8,128)(2,1)S(1)}, u32[]{:S(2)}, u32[]{:S(2)}) collective-permute-start(bf16[896,640]{1,0:T(8,128)(2,1)S(1)} %get-tuple-element.14), channel_id=1, source_target_pairs={{0,1},{1,0},{2,3},{3,2},{4,5},{5,4},{6,7},{7,6},{8,9},{9,8},{10,11... | collective-permute-start | bytes 3440648 | tf_op jit(solution)/shard_map/ppermute | solution.py:47
  47.1 0.5 fusion.1
  47.6 21.5 %all-gather.2 = f32[16,2,896]{2,1,0:T(2,128)S(1)} all-gather(f32[1,2,896]{2,1,0:T(2,128)S(1)} %maximum_bitcast_fusion), channel_id=3, replica_groups=mesh['ly'=8,'lx'=4,'tz'=8,'tc'=2] {'tz','tc'}, dimensions={0}, use_global_device_ids=true | all-gather | bytes 121856 | tf_op jit(solution)/shard_map/all_gather | solution.py:51
  69.0 0.1 slice_reduce_fusion.1
  69.2 0.0 collective-permute-done.3
  69.2 1.0 fusion.5
  70.2 0.1 slice.85
  70.3 1.2 select_convert_fusion
  71.5 0.1 slice.91
  71.6 0.2 slice.92
  71.9 0.7 constant_dynamic-slice_fusion
  72.6 0.7 constant_dynamic-slice_fusion.1
  73.3 1.8 %convolution_dynamic-update-slice_fusion.8 = f32[64,6912]{1,0:T(8,128)} fusion(bf16[64,1024]{1,0:T(8,128)(2,1)S(1)} %get-tuple-element.33, bf16[64,1152]{1,0:T(8,128)(2,1)S(1)} %get-tuple-element.24, bf16[768,1024]{1,0:T(8,128)(2,1)S(1)} %slice.92, bf16[768,1152]{1,0:T(8,128)(2,1)S(1)} %slice.91), kind=kOutput, calls=%fused_computation.19 | convolution fusion | flops 221151232 | bytes 3817472 | tf_op jit(solution)/shard_map/dot_general | solution.py:94
  75.1 1.8 %convolution_dynamic-update-slice_fusion.7 = f32[64,6912]{1,0:T(8,128)} fusion(f32[64,6912]{1,0:T(8,128)} %convolution_dynamic-update-slice_fusion.8, bf16[64,1024]{1,0:T(8,128)(2,1)S(1)} %get-tuple-element.32, bf16[64,1152]{1,0:T(8,128)(2,1)S(1)} %get-tuple-element.23, bf16[768,1024]{1,0:T(8,128)(2,1)S(1)} %slice.92, bf16[768,1152]{1,0:T(8,128)(2,1)S(1)} %slice.91), kind=kOutput, calls=%fused_computation.18 | convolution fusion | flops 221151232 | bytes 3817472 | tf_op jit(solution)/shard_map/dot_general | solution.py:94
  76.9 1.8 %convolution_dynamic-update-slice_fusion.6 = f32[64,6912]{1,0:T(8,128)} fusion(f32[64,6912]{1,0:T(8,128)} %convolution_dynamic-update-slice_fusion.7, bf16[64,1024]{1,0:T(8,128)(2,1)S(1)} %get-tuple-element.31, bf16[64,1152]{1,0:T(8,128)(2,1)S(1)} %get-tuple-element.22, bf16[768,1024]{1,0:T(8,128)(2,1)S(1)} %slice.92, bf16[768,1152]{1,0:T(8,128)(2,1)S(1)} %slice.91), kind=kOutput, calls=%fused_computation.17 | convolution fusion | flops 221151232 | bytes 3817472 | tf_op jit(solution)/shard_map/dot_general | solution.py:94
  78.7 1.8 %convolution_dynamic-update-slice_fusion.5 = f32[64,6912]{1,0:T(8,128)} fusion(f32[64,6912]{1,0:T(8,128)} %convolution_dynamic-update-slice_fusion.6, bf16[64,1024]{1,0:T(8,128)(2,1)S(1)} %get-tuple-element.30, bf16[64,1152]{1,0:T(8,128)(2,1)S(1)} %get-tuple-element.21, bf16[768,1024]{1,0:T(8,128)(2,1)S(1)} %slice.92, bf16[768,1152]{1,0:T(8,128)(2,1)S(1)} %slice.91), kind=kOutput, calls=%fused_computation.16 | convolution fusion | flops 221151232 | bytes 3817472 | tf_op jit(solution)/shard_map/dot_general | solution.py:94
  80.5 1.8 %convolution_dynamic-update-slice_fusion.4 = f32[64,6912]{1,0:T(8,128)} fusion(f32[64,6912]{1,0:T(8,128)} %convolution_dynamic-update-slice_fusion.5, bf16[64,1024]{1,0:T(8,128)(2,1)S(1)} %get-tuple-element.29, bf16[64,1152]{1,0:T(8,128)(2,1)S(1)} %get-tuple-element.20, bf16[768,1024]{1,0:T(8,128)(2,1)S(1)} %slice.92, bf16[768,1152]{1,0:T(8,128)(2,1)S(1)} %slice.91), kind=kOutput, calls=%fused_computation.15 | convolution fusion | flops 221151232 | bytes 3817472 | tf_op jit(solution)/shard_map/dot_general | solution.py:94
  82.3 1.8 %convolution_dynamic-update-slice_fusion.3 = f32[64,6912]{1,0:T(8,128)} fusion(f32[64,6912]{1,0:T(8,128)} %convolution_dynamic-update-slice_fusion.4, bf16[64,1024]{1,0:T(8,128)(2,1)S(1)} %get-tuple-element.28, bf16[64,1152]{1,0:T(8,128)(2,1)S(1)} %get-tuple-element.19, bf16[768,1024]{1,0:T(8,128)(2,1)S(1)} %slice.92, bf16[768,1152]{1,0:T(8,128)(2,1)S(1)} %slice.91), kind=kOutput, calls=%fused_computation.14 | convolution fusion | flops 221151232 | bytes 3817472 | tf_op jit(solution)/shard_map/dot_general | solution.py:94
  84.0 1.8 %convolution_dynamic-update-slice_fusion.2 = f32[64,6912]{1,0:T(8,128)} fusion(f32[64,6912]{1,0:T(8,128)} %convolution_dynamic-update-slice_fusion.3, bf16[64,1024]{1,0:T(8,128)(2,1)S(1)} %get-tuple-element.27, bf16[64,1152]{1,0:T(8,128)(2,1)S(1)} %get-tuple-element.18, bf16[768,1024]{1,0:T(8,128)(2,1)S(1)} %slice.92, bf16[768,1152]{1,0:T(8,128)(2,1)S(1)} %slice.91), kind=kOutput, calls=%fused_computation.13 | convolution fusion | flops 221151232 | bytes 3817472 | tf_op jit(solution)/shard_map/dot_general | solution.py:94
  85.8 1.8 %convolution_dynamic-update-slice_fusion.1 = f32[64,6912]{1,0:T(8,128)} fusion(f32[64,6912]{1,0:T(8,128)} %convolution_dynamic-update-slice_fusion.2, bf16[64,1024]{1,0:T(8,128)(2,1)S(1)} %get-tuple-element.26, bf16[64,1152]{1,0:T(8,128)(2,1)S(1)} %get-tuple-element.17, bf16[768,1024]{1,0:T(8,128)(2,1)S(1)} %slice.92, bf16[768,1152]{1,0:T(8,128)(2,1)S(1)} %slice.91), kind=kOutput, calls=%fused_computation.12 | convolution fusion | flops 221151232 | bytes 3817472 | tf_op jit(solution)/shard_map/dot_general | solution.py:94
  87.6 1.8 %convolution_dynamic-update-slice_fusion = f32[64,6912]{1,0:T(8,128)} fusion(f32[64,6912]{1,0:T(8,128)} %convolution_dynamic-update-slice_fusion.1, bf16[64,1024]{1,0:T(8,128)(2,1)S(1)} %get-tuple-element.25, bf16[64,1152]{1,0:T(8,128)(2,1)S(1)} %get-tuple-element.16, bf16[768,1024]{1,0:T(8,128)(2,1)S(1)} %slice.92, bf16[768,1152]{1,0:T(8,128)(2,1)S(1)} %slice.91), kind=kOutput, calls=%fused_computation.11 | convolution fusion | flops 221151232 | bytes 3817472 | tf_op jit(solution)/shard_map/dot_general | solution.py:94
  89.4 5.0 %all-to-all-start = ((f32[8,8,6912]{2,1,0:T(8,128)}), f32[8,8,6912]{2,1,0:T(8,128)S(1)}, u32[]{:S(2)}, u32[]{:S(2)}) async-start(f32[8,8,6912]{2,1,0:T(8,128)} %bitcast.24), calls=%async_computation | async-start | bytes 3538944 | tf_op jit(solution)/shard_map/all_to_all | solution.py:100
  94.4 0.0 copy-done.1
  94.4 0.6 dynamic_slice.78
  95.6 0.7 iota_compare_fusion.1
  96.3 0.0 copy-done
  96.3 42.8 %all-to-all-done = f32[8,8,6912]{2,1,0:T(8,128)S(1)} async-done(((f32[8,8,6912]{2,1,0:T(8,128)}), f32[8,8,6912]{2,1,0:T(8,128)S(1)}, u32[]{:S(2)}, u32[]{:S(2)}) %all-to-all-start) | async-done | bytes 1769504 | tf_op jit(solution)/shard_map/all_to_all | solution.py:100
  139.1 0.1 reduce_sum.68
  139.2 0.1 reshape.96
  139.3 0.3 multiply_reduce_fusion
  139.6 0.1 divide_bitcast_fusion
  139.7 0.7 copy.6
  (18 shorter events, 0.2 us)
Async XLA Ops:
  0.8 3.1 %collective-permute-start = (bf16[128,128]{1,0:T(8,128)(2,1)S(1)}, bf16[128,128]{1,0:T(8,128)(2,1)S(1)}, u32[]{:S(2)}, u32[]{:S(2)}) collective-permute-start(bf16[128,128]{1,0:T(8,128)(2,1)S(1)} %slice.64), channel_id=1, source_target_pairs={{1,0},{2,1},{3,2},{4,3},{5,4},{6,5},{7,6},{8,7},{9,8},{10,9},{11,1... | collective-permute-start | bytes 98312 | tf_op jit(solution)/shard_map/ppermute | solution.py:25
  18.1 18.9 %collective-permute-start.1 = (bf16[4,128,640]{2,1,0:T(8,128)(2,1)S(1)}, bf16[4,128,640]{2,1,0:T(8,128)(2,1)S(1)}, u32[]{:S(2)}, u32[]{:S(2)}) collective-permute-start(bf16[4,128,640]{2,1,0:T(8,128)(2,1)S(1)} %bitcast.39), channel_id=1, source_target_pairs={{0,64},{64,128},{128,192},{192,256},{256,320},{320,384},{384,448},... | collective-permute-start | bytes 1966088 | tf_op jit(solution)/shard_map/ppermute | solution.py:35
  22.8 19.6 %collective-permute-start.2 = (bf16[4,128,640]{2,1,0:T(8,128)(2,1)S(1)}, bf16[4,128,640]{2,1,0:T(8,128)(2,1)S(1)}, u32[]{:S(2)}, u32[]{:S(2)}) collective-permute-start(bf16[4,128,640]{2,1,0:T(8,128)(2,1)S(1)} %bitcast.40), channel_id=1, source_target_pairs={{0,448},{64,0},{128,64},{192,128},{256,192},{320,256},{384,320},{4... | collective-permute-start | bytes 1966088 | tf_op jit(solution)/shard_map/ppermute | solution.py:36
  45.1 24.1 %collective-permute-start.3 = (bf16[896,640]{1,0:T(8,128)(2,1)S(1)}, bf16[896,640]{1,0:T(8,128)(2,1)S(1)}, u32[]{:S(2)}, u32[]{:S(2)}) collective-permute-start(bf16[896,640]{1,0:T(8,128)(2,1)S(1)} %get-tuple-element.14), channel_id=1, source_target_pairs={{0,1},{1,0},{2,3},{3,2},{4,5},{5,4},{6,7},{7,6},{8,9},{9,8},{10,11... | collective-permute-start | bytes 3440648 | tf_op jit(solution)/shard_map/ppermute | solution.py:47
  89.4 5.0 %copy-start.1 = (s32[16]{0:T(128)S(1)}, s32[16]{0:T(128)}, u32[]{:S(2)}) copy-start(s32[16]{0:T(128)} %param.6) | copy-start | bytes 196
  89.4 6.9 %copy-start = (s32[9]{0:T(128)S(1)}, s32[9]{0:T(128)}, u32[]{:S(2)}) copy-start(s32[9]{0:T(128)} %param.7) | copy-start | bytes 112
  89.4 49.7 %all-to-all-start = ((f32[8,8,6912]{2,1,0:T(8,128)}), f32[8,8,6912]{2,1,0:T(8,128)S(1)}, u32[]{:S(2)}, u32[]{:S(2)}) async-start(f32[8,8,6912]{2,1,0:T(8,128)} %bitcast.24), calls=%async_computation | async-start | bytes 3538944 | tf_op jit(solution)/shard_map/all_to_all | solution.py:100

commit v12 on v8

--- a/solution.py
+++ b/solution.py
@@ -95,9 +95,13 @@
                 left, right, (((1,), (1,)), ((), ())), preferred_element_type=jnp.float32
             )
         )
-    product = jnp.concatenate(pieces, 1)
-
-    comoment = lax.psum_scatter(product, "tz", scatter_dimension=0, tiled=True)
+    early = 5
+    scattered = lax.psum_scatter(
+        jnp.concatenate(pieces[:early], 1), "tz", scatter_dimension=0, tiled=True
+    )
+    received = lax.all_to_all(jnp.concatenate(pieces[early:], 1), "tz", 0, 0, tiled=True)
+    summed = jnp.sum(received.reshape(tz_size, out_rows, -1), axis=0)
+    comoment = jnp.concatenate([scattered, summed], 1)
     comoment = comoment.reshape(out_rows, NLAG, K_SLOTS, block_width).transpose(0, 2, 1, 3)
     denominator = 2.0 * (total_days - lag_set).astype(jnp.float32)
     is_live = jnp.arange(K_SLOTS, dtype=jnp.int32) < live_count

time: 142 us -> 147 us (1.035); the launches traced: 142 us -> 144 us
  waiting for transfers between devices: 46.4 us -> 38.9 us
  starting transfers between devices: 10.2 us -> 15.1 us
  matrix products: 9.83 us -> 14.3 us
    reduce_scatter x1, waiting for transfers between devices: 41.8 us -> 6.97 us  [local(): lax.psum_scatter(jnp.concatenate(pieces[:early], 1), 'tz', scatter_dimens...]
    all_to_all x0 -> x1, waiting for transfers between devices: none -> 27.4 us  [local(): lax.all_to_all(jnp.concatenate(pieces[early:], 1), 'tz', 0, 0, tiled=True)]
    all_to_all x0 -> x1, starting transfers between devices: none -> 4.85 us  [local(): lax.all_to_all(jnp.concatenate(pieces[early:], 1), 'tz', 0, 0, tiled=True)]
    dot_general x9, matrix products: 9.83 us -> 14.3 us  [local(): lax.dot_general(left, right, (((1,), (1,)), ((), ())), preferred_element_...]
    dynamic_slice x4, local copies, waits for them, and re-layouts: 4.05 us -> 5.58 us  [dslice(): lax.dynamic_slice_in_dim(value, start, size, axis, allow_negative_indices...]
  transfers between devices with their start and end apart: 5 -> 6, of which waited for: 4 -> 5; matrix products, arithmetic and copies ran while one was open for 4% -> 9% of each run, Pallas kernels for 0% -> 0%
where the time goes in v12:
time: 147 us; the launch traced here: 144 us
  waiting for transfers between devices  38.9 us (26%)
  blocking collectives  37.7 us (26%)
  between operations  20 us (14%)
  starting transfers between devices  15.1 us (10%)
  matrix products  14.3 us (10%)
  local copies, waits for them, and re-layouts  10.8 us (7%)
  other arithmetic  7.27 us (5%)
    all_to_all x1, waiting for transfers between devices, local(): lax.all_to_all(jnp.concatenate(pieces[early:], 1), 'tz', 0, 0, tiled=True)  27.4 us
    all_gather x1, blocking collectives, local(): stats = lax.all_gather(jnp.stack([shard_mean, shard_square], 0), TIME)  21.4 us
    all_gather x1, blocking collectives, local(): row = lax.all_gather(extended, 'lx')  16.3 us
    dot_general x9, matrix products, local(): lax.dot_general(left, right, (((1,), (1,)), ((), ())), preferred_element_...  14.3 us
    reduce_scatter x1, waiting for transfers between devices, local(): lax.psum_scatter(jnp.concatenate(pieces[:early], 1), 'tz', scatter_dimens...  6.97 us
    dynamic_slice x4, local copies, waits for them, and re-layouts, dslice(): lax.dynamic_slice_in_dim(value, start, size, axis, allow_negative_indices...  5.58 us
    ppermute x1, starting transfers between devices, local(): lax.ppermute(row, 'ly', [(i, (i - 1) % rows_size) for i in range(rows_siz...  5.13 us
    all_to_all x1, starting transfers between devices, local(): lax.all_to_all(jnp.concatenate(pieces[early:], 1), 'tz', 0, 0, tiled=True)  4.85 us
  transfers between devices with their start and end apart: 6, of which 5 were waited for; matrix products, arithmetic and copies ran while one was open for 9% of the time, Pallas kernels for 0%

profile of v12, /device:TPU:6, one launch (start us, length us, event | category | flops | bytes accessed | tf_op | source)
XLA Modules:
  0.0 144.1 jit_solution(13730156525233412112)
XLA Ops:
  6.5 0.8 slice.64
  7.3 1.3 collective-permute-start
  8.6 0.9 constant_dynamic-update-slice_fusion.1
  9.5 0.9 collective-permute-done
  10.4 16.3 %all-gather = bf16[512,640]{1,0:T(8,128)(2,1)S(1)} all-gather(bf16[128,640]{1,0:T(8,128)(2,1)S(1)} %constant_dynamic-update-slice_fusion), channel_id=2, replica_groups=mesh['ly'=8,'lx'=4,'tz'=8,'tc'=2] {'lx'}, dimensions={0}, use_global_device_ids=true | all-gather | bytes 819200 | tf_op jit(solution)/shard_map/all_gather | solution.py:33
  26.7 1.9 %collective-permute-start.1 = (bf16[4,128,640]{2,1,0:T(8,128)(2,1)S(1)}, bf16[4,128,640]{2,1,0:T(8,128)(2,1)S(1)}, u32[]{:S(2)}, u32[]{:S(2)}) collective-permute-start(bf16[4,128,640]{2,1,0:T(8,128)(2,1)S(1)} %bitcast.41), channel_id=1, source_target_pairs={{0,64},{64,128},{128,192},{192,256},{256,320},{320,384},{384,448},... | collective-permute-start | bytes 1966088 | tf_op jit(solution)/shard_map/ppermute | solution.py:35
  28.6 5.1 %collective-permute-start.2 = (bf16[4,128,640]{2,1,0:T(8,128)(2,1)S(1)}, bf16[4,128,640]{2,1,0:T(8,128)(2,1)S(1)}, u32[]{:S(2)}, u32[]{:S(2)}) collective-permute-start(bf16[4,128,640]{2,1,0:T(8,128)(2,1)S(1)} %bitcast.42), channel_id=1, source_target_pairs={{0,448},{64,0},{128,64},{192,128},{256,192},{320,256},{384,320},{4... | collective-permute-start | bytes 1966088 | tf_op jit(solution)/shard_map/ppermute | solution.py:36
  33.8 1.7 %fusion.56 = (s32[1]{0:T(128)}, s32[1]{0:T(128)}, s32[1]{0:T(128)}, s32[1]{0:T(128)}, s32[1]{0:T(128)}, /*index=5*/s32[1]{0:T(128)}, s32[1]{0:T(128)}, s32[1]{0:T(128)}, s32[1]{0:T(128)}) fusion(s32[9]{0:T(128)} %param.7), kind=kLoop, calls=%fused_computation.115 | loop fusion | bytes 72 | tf_op jit(solution)/shard_map/slice | solution.py:85
  41.0 0.9 fusion.42
  41.9 0.7 fusion.57
  42.6 2.5 %collective-permute-done.1 = bf16[4,128,640]{2,1,0:T(8,128)(2,1)S(1)} collective-permute-done((bf16[4,128,640]{2,1,0:T(8,128)(2,1)S(1)}, bf16[4,128,640]{2,1,0:T(8,128)(2,1)S(1)}, u32[]{:S(2)}, u32[]{:S(2)}) %collective-permute-start.1) | collective-permute-done | bytes 655392 | tf_op jit(solution)/shard_map/ppermute | solution.py:35
  45.1 1.2 collective-permute-done.2
  46.3 0.2 pad_maximum_fusion.1
  46.5 2.0 %constant_dynamic-slice_fusion.20 = (bf16[2,128,640]{2,1,0:T(8,128)(2,1)S(1)}, bf16[2,128,640]{2,1,0:T(8,128)(2,1)S(1)}, bf16[2,128,640]{2,1,0:T(8,128)(2,1)S(1)}) fusion(bf16[12,128,640]{2,1,0:T(8,128)(2,1)S(1)} %pad_maximum_fusion.1, s32[]{:T(128)} %bitcast.2, s32[]{:T(128)} %bitcast.6, s32[]{:T(128)} %bitcast.4), kind=kLoop, calls=%fused_computation.88 | loop fusion | bytes 1966092 | tf_op jit(solution)/shard_map/dynamic_slice | solution.py:14
  48.6 0.2 pad_maximum_fusion.2
  48.7 0.2 convert_reduce_fusion
  49.0 1.9 %collective-permute-start.3 = (bf16[896,640]{1,0:T(8,128)(2,1)S(1)}, bf16[896,640]{1,0:T(8,128)(2,1)S(1)}, u32[]{:S(2)}, u32[]{:S(2)}) collective-permute-start(bf16[896,640]{1,0:T(8,128)(2,1)S(1)} %get-tuple-element.12), channel_id=1, source_target_pairs={{0,1},{1,0},{2,3},{3,2},{4,5},{5,4},{6,7},{7,6},{8,9},{9,8},{10,11... | collective-permute-start | bytes 3440648 | tf_op jit(solution)/shard_map/ppermute | solution.py:47
  50.9 0.5 fusion.1
  51.4 21.4 %all-gather.2 = f32[16,2,896]{2,1,0:T(2,128)S(1)} all-gather(f32[1,2,896]{2,1,0:T(2,128)S(1)} %maximum_bitcast_fusion.1), channel_id=3, replica_groups=mesh['ly'=8,'lx'=4,'tz'=8,'tc'=2] {'tz','tc'}, dimensions={0}, use_global_device_ids=true | all-gather | bytes 121856 | tf_op jit(solution)/shard_map/all_gather | solution.py:51
  72.8 0.1 slice_reduce_fusion.1
  73.0 1.0 fusion.5
  74.0 0.1 slice.85
  74.0 1.2 select_convert_fusion
  75.2 0.1 slice.91
  75.4 0.2 slice.92
  75.6 1.5 %constant_dynamic-slice_fusion.8 = (bf16[64,1024]{1,0:T(8,128)(2,1)S(1)}, bf16[64,1024]{1,0:T(8,128)(2,1)}, bf16[64,1024]{1,0:T(8,128)(2,1)}, bf16[64,1024]{1,0:...) fusion(bf16[64,1152]{1,0:T(8,128)(2,1)S(1)} %dynamic-slice_bitc, ...), kind=kLoop, calls=%fused_computation.76 | loop fusion | bytes 2621476 | tf_op jit(solution)/shard_map/dynamic_slice | solution.py:14
  77.1 1.5 %constant_dynamic-slice_fusion.9 = (bf16[64,1152]{1,0:T(8,128)(2,1)S(1)}, bf16[64,1152]{1,0:T(8,128)(2,1)S(1)}, bf16[64,1152]{1,0:T(8,128)(2,1)}, bf16[64,1152]{...) fusion(bf16[64,1280]{1,0:T(8,128)(2,1)S(1)} %pad_maximum_fusion, ...), kind=kLoop, calls=%fused_computation.77 | loop fusion | bytes 2654244 | tf_op jit(solution)/shard_map/dynamic_slice | solution.py:14
  78.6 1.8 %convolution_dynamic-update-slice_fusion.4 = f32[64,3840]{1,0:T(8,128)} fusion(bf16[64,1024]{1,0:T(8,128)(2,1)S(1)} %get-tuple-element.31, bf16[64,1152]{1,0:T(8,128)(2,1)S(1)} %get-tuple-element.22, bf16[768,1024]{1,0:T(8,128)(2,1)S(1)} %slice.92, bf16[768,1152]{1,0:T(8,128)(2,1)S(1)} %slice.91), kind=kOutput, calls=%fused_computation.15 | convolution fusion | flops 221151232 | bytes 3817472 | tf_op jit(solution)/shard_map/dot_general | solution.py:94
  80.4 1.8 %convolution_dynamic-update-slice_fusion.3 = f32[64,3840]{1,0:T(8,128)} fusion(f32[64,3840]{1,0:T(8,128)} %convolution_dynamic-update-slice_fusion.4, bf16[64,1024]{1,0:T(8,128)(2,1)S(1)} %get-tuple-element.30, bf16[64,1152]{1,0:T(8,128)(2,1)S(1)} %get-tuple-element.21, bf16[768,1024]{1,0:T(8,128)(2,1)S(1)} %slice.92, bf16[768,1152]{1,0:T(8,128)(2,1)S(1)} %slice.91), kind=kOutput, calls=%fused_computation.14 | convolution fusion | flops 221151232 | bytes 3817472 | tf_op jit(solution)/shard_map/dot_general | solution.py:94
  82.2 1.8 %convolution_dynamic-update-slice_fusion.2 = f32[64,3840]{1,0:T(8,128)} fusion(f32[64,3840]{1,0:T(8,128)} %convolution_dynamic-update-slice_fusion.3, bf16[64,1024]{1,0:T(8,128)(2,1)S(1)} %get-tuple-element.29, bf16[64,1152]{1,0:T(8,128)(2,1)S(1)} %get-tuple-element.20, bf16[768,1024]{1,0:T(8,128)(2,1)S(1)} %slice.92, bf16[768,1152]{1,0:T(8,128)(2,1)S(1)} %slice.91), kind=kOutput, calls=%fused_computation.13 | convolution fusion | flops 221151232 | bytes 3817472 | tf_op jit(solution)/shard_map/dot_general | solution.py:94
  84.0 1.8 %convolution_dynamic-update-slice_fusion.1 = f32[64,3840]{1,0:T(8,128)} fusion(f32[64,3840]{1,0:T(8,128)} %convolution_dynamic-update-slice_fusion.2, bf16[64,1024]{1,0:T(8,128)(2,1)S(1)} %get-tuple-element.28, bf16[64,1152]{1,0:T(8,128)(2,1)S(1)} %get-tuple-element.19, bf16[768,1024]{1,0:T(8,128)(2,1)S(1)} %slice.92, bf16[768,1152]{1,0:T(8,128)(2,1)S(1)} %slice.91), kind=kOutput, calls=%fused_computation.12 | convolution fusion | flops 221151232 | bytes 3817472 | tf_op jit(solution)/shard_map/dot_general | solution.py:94
  85.8 1.8 %convolution_dynamic-update-slice_fusion = f32[64,3840]{1,0:T(8,128)} fusion(f32[64,3840]{1,0:T(8,128)} %convolution_dynamic-update-slice_fusion.1, bf16[64,1024]{1,0:T(8,128)(2,1)S(1)} %get-tuple-element.23, bf16[64,1152]{1,0:T(8,128)(2,1)S(1)} %get-tuple-element.14, bf16[768,1024]{1,0:T(8,128)(2,1)S(1)} %slice.92, bf16[768,1152]{1,0:T(8,128)(2,1)S(1)} %slice.91), kind=kOutput, calls=%fused_computation.11 | convolution fusion | flops 221151232 | bytes 3817472 | tf_op jit(solution)/shard_map/dot_general | solution.py:94
  87.6 0.0 reduce-scatter.2.cloned.1.call-update
  87.6 2.1 %fusion.21 = f32[64,768]{1,0:T(8,128)S(1)} fusion(bf16[64,1024]{1,0:T(8,128)(2,1)} %get-tuple-element.27, bf16[64,1152]{1,0:T(8,128)(2,1)} %get-tuple-element.18, bf16[768,1024]{1,0:T(8,128)(2,1)S(1)} %slice.92, bf16[768,1152]{1,0:T(8,128)(2,1)S(1)} %slice.91), kind=kOutput, calls=%fused_computation.37 | convolution fusion | flops 221151232 | bytes 3817472 | tf_op jit(solution)/shard_map/dot_general | solution.py:94
  89.8 1.1 fusion.25
  90.9 1.1 fusion.29
  92.0 1.1 fusion.33
  93.1 0.0 copy-start.5
  93.1 1.0 maximum_bitcast_fusion
  94.1 4.8 %all-to-all-start = ((f32[8,8,3072]{2,1,0:T(8,128)}), f32[8,8,3072]{2,1,0:T(8,128)S(1)}, u32[]{:S(2)}, u32[]{:S(2)}) async-start(f32[8,8,3072]{2,1,0:T(8,128)} %maximum_bitcast_fusion), calls=%async_computation.1 | async-start | bytes 1572864 | tf_op jit(solution)/shard_map/all_to_all | solution.py:102
  98.9 0.6 dynamic_slice.78
  100.2 0.7 iota_compare_fusion.1
  100.9 27.4 %all-to-all-done = f32[8,8,3072]{2,1,0:T(8,128)S(1)} async-done(((f32[8,8,3072]{2,1,0:T(8,128)}), f32[8,8,3072]{2,1,0:T(8,128)S(1)}, u32[]{:S(2)}, u32[]{:S(2)}) %all-to-all-start) | async-done | bytes 786464 | tf_op jit(solution)/shard_map/all_to_all | solution.py:102
  128.3 7.0 %reduce-scatter.2.cloned.1.call-done = f32[8,3840]{1,0:T(8,128)} async-done(((f32[64,3840]{1,0:T(8,128)}), f32[8,3840]{1,0:T(8,128)}) %reduce-scatter.2.cloned.1.call-update) | async-done | bytes 122896 | tf_op jit(solution)/shard_map/reduce_scatter | solution.py:99
  135.2 0.9 pad_maximum_fusion.3
  136.2 0.2 multiply_reduce_fusion
  136.4 0.1 divide_bitcast_fusion
  136.5 0.7 copy.6
  (32 shorter events, 0.2 us)
Async XLA Ops:
  6.5 128.7 %reduce-scatter.2.cloned.1.call-start = ((), (), s32[]{:S(2)}) async-start(), calls=%async_computation.2 | async-start | bytes 1105920 | tf_op jit(solution)/shard_map/reduce_scatter | solution.py:99
  7.3 3.1 %collective-permute-start = (bf16[128,128]{1,0:T(8,128)(2,1)S(1)}, bf16[128,128]{1,0:T(8,128)(2,1)S(1)}, u32[]{:S(2)}, u32[]{:S(2)}) collective-permute-start(bf16[128,128]{1,0:T(8,128)(2,1)S(1)} %slice.64), channel_id=1, source_target_pairs={{1,0},{2,1},{3,2},{4,3},{5,4},{6,5},{7,6},{8,7},{9,8},{10,9},{11,1... | collective-permute-start | bytes 98312 | tf_op jit(solution)/shard_map/ppermute | solution.py:25
  26.7 18.4 %collective-permute-start.1 = (bf16[4,128,640]{2,1,0:T(8,128)(2,1)S(1)}, bf16[4,128,640]{2,1,0:T(8,128)(2,1)S(1)}, u32[]{:S(2)}, u32[]{:S(2)}) collective-permute-start(bf16[4,128,640]{2,1,0:T(8,128)(2,1)S(1)} %bitcast.41), channel_id=1, source_target_pairs={{0,64},{64,128},{128,192},{192,256},{256,320},{320,384},{384,448},... | collective-permute-start | bytes 1966088 | tf_op jit(solution)/shard_map/ppermute | solution.py:35
  28.6 17.6 %collective-permute-start.2 = (bf16[4,128,640]{2,1,0:T(8,128)(2,1)S(1)}, bf16[4,128,640]{2,1,0:T(8,128)(2,1)S(1)}, u32[]{:S(2)}, u32[]{:S(2)}) collective-permute-start(bf16[4,128,640]{2,1,0:T(8,128)(2,1)S(1)} %bitcast.42), channel_id=1, source_target_pairs={{0,448},{64,0},{128,64},{192,128},{256,192},{320,256},{384,320},{4... | collective-permute-start | bytes 1966088 | tf_op jit(solution)/shard_map/ppermute | solution.py:36
  49.0 24.0 %collective-permute-start.3 = (bf16[896,640]{1,0:T(8,128)(2,1)S(1)}, bf16[896,640]{1,0:T(8,128)(2,1)S(1)}, u32[]{:S(2)}, u32[]{:S(2)}) collective-permute-start(bf16[896,640]{1,0:T(8,128)(2,1)S(1)} %get-tuple-element.12), channel_id=1, source_target_pairs={{0,1},{1,0},{2,3},{3,2},{4,5},{5,4},{6,7},{7,6},{8,9},{9,8},{10,11... | collective-permute-start | bytes 3440648 | tf_op jit(solution)/shard_map/ppermute | solution.py:47
  87.6 2.1 %copy-start.1 = (bf16[64,1152]{1,0:T(8,128)(2,1)S(1)}, bf16[64,1152]{1,0:T(8,128)(2,1)}, u32[]{:S(2)}) copy-start(bf16[64,1152]{1,0:T(8,128)(2,1)} %get-tuple-element.17) | copy-start | bytes 442372
  87.6 2.1 %copy-start.4 = (bf16[64,1024]{1,0:T(8,128)(2,1)S(1)}, bf16[64,1024]{1,0:T(8,128)(2,1)}, u32[]{:S(2)}) copy-start(bf16[64,1024]{1,0:T(8,128)(2,1)} %get-tuple-element.26) | copy-start | bytes 393220
  89.8 1.1 copy-start
  89.8 1.1 copy-start.3
  90.9 1.1 copy-start.2
  93.1 5.8 %copy-start.6 = (s32[16]{0:T(128)S(1)}, s32[16]{0:T(128)}, u32[]{:S(2)}) copy-start(s32[16]{0:T(128)} %param.6) | copy-start | bytes 196
  93.1 7.7 %copy-start.5 = (s32[9]{0:T(128)S(1)}, s32[9]{0:T(128)}, u32[]{:S(2)}) copy-start(s32[9]{0:T(128)} %param.7) | copy-start | bytes 112
  94.1 34.2 %all-to-all-start = ((f32[8,8,3072]{2,1,0:T(8,128)}), f32[8,8,3072]{2,1,0:T(8,128)S(1)}, u32[]{:S(2)}, u32[]{:S(2)}) async-start(f32[8,8,3072]{2,1,0:T(8,128)} %maximum_bitcast_fusion), calls=%async_computation.1 | async-start | bytes 1572864 | tf_op jit(solution)/shard_map/all_to_all | solution.py:102
Sparse Core Ops, SparseCore 0:
  87.7 47.4 reduce-scatter.1

commit v13 on v8

--- a/solution.py
+++ b/solution.py
@@ -95,9 +95,12 @@
                 left, right, (((1,), (1,)), ((), ())), preferred_element_type=jnp.float32
             )
         )
-    product = jnp.concatenate(pieces, 1)
-
-    comoment = lax.psum_scatter(product, "tz", scatter_dimension=0, tiled=True)
+    early = 5
+    sums = []
+    for part in (pieces[:early], pieces[early:]):
+        received = lax.all_to_all(jnp.concatenate(part, 1), "tz", 0, 0, tiled=True)
+        sums.append(jnp.sum(received.reshape(tz_size, out_rows, -1), axis=0))
+    comoment = jnp.concatenate(sums, 1)
     comoment = comoment.reshape(out_rows, NLAG, K_SLOTS, block_width).transpose(0, 2, 1, 3)
     denominator = 2.0 * (total_days - lag_set).astype(jnp.float32)
     is_live = jnp.arange(K_SLOTS, dtype=jnp.int32) < live_count

time: 142 us -> 141 us (level)
  the two profiles are of different devices: /device:TPU:6 before, /device:TPU:24 now
where the time goes in v13:
time: 141 us
  waiting for transfers between devices  48.4 us (34%)
  blocking collectives  35.8 us (25%)
  starting transfers between devices  18.2 us (13%)
  matrix products  15 us (11%)
  local copies, waits for them, and re-layouts  10.1 us (7%)
  between operations  6.63 us (5%)
  other arithmetic  6.45 us (5%)
    all_to_all x2, waiting for transfers between devices, local(): received = lax.all_to_all(jnp.concatenate(part, 1), 'tz', 0, 0, tiled=True)  38.8 us
    all_gather x1, blocking collectives, local(): stats = lax.all_gather(jnp.stack([shard_mean, shard_square], 0), TIME)  21.5 us
    dot_general x9, matrix products, local(): lax.dot_general(left, right, (((1,), (1,)), ((), ())), preferred_element_...  15 us
    all_gather x1, blocking collectives, local(): row = lax.all_gather(extended, 'lx')  14.3 us
    all_to_all x2, starting transfers between devices, local(): received = lax.all_to_all(jnp.concatenate(part, 1), 'tz', 0, 0, tiled=True)  8.4 us
    ppermute x1, waiting for transfers between devices, local(): lax.ppermute(row, 'ly', [(i, (i - 1) % rows_size) for i in range(rows_siz...  5.33 us
    dynamic_slice x4, local copies, waits for them, and re-layouts, dslice(): lax.dynamic_slice_in_dim(value, start, size, axis, allow_negative_indices...  4.75 us
    ppermute x1, starting transfers between devices, local(): lax.ppermute(row, 'ly', [(i, (i + 1) % rows_size) for i in range(rows_siz...  4.68 us
  transfers between devices with their start and end apart: 6, of which 5 were waited for; matrix products, arithmetic and copies ran while one was open for 12% of the time, Pallas kernels for 0%

profile of v13, /device:TPU:24, one launch (start us, length us, event | category | flops | bytes accessed | tf_op | source)
XLA Modules:
  0.0 140.5 jit_solution(8235546252733854690)
XLA Ops:
  0.0 0.8 slice.64
  0.8 1.3 collective-permute-start
  2.0 0.9 constant_dynamic-update-slice_fusion.1
  3.0 0.9 collective-permute-done
  3.9 14.3 %all-gather = bf16[512,640]{1,0:T(8,128)(2,1)S(1)} all-gather(bf16[128,640]{1,0:T(8,128)(2,1)S(1)} %constant_dynamic-update-slice_fusion), channel_id=2, replica_groups=mesh['ly'=8,'lx'=4,'tz'=8,'tc'=2] {'lx'}, dimensions={0}, use_global_device_ids=true | all-gather | bytes 819200 | tf_op jit(solution)/shard_map/all_gather | solution.py:33
  18.1 4.7 %collective-permute-start.1 = (bf16[4,128,640]{2,1,0:T(8,128)(2,1)S(1)}, bf16[4,128,640]{2,1,0:T(8,128)(2,1)S(1)}, u32[]{:S(2)}, u32[]{:S(2)}) collective-permute-start(bf16[4,128,640]{2,1,0:T(8,128)(2,1)S(1)} %bitcast.41), channel_id=1, source_target_pairs={{0,64},{64,128},{128,192},{192,256},{256,320},{320,384},{384,448},... | collective-permute-start | bytes 1966088 | tf_op jit(solution)/shard_map/ppermute | solution.py:35
  22.8 1.9 %collective-permute-start.2 = (bf16[4,128,640]{2,1,0:T(8,128)(2,1)S(1)}, bf16[4,128,640]{2,1,0:T(8,128)(2,1)S(1)}, u32[]{:S(2)}, u32[]{:S(2)}) collective-permute-start(bf16[4,128,640]{2,1,0:T(8,128)(2,1)S(1)} %bitcast.42), channel_id=1, source_target_pairs={{0,448},{64,0},{128,64},{192,128},{256,192},{320,256},{384,320},{4... | collective-permute-start | bytes 1966088 | tf_op jit(solution)/shard_map/ppermute | solution.py:36
  24.8 1.7 %fusion.56 = (s32[1]{0:T(128)}, s32[1]{0:T(128)}, s32[1]{0:T(128)}, s32[1]{0:T(128)}, s32[1]{0:T(128)}, /*index=5*/s32[1]{0:T(128)}, s32[1]{0:T(128)}, s32[1]{0:T(128)}, s32[1]{0:T(128)}) fusion(s32[9]{0:T(128)} %param.7), kind=kLoop, calls=%fused_computation.115 | loop fusion | bytes 72 | tf_op jit(solution)/shard_map/slice | solution.py:85
  32.1 0.9 fusion.42
  33.0 0.7 fusion.57
  33.7 3.4 %collective-permute-done.1 = bf16[4,128,640]{2,1,0:T(8,128)(2,1)S(1)} collective-permute-done((bf16[4,128,640]{2,1,0:T(8,128)(2,1)S(1)}, bf16[4,128,640]{2,1,0:T(8,128)(2,1)S(1)}, u32[]{:S(2)}, u32[]{:S(2)}) %collective-permute-start.1) | collective-permute-done | bytes 655392 | tf_op jit(solution)/shard_map/ppermute | solution.py:35
  37.1 5.3 %collective-permute-done.2 = bf16[4,128,640]{2,1,0:T(8,128)(2,1)S(1)} collective-permute-done((bf16[4,128,640]{2,1,0:T(8,128)(2,1)S(1)}, bf16[4,128,640]{2,1,0:T(8,128)(2,1)S(1)}, u32[]{:S(2)}, u32[]{:S(2)}) %collective-permute-start.2) | collective-permute-done | bytes 655392 | tf_op jit(solution)/shard_map/ppermute | solution.py:36
  42.4 0.2 pad_maximum_fusion.1
  42.7 2.0 %constant_dynamic-slice_fusion.20 = (bf16[2,128,640]{2,1,0:T(8,128)(2,1)S(1)}, bf16[2,128,640]{2,1,0:T(8,128)(2,1)S(1)}, bf16[2,128,640]{2,1,0:T(8,128)(2,1)S(1)}) fusion(bf16[12,128,640]{2,1,0:T(8,128)(2,1)S(1)} %pad_maximum_fusion.1, s32[]{:T(128)} %bitcast.2, s32[]{:T(128)} %bitcast.6, s32[]{:T(128)} %bitcast.4), kind=kLoop, calls=%fused_computation.88 | loop fusion | bytes 1966092 | tf_op jit(solution)/shard_map/dynamic_slice | solution.py:14
  44.7 0.2 pad_maximum_fusion.2
  44.9 0.2 convert_reduce_fusion
  45.1 1.9 %collective-permute-start.3 = (bf16[896,640]{1,0:T(8,128)(2,1)S(1)}, bf16[896,640]{1,0:T(8,128)(2,1)S(1)}, u32[]{:S(2)}, u32[]{:S(2)}) collective-permute-start(bf16[896,640]{1,0:T(8,128)(2,1)S(1)} %get-tuple-element.14), channel_id=1, source_target_pairs={{0,1},{1,0},{2,3},{3,2},{4,5},{5,4},{6,7},{7,6},{8,9},{9,8},{10,11... | collective-permute-start | bytes 3440648 | tf_op jit(solution)/shard_map/ppermute | solution.py:47
  47.0 0.5 fusion.1
  47.5 21.5 %all-gather.2 = f32[16,2,896]{2,1,0:T(2,128)S(1)} all-gather(f32[1,2,896]{2,1,0:T(2,128)S(1)} %maximum_bitcast_fusion.1), channel_id=3, replica_groups=mesh['ly'=8,'lx'=4,'tz'=8,'tc'=2] {'tz','tc'}, dimensions={0}, use_global_device_ids=true | all-gather | bytes 121856 | tf_op jit(solution)/shard_map/all_gather | solution.py:51
  69.0 0.1 slice_reduce_fusion.1
  69.2 1.0 fusion.5
  70.1 0.1 slice.85
  70.2 1.2 select_convert_fusion
  71.4 0.1 slice.91
  71.6 0.2 slice.92
  71.8 1.4 %constant_dynamic-slice_fusion.8 = (bf16[64,1024]{1,0:T(8,128)(2,1)S(1)}, bf16[64,1024]{1,0:T(8,128)(2,1)S(1)}, bf16[64,1024]{1,0:T(8,128)(2,1)S(1)}, bf16[64,10...) fusion(bf16[64,1152]{1,0:T(8,128)(2,1)S(1)} %dynamic-slice_bitc, ...), kind=kLoop, calls=%fused_computation.76 | loop fusion | bytes 2621476 | tf_op jit(solution)/shard_map/dynamic_slice | solution.py:14
  73.3 0.7 constant_dynamic-slice_fusion.9
  74.0 1.1 fusion.21
  75.1 1.1 fusion.25
  76.2 1.1 fusion.29
  77.3 1.1 fusion.33
  78.4 0.9 maximum_bitcast_fusion
  79.4 4.8 %all-to-all-start.1 = ((f32[8,8,3072]{2,1,0:T(8,128)}), f32[8,8,3072]{2,1,0:T(8,128)S(1)}, u32[]{:S(2)}, u32[]{:S(2)}) async-start(f32[8,8,3072]{2,1,0:T(8,128)} %maximum_bitcast_fusion), calls=%async_computation.1 | async-start | bytes 1572864 | tf_op jit(solution)/shard_map/all_to_all | solution.py:101
  84.2 3.4 %convolution_dynamic-update-slice_fusion.4 = f32[64,3840]{1,0:T(8,128)} fusion(bf16[64,1024]{1,0:T(8,128)(2,1)} %get-tuple-element.33, bf16[64,1152]{1,0:T(8,128)(2,1)S(1)} %get-tuple-element.24, bf16[768,1024]{1,0:T(8,128)(2,1)} %copy-done, bf16[768,1152]{1,0:T(8,128)(2,1)S(1)} %slice.91), kind=kOutput, calls=%fused_computation.15 | convolution fusion | flops 221151232 | bytes 3817472 | tf_op jit(solution)/shard_map/dot_general | solution.py:94
  87.6 1.8 %convolution_dynamic-update-slice_fusion.3 = f32[64,3840]{1,0:T(8,128)} fusion(f32[64,3840]{1,0:T(8,128)} %convolution_dynamic-update-slice_fusion.4, bf16[64,1024]{1,0:T(8,128)(2,1)S(1)} %copy-done.3, bf16[64,1152]{1,0:T(8,128)(2,1)S(1)} %get-tuple-element.23, bf16[768,1024]{1,0:T(8,128)(2,1)S(1)} %copy-done.1, bf16[768,1152]{1,0:T(8,128)(2,1)S(1)} %slice.91), kind=kOutput, calls=%fused_computation.14 | convolution fusion | flops 221151232 | bytes 3817472 | tf_op jit(solution)/shard_map/dot_general | solution.py:94
  89.4 1.8 %convolution_dynamic-update-slice_fusion.2 = f32[64,3840]{1,0:T(8,128)} fusion(f32[64,3840]{1,0:T(8,128)} %convolution_dynamic-update-slice_fusion.3, bf16[64,1024]{1,0:T(8,128)(2,1)S(1)} %copy-done.2, bf16[64,1152]{1,0:T(8,128)(2,1)S(1)} %get-tuple-element.22, bf16[768,1024]{1,0:T(8,128)(2,1)S(1)} %copy-done.1, bf16[768,1152]{1,0:T(8,128)(2,1)S(1)} %slice.91), kind=kOutput, calls=%fused_computation.13 | convolution fusion | flops 221151232 | bytes 3817472 | tf_op jit(solution)/shard_map/dot_general | solution.py:94
  91.2 1.8 %convolution_dynamic-update-slice_fusion.1 = f32[64,3840]{1,0:T(8,128)} fusion(f32[64,3840]{1,0:T(8,128)} %convolution_dynamic-update-slice_fusion.2, bf16[64,1024]{1,0:T(8,128)(2,1)S(1)} %get-tuple-element.30, bf16[64,1152]{1,0:T(8,128)(2,1)S(1)} %get-tuple-element.21, bf16[768,1024]{1,0:T(8,128)(2,1)S(1)} %copy-done.1, bf16[768,1152]{1,0:T(8,128)(2,1)S(1)} %slice.91), kind=kOutput, calls=%fused_computation.12 | convolution fusion | flops 221151232 | bytes 3817472 | tf_op jit(solution)/shard_map/dot_general | solution.py:94
  93.1 1.8 %convolution_dynamic-update-slice_fusion = f32[64,3840]{1,0:T(8,128)} fusion(f32[64,3840]{1,0:T(8,128)} %convolution_dynamic-update-slice_fusion.1, bf16[64,1024]{1,0:T(8,128)(2,1)S(1)} %get-tuple-element.25, bf16[64,1152]{1,0:T(8,128)(2,1)S(1)} %get-tuple-element.16, bf16[768,1024]{1,0:T(8,128)(2,1)S(1)} %copy-done.1, bf16[768,1152]{1,0:T(8,128)(2,1)S(1)} %slice.91), kind=kOutput, calls=%fused_computation.11 | convolution fusion | flops 221151232 | bytes 3817472 | tf_op jit(solution)/shard_map/dot_general | solution.py:94
  94.9 13.0 %all-to-all-done.1 = f32[8,8,3072]{2,1,0:T(8,128)S(1)} async-done(((f32[8,8,3072]{2,1,0:T(8,128)}), f32[8,8,3072]{2,1,0:T(8,128)S(1)}, u32[]{:S(2)}, u32[]{:S(2)}) %all-to-all-start.1) | async-done | bytes 786464 | tf_op jit(solution)/shard_map/all_to_all | solution.py:101
  107.9 3.6 %all-to-all-start = ((f32[8,8,3840]{2,1,0:T(8,128)}), f32[8,8,3840]{2,1,0:T(8,128)S(1)}, u32[]{:S(2)}, u32[]{:S(2)}) async-start(f32[8,8,3840]{2,1,0:T(8,128)} %bitcast.20), calls=%async_computation | async-start | bytes 1966080 | tf_op jit(solution)/shard_map/all_to_all | solution.py:101
  111.5 0.6 dynamic_slice.78
  112.7 0.7 iota_compare_fusion.1
  113.4 25.7 %all-to-all-done = f32[8,8,3840]{2,1,0:T(8,128)S(1)} async-done(((f32[8,8,3840]{2,1,0:T(8,128)}), f32[8,8,3840]{2,1,0:T(8,128)S(1)}, u32[]{:S(2)}, u32[]{:S(2)}) %all-to-all-start) | async-done | bytes 983072 | tf_op jit(solution)/shard_map/all_to_all | solution.py:101
  139.2 0.1 reduce_sum.77
  139.2 0.1 reshape.100
  139.4 0.3 multiply_reduce_fusion
  139.7 0.1 divide_bitcast_fusion
  139.8 0.7 copy.6
  (31 shorter events, 0.3 us)
Async XLA Ops:
  0.8 3.1 %collective-permute-start = (bf16[128,128]{1,0:T(8,128)(2,1)S(1)}, bf16[128,128]{1,0:T(8,128)(2,1)S(1)}, u32[]{:S(2)}, u32[]{:S(2)}) collective-permute-start(bf16[128,128]{1,0:T(8,128)(2,1)S(1)} %slice.64), channel_id=1, source_target_pairs={{1,0},{2,1},{3,2},{4,3},{5,4},{6,5},{7,6},{8,7},{9,8},{10,9},{11,1... | collective-permute-start | bytes 98312 | tf_op jit(solution)/shard_map/ppermute | solution.py:25
  18.1 18.9 %collective-permute-start.1 = (bf16[4,128,640]{2,1,0:T(8,128)(2,1)S(1)}, bf16[4,128,640]{2,1,0:T(8,128)(2,1)S(1)}, u32[]{:S(2)}, u32[]{:S(2)}) collective-permute-start(bf16[4,128,640]{2,1,0:T(8,128)(2,1)S(1)} %bitcast.41), channel_id=1, source_target_pairs={{0,64},{64,128},{128,192},{192,256},{256,320},{320,384},{384,448},... | collective-permute-start | bytes 1966088 | tf_op jit(solution)/shard_map/ppermute | solution.py:35
  22.8 19.6 %collective-permute-start.2 = (bf16[4,128,640]{2,1,0:T(8,128)(2,1)S(1)}, bf16[4,128,640]{2,1,0:T(8,128)(2,1)S(1)}, u32[]{:S(2)}, u32[]{:S(2)}) collective-permute-start(bf16[4,128,640]{2,1,0:T(8,128)(2,1)S(1)} %bitcast.42), channel_id=1, source_target_pairs={{0,448},{64,0},{128,64},{192,128},{256,192},{320,256},{384,320},{4... | collective-permute-start | bytes 1966088 | tf_op jit(solution)/shard_map/ppermute | solution.py:36
  45.1 24.1 %collective-permute-start.3 = (bf16[896,640]{1,0:T(8,128)(2,1)S(1)}, bf16[896,640]{1,0:T(8,128)(2,1)S(1)}, u32[]{:S(2)}, u32[]{:S(2)}) collective-permute-start(bf16[896,640]{1,0:T(8,128)(2,1)S(1)} %get-tuple-element.14), channel_id=1, source_target_pairs={{0,1},{1,0},{2,3},{3,2},{4,5},{5,4},{6,7},{7,6},{8,9},{9,8},{10,11... | collective-permute-start | bytes 3440648 | tf_op jit(solution)/shard_map/ppermute | solution.py:47
  71.8 5.6 %copy-start = (bf16[768,1024]{1,0:T(8,128)(2,1)}, bf16[768,1024]{1,0:T(8,128)(2,1)S(1)}, u32[]{:S(2)}) copy-start(bf16[768,1024]{1,0:T(8,128)(2,1)S(1)} %slice.92) | copy-start | bytes 4718596
  79.4 28.5 %all-to-all-start.1 = ((f32[8,8,3072]{2,1,0:T(8,128)}), f32[8,8,3072]{2,1,0:T(8,128)S(1)}, u32[]{:S(2)}, u32[]{:S(2)}) async-start(f32[8,8,3072]{2,1,0:T(8,128)} %maximum_bitcast_fusion), calls=%async_computation.1 | async-start | bytes 1572864 | tf_op jit(solution)/shard_map/all_to_all | solution.py:101
  84.2 3.4 %copy-start.1 = (bf16[768,1024]{1,0:T(8,128)(2,1)S(1)}, bf16[768,1024]{1,0:T(8,128)(2,1)}, u32[]{:S(2)}) copy-start(bf16[768,1024]{1,0:T(8,128)(2,1)} %copy-done) | copy-start | bytes 4718596
  84.2 3.4 %copy-start.3 = (bf16[64,1024]{1,0:T(8,128)(2,1)S(1)}, bf16[64,1024]{1,0:T(8,128)(2,1)}, u32[]{:S(2)}) copy-start(bf16[64,1024]{1,0:T(8,128)(2,1)} %get-tuple-element.32) | copy-start | bytes 393220
  87.6 1.8 %copy-start.2 = (bf16[64,1024]{1,0:T(8,128)(2,1)S(1)}, bf16[64,1024]{1,0:T(8,128)(2,1)}, u32[]{:S(2)}) copy-start(bf16[64,1024]{1,0:T(8,128)(2,1)} %get-tuple-element.31) | copy-start | bytes 393220
  93.0 18.4 %copy-start.5 = (s32[16]{0:T(128)S(1)}, s32[16]{0:T(128)}, u32[]{:S(2)}) copy-start(s32[16]{0:T(128)} %param.6) | copy-start | bytes 196
  93.0 20.3 %copy-start.4 = (s32[9]{0:T(128)S(1)}, s32[9]{0:T(128)}, u32[]{:S(2)}) copy-start(s32[9]{0:T(128)} %param.7) | copy-start | bytes 112
  107.9 31.3 %all-to-all-start = ((f32[8,8,3840]{2,1,0:T(8,128)}), f32[8,8,3840]{2,1,0:T(8,128)S(1)}, u32[]{:S(2)}, u32[]{:S(2)}) async-start(f32[8,8,3840]{2,1,0:T(8,128)} %bitcast.20), calls=%async_computation | async-start | bytes 1966080 | tf_op jit(solution)/shard_map/all_to_all | solution.py:101

commit v14 on v11

--- a/solution.py
+++ b/solution.py
@@ -30,7 +30,12 @@
     lx_index = lax.axis_index("lx")
     parity = lax.rem(lx_index, 2)
     block_index = lax.axis_index("ly") * (row_size // 2) + lax.div(lx_index, 2)
-    row = lax.all_gather(extended, "lx")
+    received = [extended] + [
+        lax.ppermute(extended, "lx", [(i, (i - k) % row_size) for i in range(row_size)])
+        for k in range(1, row_size)
+    ]
+    doubled = jnp.stack(received + received, 0)
+    row = dslice(doubled, lax.rem(row_size - lx_index, row_size), row_size, 0)
     rows_size = lax.axis_size("ly")
     before = lax.ppermute(row, "ly", [(i, (i + 1) % rows_size) for i in range(rows_size)])
     after = lax.ppermute(row, "ly", [(i, (i - 1) % rows_size) for i in range(rows_size)])

time: 141 us -> 146 us (1.035)
  blocking collectives: 35.8 us -> 22 us
  starting transfers between devices: 14.8 us -> 25 us
  waiting for transfers between devices: 52.5 us -> 62.5 us
    all_gather x1 -> x0, blocking collectives: 14.3 us -> none  [local(): row = lax.all_gather(extended, 'lx')]
    ppermute x0 -> x3, starting transfers between devices: none -> 10.2 us  [local(): lax.ppermute(extended, 'lx', [(i, (i - k) % row_size) for i in range(row_...]
    ppermute x0 -> x3, waiting for transfers between devices: none -> 7.87 us  [local(): lax.ppermute(extended, 'lx', [(i, (i - k) % row_size) for i in range(row_...]
    ppermute x1, waiting for transfers between devices: 3.55 us -> 5.64 us  [local(): lax.ppermute(row, 'ly', [(i, (i + 1) % rows_size) for i in range(rows_siz...]
    dynamic_slice x4 -> x5, local copies, waits for them, and re-layouts: 4.05 us -> 4.12 us  [dslice(): lax.dynamic_slice_in_dim(value, start, size, axis, allow_negative_indices...]
  transfers between devices with their start and end apart: 5 -> 8, of which waited for: 4 -> 6; matrix products, arithmetic and copies ran while one was open for 4% -> 3% of each run, Pallas kernels for 0% -> 0%
where the time goes in v14:
time: 146 us
  waiting for transfers between devices  62.5 us (43%)
  starting transfers between devices  25 us (17%)
  blocking collectives  22 us (15%)
  matrix products  16.1 us (11%)
  local copies, waits for them, and re-layouts  8.65 us (6%)
  between operations  6.57 us (4%)
  other arithmetic  4.81 us (3%)
    all_to_all x1, waiting for transfers between devices, local(): received = lax.all_to_all(product, 'tz', 0, 0, tiled=True)  42.8 us
    all_gather x1, blocking collectives, local(): stats = lax.all_gather(jnp.stack([shard_mean, shard_square], 0), TIME)  22 us
    dot_general x9, matrix products, local(): lax.dot_general(left, right, (((1,), (1,)), ((), ())), preferred_element_...  16.1 us
    ppermute x3, starting transfers between devices, local(): lax.ppermute(extended, 'lx', [(i, (i - k) % row_size) for i in range(row_...  10.2 us
    ppermute x3, waiting for transfers between devices, local(): lax.ppermute(extended, 'lx', [(i, (i - k) % row_size) for i in range(row_...  7.87 us
    ppermute x1, waiting for transfers between devices, local(): lax.ppermute(row, 'ly', [(i, (i + 1) % rows_size) for i in range(rows_siz...  5.64 us
    ppermute x1, waiting for transfers between devices, local(): lax.ppermute(row, 'ly', [(i, (i - 1) % rows_size) for i in range(rows_siz...  5.33 us
    all_to_all x1, starting transfers between devices, local(): received = lax.all_to_all(product, 'tz', 0, 0, tiled=True)  4.99 us
  transfers between devices with their start and end apart: 8, of which 6 were waited for; matrix products, arithmetic and copies ran while one was open for 3% of the time, Pallas kernels for 0%

profile of v14, /device:TPU:24, one launch (start us, length us, event | category | flops | bytes accessed | tf_op | source)
XLA Modules:
  0.0 145.5 jit_solution(17309494504243320088)
XLA Ops:
  0.0 0.8 slice.64
  0.8 1.3 collective-permute-start
  2.0 0.9 constant_dynamic-update-slice_fusion.1
  3.0 0.9 collective-permute-done
  3.9 4.7 %collective-permute-start.1 = (bf16[128,640]{1,0:T(8,128)(2,1)S(1)}, bf16[128,640]{1,0:T(8,128)(2,1)S(1)}, u32[]{:S(2)}, u32[]{:S(2)}) collective-permute-start(bf16[128,640]{1,0:T(8,128)(2,1)S(1)} %constant_dynamic-update-slice_fusion), channel_id=1, source_target_pairs={{0,48},{16,0},{32,16},{48,32},{1,49},{17,1},{33,17},{49,33},{2,50}... | collective-permute-start | bytes 491528 | tf_op jit(solution)/shard_map/ppermute | solution.py:34
  8.5 2.7 %collective-permute-start.2 = (bf16[128,640]{1,0:T(8,128)(2,1)S(1)}, bf16[128,640]{1,0:T(8,128)(2,1)S(1)}, u32[]{:S(2)}, u32[]{:S(2)}) collective-permute-start(bf16[128,640]{1,0:T(8,128)(2,1)S(1)} %constant_dynamic-update-slice_fusion), channel_id=1, source_target_pairs={{0,32},{16,48},{32,0},{48,16},{1,33},{17,49},{33,1},{49,17},{2,34}... | collective-permute-start | bytes 491528 | tf_op jit(solution)/shard_map/ppermute | solution.py:34
  11.3 2.8 %collective-permute-start.3 = (bf16[128,640]{1,0:T(8,128)(2,1)S(1)}, bf16[128,640]{1,0:T(8,128)(2,1)S(1)}, u32[]{:S(2)}, u32[]{:S(2)}) collective-permute-start(bf16[128,640]{1,0:T(8,128)(2,1)S(1)} %constant_dynamic-update-slice_fusion), channel_id=1, source_target_pairs={{0,16},{16,32},{32,48},{48,0},{1,17},{17,33},{33,49},{49,1},{2,18}... | collective-permute-start | bytes 491528 | tf_op jit(solution)/shard_map/ppermute | solution.py:34
  14.1 3.2 %collective-permute-done.2 = bf16[128,640]{1,0:T(8,128)(2,1)S(1)} collective-permute-done((bf16[128,640]{1,0:T(8,128)(2,1)S(1)}, bf16[128,640]{1,0:T(8,128)(2,1)S(1)}, u32[]{:S(2)}, u32[]{:S(2)}) %collective-permute-start.2) | collective-permute-done | bytes 163872 | tf_op jit(solution)/shard_map/ppermute | solution.py:34
  17.3 4.7 %collective-permute-done.3 = bf16[128,640]{1,0:T(8,128)(2,1)S(1)} collective-permute-done((bf16[128,640]{1,0:T(8,128)(2,1)S(1)}, bf16[128,640]{1,0:T(8,128)(2,1)S(1)}, u32[]{:S(2)}, u32[]{:S(2)}) %collective-permute-start.3) | collective-permute-done | bytes 163872 | tf_op jit(solution)/shard_map/ppermute | solution.py:34
  22.3 4.7 %collective-permute-start.4 = (bf16[4,128,640]{2,1,0:T(8,128)(2,1)S(1)}, bf16[4,128,640]{2,1,0:T(8,128)(2,1)S(1)}, u32[]{:S(2)}, u32[]{:S(2)}) collective-permute-start(bf16[4,128,640]{2,1,0:T(8,128)(2,1)S(1)} %constant_dynamic-slice_fusion.22), channel_id=1, source_target_pairs={{0,64},{64,128},{128,192},{192,256},{256,320},{320,384},{384,448},... | collective-permute-start | bytes 1966088 | tf_op jit(solution)/shard_map/ppermute | solution.py:40
  27.0 1.9 %collective-permute-start.5 = (bf16[4,128,640]{2,1,0:T(8,128)(2,1)S(1)}, bf16[4,128,640]{2,1,0:T(8,128)(2,1)S(1)}, u32[]{:S(2)}, u32[]{:S(2)}) collective-permute-start(bf16[4,128,640]{2,1,0:T(8,128)(2,1)S(1)} %constant_dynamic-slice_fusion.22), channel_id=1, source_target_pairs={{0,448},{64,0},{128,64},{192,128},{256,192},{320,256},{384,320},{4... | collective-permute-start | bytes 1966088 | tf_op jit(solution)/shard_map/ppermute | solution.py:41
  28.9 0.7 fusion.52
  35.1 0.2 fusion.38
  35.4 0.7 fusion.53
  36.0 5.6 %collective-permute-done.4 = bf16[4,128,640]{2,1,0:T(8,128)(2,1)S(1)} collective-permute-done((bf16[4,128,640]{2,1,0:T(8,128)(2,1)S(1)}, bf16[4,128,640]{2,1,0:T(8,128)(2,1)S(1)}, u32[]{:S(2)}, u32[]{:S(2)}) %collective-permute-start.4) | collective-permute-done | bytes 655392 | tf_op jit(solution)/shard_map/ppermute | solution.py:40
  41.6 5.3 %collective-permute-done.5 = bf16[4,128,640]{2,1,0:T(8,128)(2,1)S(1)} collective-permute-done((bf16[4,128,640]{2,1,0:T(8,128)(2,1)S(1)}, bf16[4,128,640]{2,1,0:T(8,128)(2,1)S(1)}, u32[]{:S(2)}, u32[]{:S(2)}) %collective-permute-start.5) | collective-permute-done | bytes 655392 | tf_op jit(solution)/shard_map/ppermute | solution.py:41
  47.0 0.2 pad_maximum_fusion.1
  47.2 2.0 %constant_dynamic-slice_fusion.20 = (bf16[2,128,640]{2,1,0:T(8,128)(2,1)S(1)}, bf16[2,128,640]{2,1,0:T(8,128)(2,1)S(1)}, bf16[2,128,640]{2,1,0:T(8,128)(2,1)S(1)}) fusion(bf16[12,128,640]{2,1,0:T(8,128)(2,1)S(1)} %pad_maximum_fusion.1, s32[]{:T(128)} %bitcast.5, s32[]{:T(128)} %bitcast.9, s32[]{:T(128)} %bitcast.7), kind=kLoop, calls=%fused_computation.94 | loop fusion | bytes 1966092 | tf_op jit(solution)/shard_map/dynamic_slice | solution.py:14
  49.3 0.2 pad_maximum_fusion.2
  49.5 0.2 convert_reduce_fusion
  49.7 1.9 %collective-permute-start.6 = (bf16[896,640]{1,0:T(8,128)(2,1)S(1)}, bf16[896,640]{1,0:T(8,128)(2,1)S(1)}, u32[]{:S(2)}, u32[]{:S(2)}) collective-permute-start(bf16[896,640]{1,0:T(8,128)(2,1)S(1)} %get-tuple-element.14), channel_id=1, source_target_pairs={{0,1},{1,0},{2,3},{3,2},{4,5},{5,4},{6,7},{7,6},{8,9},{9,8},{10,11... | collective-permute-start | bytes 3440648 | tf_op jit(solution)/shard_map/ppermute | solution.py:52
  51.6 0.5 fusion.1
  52.1 22.0 %all-gather.1 = f32[16,2,896]{2,1,0:T(2,128)S(1)} all-gather(f32[1,2,896]{2,1,0:T(2,128)S(1)} %maximum_bitcast_fusion), channel_id=2, replica_groups=mesh['ly'=8,'lx'=4,'tz'=8,'tc'=2] {'tz','tc'}, dimensions={0}, use_global_device_ids=true | all-gather | bytes 121856 | tf_op jit(solution)/shard_map/all_gather | solution.py:56
  74.1 0.1 slice_reduce_fusion.1
  74.3 1.0 fusion.5
  75.3 1.2 select_convert_fusion
  76.5 0.1 slice.91
  76.7 0.2 slice.92
  76.9 0.7 constant_dynamic-slice_fusion
  77.6 0.7 constant_dynamic-slice_fusion.1
  78.4 1.8 %convolution_dynamic-update-slice_fusion.8 = f32[64,6912]{1,0:T(8,128)} fusion(bf16[64,1024]{1,0:T(8,128)(2,1)S(1)} %get-tuple-element.33, bf16[64,1152]{1,0:T(8,128)(2,1)S(1)} %get-tuple-element.24, bf16[768,1024]{1,0:T(8,128)(2,1)S(1)} %slice.92, bf16[768,1152]{1,0:T(8,128)(2,1)S(1)} %slice.91), kind=kOutput, calls=%fused_computation.19 | convolution fusion | flops 221151232 | bytes 3817472 | tf_op jit(solution)/shard_map/dot_general | solution.py:99
  80.2 1.8 %convolution_dynamic-update-slice_fusion.7 = f32[64,6912]{1,0:T(8,128)} fusion(f32[64,6912]{1,0:T(8,128)} %convolution_dynamic-update-slice_fusion.8, bf16[64,1024]{1,0:T(8,128)(2,1)S(1)} %get-tuple-element.32, bf16[64,1152]{1,0:T(8,128)(2,1)S(1)} %get-tuple-element.23, bf16[768,1024]{1,0:T(8,128)(2,1)S(1)} %slice.92, bf16[768,1152]{1,0:T(8,128)(2,1)S(1)} %slice.91), kind=kOutput, calls=%fused_computation.18 | convolution fusion | flops 221151232 | bytes 3817472 | tf_op jit(solution)/shard_map/dot_general | solution.py:99
  81.9 1.8 %convolution_dynamic-update-slice_fusion.6 = f32[64,6912]{1,0:T(8,128)} fusion(f32[64,6912]{1,0:T(8,128)} %convolution_dynamic-update-slice_fusion.7, bf16[64,1024]{1,0:T(8,128)(2,1)S(1)} %get-tuple-element.31, bf16[64,1152]{1,0:T(8,128)(2,1)S(1)} %get-tuple-element.22, bf16[768,1024]{1,0:T(8,128)(2,1)S(1)} %slice.92, bf16[768,1152]{1,0:T(8,128)(2,1)S(1)} %slice.91), kind=kOutput, calls=%fused_computation.17 | convolution fusion | flops 221151232 | bytes 3817472 | tf_op jit(solution)/shard_map/dot_general | solution.py:99
  83.7 1.8 %convolution_dynamic-update-slice_fusion.5 = f32[64,6912]{1,0:T(8,128)} fusion(f32[64,6912]{1,0:T(8,128)} %convolution_dynamic-update-slice_fusion.6, bf16[64,1024]{1,0:T(8,128)(2,1)S(1)} %get-tuple-element.30, bf16[64,1152]{1,0:T(8,128)(2,1)S(1)} %get-tuple-element.21, bf16[768,1024]{1,0:T(8,128)(2,1)S(1)} %slice.92, bf16[768,1152]{1,0:T(8,128)(2,1)S(1)} %slice.91), kind=kOutput, calls=%fused_computation.16 | convolution fusion | flops 221151232 | bytes 3817472 | tf_op jit(solution)/shard_map/dot_general | solution.py:99
  85.5 1.8 %convolution_dynamic-update-slice_fusion.4 = f32[64,6912]{1,0:T(8,128)} fusion(f32[64,6912]{1,0:T(8,128)} %convolution_dynamic-update-slice_fusion.5, bf16[64,1024]{1,0:T(8,128)(2,1)S(1)} %get-tuple-element.29, bf16[64,1152]{1,0:T(8,128)(2,1)S(1)} %get-tuple-element.20, bf16[768,1024]{1,0:T(8,128)(2,1)S(1)} %slice.92, bf16[768,1152]{1,0:T(8,128)(2,1)S(1)} %slice.91), kind=kOutput, calls=%fused_computation.15 | convolution fusion | flops 221151232 | bytes 3817472 | tf_op jit(solution)/shard_map/dot_general | solution.py:99
  87.3 1.8 %convolution_dynamic-update-slice_fusion.3 = f32[64,6912]{1,0:T(8,128)} fusion(f32[64,6912]{1,0:T(8,128)} %convolution_dynamic-update-slice_fusion.4, bf16[64,1024]{1,0:T(8,128)(2,1)S(1)} %get-tuple-element.28, bf16[64,1152]{1,0:T(8,128)(2,1)S(1)} %get-tuple-element.19, bf16[768,1024]{1,0:T(8,128)(2,1)S(1)} %slice.92, bf16[768,1152]{1,0:T(8,128)(2,1)S(1)} %slice.91), kind=kOutput, calls=%fused_computation.14 | convolution fusion | flops 221151232 | bytes 3817472 | tf_op jit(solution)/shard_map/dot_general | solution.py:99
  89.1 1.8 %convolution_dynamic-update-slice_fusion.2 = f32[64,6912]{1,0:T(8,128)} fusion(f32[64,6912]{1,0:T(8,128)} %convolution_dynamic-update-slice_fusion.3, bf16[64,1024]{1,0:T(8,128)(2,1)S(1)} %get-tuple-element.27, bf16[64,1152]{1,0:T(8,128)(2,1)S(1)} %get-tuple-element.18, bf16[768,1024]{1,0:T(8,128)(2,1)S(1)} %slice.92, bf16[768,1152]{1,0:T(8,128)(2,1)S(1)} %slice.91), kind=kOutput, calls=%fused_computation.13 | convolution fusion | flops 221151232 | bytes 3817472 | tf_op jit(solution)/shard_map/dot_general | solution.py:99
  90.9 1.8 %convolution_dynamic-update-slice_fusion.1 = f32[64,6912]{1,0:T(8,128)} fusion(f32[64,6912]{1,0:T(8,128)} %convolution_dynamic-update-slice_fusion.2, bf16[64,1024]{1,0:T(8,128)(2,1)S(1)} %get-tuple-element.26, bf16[64,1152]{1,0:T(8,128)(2,1)S(1)} %get-tuple-element.17, bf16[768,1024]{1,0:T(8,128)(2,1)S(1)} %slice.92, bf16[768,1152]{1,0:T(8,128)(2,1)S(1)} %slice.91), kind=kOutput, calls=%fused_computation.12 | convolution fusion | flops 221151232 | bytes 3817472 | tf_op jit(solution)/shard_map/dot_general | solution.py:99
  92.6 1.8 %convolution_dynamic-update-slice_fusion = f32[64,6912]{1,0:T(8,128)} fusion(f32[64,6912]{1,0:T(8,128)} %convolution_dynamic-update-slice_fusion.1, bf16[64,1024]{1,0:T(8,128)(2,1)S(1)} %get-tuple-element.25, bf16[64,1152]{1,0:T(8,128)(2,1)S(1)} %get-tuple-element.16, bf16[768,1024]{1,0:T(8,128)(2,1)S(1)} %slice.92, bf16[768,1152]{1,0:T(8,128)(2,1)S(1)} %slice.91), kind=kOutput, calls=%fused_computation.11 | convolution fusion | flops 221151232 | bytes 3817472 | tf_op jit(solution)/shard_map/dot_general | solution.py:99
  94.5 5.0 %all-to-all-start = ((f32[8,8,6912]{2,1,0:T(8,128)}), f32[8,8,6912]{2,1,0:T(8,128)S(1)}, u32[]{:S(2)}, u32[]{:S(2)}) async-start(f32[8,8,6912]{2,1,0:T(8,128)} %bitcast.27), calls=%async_computation | async-start | bytes 3538944 | tf_op jit(solution)/shard_map/all_to_all | solution.py:105
  99.4 0.6 dynamic_slice.81
  100.7 0.7 iota_compare_fusion.1
  101.4 42.8 %all-to-all-done = f32[8,8,6912]{2,1,0:T(8,128)S(1)} async-done(((f32[8,8,6912]{2,1,0:T(8,128)}), f32[8,8,6912]{2,1,0:T(8,128)S(1)}, u32[]{:S(2)}, u32[]{:S(2)}) %all-to-all-start) | async-done | bytes 1769504 | tf_op jit(solution)/shard_map/all_to_all | solution.py:105
  144.1 0.1 reduce_sum.68
  144.2 0.1 reshape.96
  144.4 0.3 multiply_reduce_fusion
  144.6 0.1 divide_bitcast_fusion
  144.8 0.7 copy.6
  (34 shorter events, 0.5 us)
Async XLA Ops:
  0.8 3.1 %collective-permute-start = (bf16[128,128]{1,0:T(8,128)(2,1)S(1)}, bf16[128,128]{1,0:T(8,128)(2,1)S(1)}, u32[]{:S(2)}, u32[]{:S(2)}) collective-permute-start(bf16[128,128]{1,0:T(8,128)(2,1)S(1)} %slice.64), channel_id=1, source_target_pairs={{1,0},{2,1},{3,2},{4,3},{5,4},{6,5},{7,6},{8,7},{9,8},{10,9},{11,1... | collective-permute-start | bytes 98312 | tf_op jit(solution)/shard_map/ppermute | solution.py:25
  3.9 10.2 %collective-permute-start.1 = (bf16[128,640]{1,0:T(8,128)(2,1)S(1)}, bf16[128,640]{1,0:T(8,128)(2,1)S(1)}, u32[]{:S(2)}, u32[]{:S(2)}) collective-permute-start(bf16[128,640]{1,0:T(8,128)(2,1)S(1)} %constant_dynamic-update-slice_fusion), channel_id=1, source_target_pairs={{0,48},{16,0},{32,16},{48,32},{1,49},{17,1},{33,17},{49,33},{2,50}... | collective-permute-start | bytes 491528 | tf_op jit(solution)/shard_map/ppermute | solution.py:34
  8.5 8.8 %collective-permute-start.2 = (bf16[128,640]{1,0:T(8,128)(2,1)S(1)}, bf16[128,640]{1,0:T(8,128)(2,1)S(1)}, u32[]{:S(2)}, u32[]{:S(2)}) collective-permute-start(bf16[128,640]{1,0:T(8,128)(2,1)S(1)} %constant_dynamic-update-slice_fusion), channel_id=1, source_target_pairs={{0,32},{16,48},{32,0},{48,16},{1,33},{17,49},{33,1},{49,17},{2,34}... | collective-permute-start | bytes 491528 | tf_op jit(solution)/shard_map/ppermute | solution.py:34
  11.3 10.8 %collective-permute-start.3 = (bf16[128,640]{1,0:T(8,128)(2,1)S(1)}, bf16[128,640]{1,0:T(8,128)(2,1)S(1)}, u32[]{:S(2)}, u32[]{:S(2)}) collective-permute-start(bf16[128,640]{1,0:T(8,128)(2,1)S(1)} %constant_dynamic-update-slice_fusion), channel_id=1, source_target_pairs={{0,16},{16,32},{32,48},{48,0},{1,17},{17,33},{33,49},{49,1},{2,18}... | collective-permute-start | bytes 491528 | tf_op jit(solution)/shard_map/ppermute | solution.py:34
  14.1 14.8 %copy-start = (s32[9]{0:T(128)S(1)}, s32[9]{0:T(128)}, u32[]{:S(2)}) copy-start(s32[9]{0:T(128)} %param.7) | copy-start | bytes 112
  14.1 21.0 %copy-start.1 = (s32[16,3]{0,1:T(4,128)S(1)}, s32[16,3]{0,1:T(4,128)}, u32[]{:S(2)}) copy-start(s32[16,3]{0,1:T(4,128)} %param.5) | copy-start | bytes 580
  22.3 19.4 %collective-permute-start.4 = (bf16[4,128,640]{2,1,0:T(8,128)(2,1)S(1)}, bf16[4,128,640]{2,1,0:T(8,128)(2,1)S(1)}, u32[]{:S(2)}, u32[]{:S(2)}) collective-permute-start(bf16[4,128,640]{2,1,0:T(8,128)(2,1)S(1)} %constant_dynamic-slice_fusion.22), channel_id=1, source_target_pairs={{0,64},{64,128},{128,192},{192,256},{256,320},{320,384},{384,448},... | collective-permute-start | bytes 1966088 | tf_op jit(solution)/shard_map/ppermute | solution.py:40
  27.0 20.0 %collective-permute-start.5 = (bf16[4,128,640]{2,1,0:T(8,128)(2,1)S(1)}, bf16[4,128,640]{2,1,0:T(8,128)(2,1)S(1)}, u32[]{:S(2)}, u32[]{:S(2)}) collective-permute-start(bf16[4,128,640]{2,1,0:T(8,128)(2,1)S(1)} %constant_dynamic-slice_fusion.22), channel_id=1, source_target_pairs={{0,448},{64,0},{128,64},{192,128},{256,192},{320,256},{384,320},{4... | collective-permute-start | bytes 1966088 | tf_op jit(solution)/shard_map/ppermute | solution.py:41
  49.7 24.6 %collective-permute-start.6 = (bf16[896,640]{1,0:T(8,128)(2,1)S(1)}, bf16[896,640]{1,0:T(8,128)(2,1)S(1)}, u32[]{:S(2)}, u32[]{:S(2)}) collective-permute-start(bf16[896,640]{1,0:T(8,128)(2,1)S(1)} %get-tuple-element.14), channel_id=1, source_target_pairs={{0,1},{1,0},{2,3},{3,2},{4,5},{5,4},{6,7},{7,6},{8,9},{9,8},{10,11... | collective-permute-start | bytes 3440648 | tf_op jit(solution)/shard_map/ppermute | solution.py:52
  94.4 5.0 %copy-start.2 = (s32[16]{0:T(128)S(1)}, s32[16]{0:T(128)}, u32[]{:S(2)}) copy-start(s32[16]{0:T(128)} %param.6) | copy-start | bytes 196
  94.5 49.7 %all-to-all-start = ((f32[8,8,6912]{2,1,0:T(8,128)}), f32[8,8,6912]{2,1,0:T(8,128)S(1)}, u32[]{:S(2)}, u32[]{:S(2)}) async-start(f32[8,8,6912]{2,1,0:T(8,128)} %bitcast.27), calls=%async_computation | async-start | bytes 3538944 | tf_op jit(solution)/shard_map/all_to_all | solution.py:105

commit v15 on v11

--- a/solution.py
+++ b/solution.py
@@ -48,7 +48,12 @@
     values = raw[:, :days_dev].astype(jnp.float32)
     shard_mean = jnp.mean(values, axis=1)
     shard_square = jnp.sum(jnp.square(values - shard_mean[:, None]), axis=1)
-    stats = lax.all_gather(jnp.stack([shard_mean, shard_square], 0), TIME)
+    along = lax.all_gather(jnp.stack([shard_mean, shard_square], 0), "tz")
+    across = lax.ppermute(along, "tc", [(0, 1), (1, 0)])
+    ordered = jnp.stack([along, across], 0)
+    stats = jnp.concatenate(
+        [dslice(ordered, core, 1, 0)[0], dslice(ordered, 1 - core, 1, 0)[0]], 0
+    )
     means, squares = stats[:, 0], stats[:, 1]
     point_mean = jnp.mean(means, axis=0)
     point_m2 = jnp.sum(squares, axis=0) + days_dev * jnp.sum(

time: 141 us -> 153 us (1.085)
  blocking collectives: 35.8 us -> 45.5 us
    all_gather x1, blocking collectives: 21.5 us -> 31.2 us  [local(): along = lax.all_gather(jnp.stack([shard_mean, shard_square], 0), 'tz')]
    ppermute x0 -> x1, starting transfers between devices: none -> 1.91 us  [local(): across = lax.ppermute(along, 'tc', [(0, 1), (1, 0)])]
  transfers between devices with their start and end apart: 5 -> 6, of which waited for: 4 -> 5; matrix products, arithmetic and copies ran while one was open for 4% -> 4% of each run, Pallas kernels for 0% -> 0%
where the time goes in v15:
time: 153 us; the launch traced here: 152 us
  waiting for transfers between devices  53.5 us (35%)
  blocking collectives  45.5 us (30%)
  matrix products  16.1 us (11%)
  starting transfers between devices  15.8 us (10%)
  local copies, waits for them, and re-layouts  9.39 us (6%)
  between operations  6.47 us (4%)
  other arithmetic  5.59 us (4%)
    all_to_all x1, waiting for transfers between devices, local(): received = lax.all_to_all(product, 'tz', 0, 0, tiled=True)  42.6 us
    all_gather x1, blocking collectives, local(): along = lax.all_gather(jnp.stack([shard_mean, shard_square], 0), 'tz')  31.2 us
    dot_general x9, matrix products, local(): lax.dot_general(left, right, (((1,), (1,)), ((), ())), preferred_element_...  16.1 us
    all_gather x1, blocking collectives, local(): row = lax.all_gather(extended, 'lx')  14.3 us
    ppermute x1, waiting for transfers between devices, local(): lax.ppermute(row, 'ly', [(i, (i - 1) % rows_size) for i in range(rows_siz...  5.33 us
    ppermute x1, starting transfers between devices, local(): lax.ppermute(row, 'ly', [(i, (i + 1) % rows_size) for i in range(rows_siz...  4.68 us
    all_to_all x1, starting transfers between devices, local(): received = lax.all_to_all(product, 'tz', 0, 0, tiled=True)  4.07 us
    dynamic_slice x4, local copies, waits for them, and re-layouts, dslice(): lax.dynamic_slice_in_dim(value, start, size, axis, allow_negative_indices...  4.05 us
  transfers between devices with their start and end apart: 6, of which 5 were waited for; matrix products, arithmetic and copies ran while one was open for 4% of the time, Pallas kernels for 0%

profile of v15, /device:TPU:24, one launch (start us, length us, event | category | flops | bytes accessed | tf_op | source)
XLA Modules:
  0.0 152.3 jit_solution(14136033504129895360)
XLA Ops:
  0.0 0.8 slice.64
  0.8 1.3 collective-permute-start
  2.0 0.9 constant_dynamic-update-slice_fusion.1
  3.0 0.9 collective-permute-done
  3.9 14.3 %all-gather = bf16[512,640]{1,0:T(8,128)(2,1)S(1)} all-gather(bf16[128,640]{1,0:T(8,128)(2,1)S(1)} %constant_dynamic-update-slice_fusion), channel_id=2, replica_groups=mesh['ly'=8,'lx'=4,'tz'=8,'tc'=2] {'lx'}, dimensions={0}, use_global_device_ids=true | all-gather | bytes 819200 | tf_op jit(solution)/shard_map/all_gather | solution.py:33
  18.1 4.7 %collective-permute-start.1 = (bf16[4,128,640]{2,1,0:T(8,128)(2,1)S(1)}, bf16[4,128,640]{2,1,0:T(8,128)(2,1)S(1)}, u32[]{:S(2)}, u32[]{:S(2)}) collective-permute-start(bf16[4,128,640]{2,1,0:T(8,128)(2,1)S(1)} %bitcast.45), channel_id=1, source_target_pairs={{0,64},{64,128},{128,192},{192,256},{256,320},{320,384},{384,448},... | collective-permute-start | bytes 1966088 | tf_op jit(solution)/shard_map/ppermute | solution.py:35
  22.8 1.9 %collective-permute-start.2 = (bf16[4,128,640]{2,1,0:T(8,128)(2,1)S(1)}, bf16[4,128,640]{2,1,0:T(8,128)(2,1)S(1)}, u32[]{:S(2)}, u32[]{:S(2)}) collective-permute-start(bf16[4,128,640]{2,1,0:T(8,128)(2,1)S(1)} %bitcast.46), channel_id=1, source_target_pairs={{0,448},{64,0},{128,64},{192,128},{256,192},{320,256},{384,320},{4... | collective-permute-start | bytes 1966088 | tf_op jit(solution)/shard_map/ppermute | solution.py:36
  24.8 1.7 %fusion.60 = (s32[1]{0:T(128)}, s32[1]{0:T(128)}, s32[1]{0:T(128)}, s32[1]{0:T(128)}, s32[1]{0:T(128)}, /*index=5*/s32[1]{0:T(128)}, s32[1]{0:T(128)}, s32[1]{0:T(128)}, s32[1]{0:T(128)}) fusion(s32[9]{0:T(128)} %param.7), kind=kLoop, calls=%fused_computation.125 | loop fusion | bytes 72 | tf_op jit(solution)/shard_map/slice | solution.py:90
  32.0 0.9 fusion.44
  32.9 0.7 fusion.61
  33.5 3.6 %collective-permute-done.1 = bf16[4,128,640]{2,1,0:T(8,128)(2,1)S(1)} collective-permute-done((bf16[4,128,640]{2,1,0:T(8,128)(2,1)S(1)}, bf16[4,128,640]{2,1,0:T(8,128)(2,1)S(1)}, u32[]{:S(2)}, u32[]{:S(2)}) %collective-permute-start.1) | collective-permute-done | bytes 655392 | tf_op jit(solution)/shard_map/ppermute | solution.py:35
  37.1 5.3 %collective-permute-done.2 = bf16[4,128,640]{2,1,0:T(8,128)(2,1)S(1)} collective-permute-done((bf16[4,128,640]{2,1,0:T(8,128)(2,1)S(1)}, bf16[4,128,640]{2,1,0:T(8,128)(2,1)S(1)}, u32[]{:S(2)}, u32[]{:S(2)}) %collective-permute-start.2) | collective-permute-done | bytes 655392 | tf_op jit(solution)/shard_map/ppermute | solution.py:36
  42.4 0.2 pad_maximum_fusion.1
  42.7 2.0 %constant_dynamic-slice_fusion.20 = (bf16[2,128,640]{2,1,0:T(8,128)(2,1)S(1)}, bf16[2,128,640]{2,1,0:T(8,128)(2,1)S(1)}, bf16[2,128,640]{2,1,0:T(8,128)(2,1)S(1)}) fusion(bf16[12,128,640]{2,1,0:T(8,128)(2,1)S(1)} %pad_maximum_fusion.1, s32[]{:T(128)} %bitcast.2, s32[]{:T(128)} %bitcast.6, s32[]{:T(128)} %bitcast.4), kind=kLoop, calls=%fused_computation.97 | loop fusion | bytes 1966092 | tf_op jit(solution)/shard_map/dynamic_slice | solution.py:14
  44.7 0.2 pad_maximum_fusion.2
  44.9 0.2 convert_reduce_fusion
  45.1 1.9 %collective-permute-start.3 = (bf16[896,640]{1,0:T(8,128)(2,1)S(1)}, bf16[896,640]{1,0:T(8,128)(2,1)S(1)}, u32[]{:S(2)}, u32[]{:S(2)}) collective-permute-start(bf16[896,640]{1,0:T(8,128)(2,1)S(1)} %get-tuple-element.14), channel_id=1, source_target_pairs={{0,1},{1,0},{2,3},{3,2},{4,5},{5,4},{6,7},{7,6},{8,9},{9,8},{10,11... | collective-permute-start | bytes 3440648 | tf_op jit(solution)/shard_map/ppermute | solution.py:47
  47.1 0.5 fusion.1
  47.6 31.2 %all-gather.2 = f32[8,2,896]{2,1,0:T(2,128)S(1)} all-gather(f32[1,2,896]{2,1,0:T(2,128)S(1)} %maximum_bitcast_fusion), channel_id=3, replica_groups=mesh['ly'=8,'lx'=4,'tz'=8,'tc'=2] {'tz'}, dimensions={0}, use_global_device_ids=true | all-gather | bytes 64512 | tf_op jit(solution)/shard_map/all_gather | solution.py:51
  78.7 1.9 %collective-permute-start.4 = (f32[8,2,896]{2,1,0:T(2,128)S(1)}, f32[8,2,896]{2,1,0:T(2,128)S(1)}, u32[]{:S(2)}, u32[]{:S(2)}) collective-permute-start(f32[8,2,896]{2,1,0:T(2,128)S(1)} %all-gather.2), channel_id=1, source_target_pairs={{0,1},{1,0},{2,3},{3,2},{4,5},{5,4},{6,7},{7,6},{8,9},{9,8},{10,11... | collective-permute-start | bytes 172040 | tf_op jit(solution)/shard_map/ppermute | solution.py:52
  80.7 1.2 collective-permute-done.4
  81.9 0.1 fusion.37
  82.0 0.1 fusion.58
  82.2 1.0 fusion.5
  83.1 0.1 slice.85
  83.2 1.2 select_convert_fusion
  84.4 0.1 slice.91
  84.6 0.2 slice.92
  84.8 0.7 constant_dynamic-slice_fusion
  85.5 0.7 constant_dynamic-slice_fusion.1
  86.3 1.8 %convolution_dynamic-update-slice_fusion.8 = f32[64,6912]{1,0:T(8,128)} fusion(bf16[64,1024]{1,0:T(8,128)(2,1)S(1)} %get-tuple-element.33, bf16[64,1152]{1,0:T(8,128)(2,1)S(1)} %get-tuple-element.24, bf16[768,1024]{1,0:T(8,128)(2,1)S(1)} %slice.92, bf16[768,1152]{1,0:T(8,128)(2,1)S(1)} %slice.91), kind=kOutput, calls=%fused_computation.19 | convolution fusion | flops 221151232 | bytes 3817472 | tf_op jit(solution)/shard_map/dot_general | solution.py:99
  88.1 1.8 %convolution_dynamic-update-slice_fusion.7 = f32[64,6912]{1,0:T(8,128)} fusion(f32[64,6912]{1,0:T(8,128)} %convolution_dynamic-update-slice_fusion.8, bf16[64,1024]{1,0:T(8,128)(2,1)S(1)} %get-tuple-element.32, bf16[64,1152]{1,0:T(8,128)(2,1)S(1)} %get-tuple-element.23, bf16[768,1024]{1,0:T(8,128)(2,1)S(1)} %slice.92, bf16[768,1152]{1,0:T(8,128)(2,1)S(1)} %slice.91), kind=kOutput, calls=%fused_computation.18 | convolution fusion | flops 221151232 | bytes 3817472 | tf_op jit(solution)/shard_map/dot_general | solution.py:99
  89.8 1.8 %convolution_dynamic-update-slice_fusion.6 = f32[64,6912]{1,0:T(8,128)} fusion(f32[64,6912]{1,0:T(8,128)} %convolution_dynamic-update-slice_fusion.7, bf16[64,1024]{1,0:T(8,128)(2,1)S(1)} %get-tuple-element.31, bf16[64,1152]{1,0:T(8,128)(2,1)S(1)} %get-tuple-element.22, bf16[768,1024]{1,0:T(8,128)(2,1)S(1)} %slice.92, bf16[768,1152]{1,0:T(8,128)(2,1)S(1)} %slice.91), kind=kOutput, calls=%fused_computation.17 | convolution fusion | flops 221151232 | bytes 3817472 | tf_op jit(solution)/shard_map/dot_general | solution.py:99
  91.6 1.8 %convolution_dynamic-update-slice_fusion.5 = f32[64,6912]{1,0:T(8,128)} fusion(f32[64,6912]{1,0:T(8,128)} %convolution_dynamic-update-slice_fusion.6, bf16[64,1024]{1,0:T(8,128)(2,1)S(1)} %get-tuple-element.30, bf16[64,1152]{1,0:T(8,128)(2,1)S(1)} %get-tuple-element.21, bf16[768,1024]{1,0:T(8,128)(2,1)S(1)} %slice.92, bf16[768,1152]{1,0:T(8,128)(2,1)S(1)} %slice.91), kind=kOutput, calls=%fused_computation.16 | convolution fusion | flops 221151232 | bytes 3817472 | tf_op jit(solution)/shard_map/dot_general | solution.py:99
  93.4 1.8 %convolution_dynamic-update-slice_fusion.4 = f32[64,6912]{1,0:T(8,128)} fusion(f32[64,6912]{1,0:T(8,128)} %convolution_dynamic-update-slice_fusion.5, bf16[64,1024]{1,0:T(8,128)(2,1)S(1)} %get-tuple-element.29, bf16[64,1152]{1,0:T(8,128)(2,1)S(1)} %get-tuple-element.20, bf16[768,1024]{1,0:T(8,128)(2,1)S(1)} %slice.92, bf16[768,1152]{1,0:T(8,128)(2,1)S(1)} %slice.91), kind=kOutput, calls=%fused_computation.15 | convolution fusion | flops 221151232 | bytes 3817472 | tf_op jit(solution)/shard_map/dot_general | solution.py:99
  95.2 1.8 %convolution_dynamic-update-slice_fusion.3 = f32[64,6912]{1,0:T(8,128)} fusion(f32[64,6912]{1,0:T(8,128)} %convolution_dynamic-update-slice_fusion.4, bf16[64,1024]{1,0:T(8,128)(2,1)S(1)} %get-tuple-element.28, bf16[64,1152]{1,0:T(8,128)(2,1)S(1)} %get-tuple-element.19, bf16[768,1024]{1,0:T(8,128)(2,1)S(1)} %slice.92, bf16[768,1152]{1,0:T(8,128)(2,1)S(1)} %slice.91), kind=kOutput, calls=%fused_computation.14 | convolution fusion | flops 221151232 | bytes 3817472 | tf_op jit(solution)/shard_map/dot_general | solution.py:99
  97.0 1.8 %convolution_dynamic-update-slice_fusion.2 = f32[64,6912]{1,0:T(8,128)} fusion(f32[64,6912]{1,0:T(8,128)} %convolution_dynamic-update-slice_fusion.3, bf16[64,1024]{1,0:T(8,128)(2,1)S(1)} %get-tuple-element.27, bf16[64,1152]{1,0:T(8,128)(2,1)S(1)} %get-tuple-element.18, bf16[768,1024]{1,0:T(8,128)(2,1)S(1)} %slice.92, bf16[768,1152]{1,0:T(8,128)(2,1)S(1)} %slice.91), kind=kOutput, calls=%fused_computation.13 | convolution fusion | flops 221151232 | bytes 3817472 | tf_op jit(solution)/shard_map/dot_general | solution.py:99
  98.7 1.8 %convolution_dynamic-update-slice_fusion.1 = f32[64,6912]{1,0:T(8,128)} fusion(f32[64,6912]{1,0:T(8,128)} %convolution_dynamic-update-slice_fusion.2, bf16[64,1024]{1,0:T(8,128)(2,1)S(1)} %get-tuple-element.26, bf16[64,1152]{1,0:T(8,128)(2,1)S(1)} %get-tuple-element.17, bf16[768,1024]{1,0:T(8,128)(2,1)S(1)} %slice.92, bf16[768,1152]{1,0:T(8,128)(2,1)S(1)} %slice.91), kind=kOutput, calls=%fused_computation.12 | convolution fusion | flops 221151232 | bytes 3817472 | tf_op jit(solution)/shard_map/dot_general | solution.py:99
  100.5 1.8 %convolution_dynamic-update-slice_fusion = f32[64,6912]{1,0:T(8,128)} fusion(f32[64,6912]{1,0:T(8,128)} %convolution_dynamic-update-slice_fusion.1, bf16[64,1024]{1,0:T(8,128)(2,1)S(1)} %get-tuple-element.25, bf16[64,1152]{1,0:T(8,128)(2,1)S(1)} %get-tuple-element.16, bf16[768,1024]{1,0:T(8,128)(2,1)S(1)} %slice.92, bf16[768,1152]{1,0:T(8,128)(2,1)S(1)} %slice.91), kind=kOutput, calls=%fused_computation.11 | convolution fusion | flops 221151232 | bytes 3817472 | tf_op jit(solution)/shard_map/dot_general | solution.py:99
  102.3 4.1 %all-to-all-start = ((f32[8,8,6912]{2,1,0:T(8,128)}), f32[8,8,6912]{2,1,0:T(8,128)S(1)}, u32[]{:S(2)}, u32[]{:S(2)}) async-start(f32[8,8,6912]{2,1,0:T(8,128)} %bitcast.28), calls=%async_computation | async-start | bytes 3538944 | tf_op jit(solution)/shard_map/all_to_all | solution.py:105
  106.4 0.6 dynamic_slice.84
  107.7 0.7 iota_compare_fusion.1
  108.3 42.6 %all-to-all-done = f32[8,8,6912]{2,1,0:T(8,128)S(1)} async-done(((f32[8,8,6912]{2,1,0:T(8,128)}), f32[8,8,6912]{2,1,0:T(8,128)S(1)}, u32[]{:S(2)}, u32[]{:S(2)}) %all-to-all-start) | async-done | bytes 1769504 | tf_op jit(solution)/shard_map/all_to_all | solution.py:105
  150.9 0.1 reduce_sum.68
  151.0 0.1 reshape.96
  151.2 0.3 multiply_reduce_fusion
  151.4 0.1 divide_bitcast_fusion
  151.6 0.7 copy.6
  (21 shorter events, 0.2 us)
Async XLA Ops:
  0.8 3.1 %collective-permute-start = (bf16[128,128]{1,0:T(8,128)(2,1)S(1)}, bf16[128,128]{1,0:T(8,128)(2,1)S(1)}, u32[]{:S(2)}, u32[]{:S(2)}) collective-permute-start(bf16[128,128]{1,0:T(8,128)(2,1)S(1)} %slice.64), channel_id=1, source_target_pairs={{1,0},{2,1},{3,2},{4,3},{5,4},{6,5},{7,6},{8,7},{9,8},{10,9},{11,1... | collective-permute-start | bytes 98312 | tf_op jit(solution)/shard_map/ppermute | solution.py:25
  18.1 18.9 %collective-permute-start.1 = (bf16[4,128,640]{2,1,0:T(8,128)(2,1)S(1)}, bf16[4,128,640]{2,1,0:T(8,128)(2,1)S(1)}, u32[]{:S(2)}, u32[]{:S(2)}) collective-permute-start(bf16[4,128,640]{2,1,0:T(8,128)(2,1)S(1)} %bitcast.45), channel_id=1, source_target_pairs={{0,64},{64,128},{128,192},{192,256},{256,320},{320,384},{384,448},... | collective-permute-start | bytes 1966088 | tf_op jit(solution)/shard_map/ppermute | solution.py:35
  22.8 19.6 %collective-permute-start.2 = (bf16[4,128,640]{2,1,0:T(8,128)(2,1)S(1)}, bf16[4,128,640]{2,1,0:T(8,128)(2,1)S(1)}, u32[]{:S(2)}, u32[]{:S(2)}) collective-permute-start(bf16[4,128,640]{2,1,0:T(8,128)(2,1)S(1)} %bitcast.46), channel_id=1, source_target_pairs={{0,448},{64,0},{128,64},{192,128},{256,192},{320,256},{384,320},{4... | collective-permute-start | bytes 1966088 | tf_op jit(solution)/shard_map/ppermute | solution.py:36
  45.1 37.0 %collective-permute-start.3 = (bf16[896,640]{1,0:T(8,128)(2,1)S(1)}, bf16[896,640]{1,0:T(8,128)(2,1)S(1)}, u32[]{:S(2)}, u32[]{:S(2)}) collective-permute-start(bf16[896,640]{1,0:T(8,128)(2,1)S(1)} %get-tuple-element.14), channel_id=1, source_target_pairs={{0,1},{1,0},{2,3},{3,2},{4,5},{5,4},{6,7},{7,6},{8,9},{9,8},{10,11... | collective-permute-start | bytes 3440648 | tf_op jit(solution)/shard_map/ppermute | solution.py:47
  78.7 3.1 %collective-permute-start.4 = (f32[8,2,896]{2,1,0:T(2,128)S(1)}, f32[8,2,896]{2,1,0:T(2,128)S(1)}, u32[]{:S(2)}, u32[]{:S(2)}) collective-permute-start(f32[8,2,896]{2,1,0:T(2,128)S(1)} %all-gather.2), channel_id=1, source_target_pairs={{0,1},{1,0},{2,3},{3,2},{4,5},{5,4},{6,7},{7,6},{8,9},{9,8},{10,11... | collective-permute-start | bytes 172040 | tf_op jit(solution)/shard_map/ppermute | solution.py:52
  102.3 4.1 %copy-start.1 = (s32[16]{0:T(128)S(1)}, s32[16]{0:T(128)}, u32[]{:S(2)}) copy-start(s32[16]{0:T(128)} %param.6) | copy-start | bytes 196
  102.3 6.0 %copy-start = (s32[9]{0:T(128)S(1)}, s32[9]{0:T(128)}, u32[]{:S(2)}) copy-start(s32[9]{0:T(128)} %param.7) | copy-start | bytes 112
  102.3 48.6 %all-to-all-start = ((f32[8,8,6912]{2,1,0:T(8,128)}), f32[8,8,6912]{2,1,0:T(8,128)S(1)}, u32[]{:S(2)}, u32[]{:S(2)}) async-start(f32[8,8,6912]{2,1,0:T(8,128)} %bitcast.28), calls=%async_computation | async-start | bytes 3538944 | tf_op jit(solution)/shard_map/all_to_all | solution.py:105

commit v16 on v11

--- a/solution.py
+++ b/solution.py
@@ -82,7 +82,7 @@
     right = jnp.concatenate([columns, columns[:, :span]], 1)
     pieces = []
     for lag_index in range(NLAG):
-        lag_days = lax.min(lag_set[lag_index], LMAX)
+        lag_days = lag_set[lag_index]
         left = jnp.concatenate(
             [
                 dslice(padded, LMAX - lag_days, span + LMAX, 1),

time: 141 us -> 147 us (1.043)
  local copies, waits for them, and re-layouts: 9.39 us -> 14.9 us
    dynamic_slice x4, local copies, waits for them, and re-layouts: 4.05 us -> 9.58 us  [dslice(): lax.dynamic_slice_in_dim(value, start, size, axis, allow_negative_indices...]
where the time goes in v16:
time: 147 us; the launch traced here: 146 us
  waiting for transfers between devices  52.5 us (36%)
  blocking collectives  35.8 us (24%)
  matrix products  16.1 us (11%)
  local copies, waits for them, and re-layouts  14.9 us (10%)
  starting transfers between devices  14.8 us (10%)
  between operations  6.49 us (4%)
  other arithmetic  5.49 us (4%)
    all_to_all x1, waiting for transfers between devices, local(): received = lax.all_to_all(product, 'tz', 0, 0, tiled=True)  42.8 us
    all_gather x1, blocking collectives, local(): stats = lax.all_gather(jnp.stack([shard_mean, shard_square], 0), TIME)  21.5 us
    dot_general x9, matrix products, local(): lax.dot_general(left, right, (((1,), (1,)), ((), ())), preferred_element_...  16.1 us
    all_gather x1, blocking collectives, local(): row = lax.all_gather(extended, 'lx')  14.3 us
    dynamic_slice x4, local copies, waits for them, and re-layouts, dslice(): lax.dynamic_slice_in_dim(value, start, size, axis, allow_negative_indices...  9.58 us
    ppermute x1, waiting for transfers between devices, local(): lax.ppermute(row, 'ly', [(i, (i - 1) % rows_size) for i in range(rows_siz...  5.33 us
    all_to_all x1, starting transfers between devices, local(): received = lax.all_to_all(product, 'tz', 0, 0, tiled=True)  4.98 us
    ppermute x1, starting transfers between devices, local(): lax.ppermute(row, 'ly', [(i, (i + 1) % rows_size) for i in range(rows_siz...  4.68 us
  transfers between devices with their start and end apart: 5, of which 4 were waited for; matrix products, arithmetic and copies ran while one was open for 4% of the time, Pallas kernels for 0%

profile of v16, /device:TPU:24, one launch (start us, length us, event | category | flops | bytes accessed | tf_op | source)
XLA Modules:
  0.0 146.0 jit_solution(13337688877600255314)
XLA Ops:
  0.0 0.8 slice.64
  0.8 1.3 collective-permute-start
  2.0 0.9 constant_dynamic-update-slice_fusion.1
  3.0 0.9 collective-permute-done
  3.9 14.3 %all-gather = bf16[512,640]{1,0:T(8,128)(2,1)S(1)} all-gather(bf16[128,640]{1,0:T(8,128)(2,1)S(1)} %constant_dynamic-update-slice_fusion), channel_id=2, replica_groups=mesh['ly'=8,'lx'=4,'tz'=8,'tc'=2] {'lx'}, dimensions={0}, use_global_device_ids=true | all-gather | bytes 819200 | tf_op jit(solution)/shard_map/all_gather | solution.py:33
  18.1 4.7 %collective-permute-start.1 = (bf16[4,128,640]{2,1,0:T(8,128)(2,1)S(1)}, bf16[4,128,640]{2,1,0:T(8,128)(2,1)S(1)}, u32[]{:S(2)}, u32[]{:S(2)}) collective-permute-start(bf16[4,128,640]{2,1,0:T(8,128)(2,1)S(1)} %bitcast.39), channel_id=1, source_target_pairs={{0,64},{64,128},{128,192},{192,256},{256,320},{320,384},{384,448},... | collective-permute-start | bytes 1966088 | tf_op jit(solution)/shard_map/ppermute | solution.py:35
  22.8 1.9 %collective-permute-start.2 = (bf16[4,128,640]{2,1,0:T(8,128)(2,1)S(1)}, bf16[4,128,640]{2,1,0:T(8,128)(2,1)S(1)}, u32[]{:S(2)}, u32[]{:S(2)}) collective-permute-start(bf16[4,128,640]{2,1,0:T(8,128)(2,1)S(1)} %bitcast.40), channel_id=1, source_target_pairs={{0,448},{64,0},{128,64},{192,128},{256,192},{320,256},{384,320},{4... | collective-permute-start | bytes 1966088 | tf_op jit(solution)/shard_map/ppermute | solution.py:36
  24.8 1.7 %fusion.52 = (s32[1]{0:T(128)}, s32[1]{0:T(128)}, s32[1]{0:T(128)}, s32[1]{0:T(128)}, s32[1]{0:T(128)}, /*index=5*/s32[1]{0:T(128)}, s32[1]{0:T(128)}, s32[1]{0:T(128)}, s32[1]{0:T(128)}) fusion(s32[9]{0:T(128)} %param.7), kind=kLoop, calls=%fused_computation.113 | loop fusion | bytes 72 | tf_op jit(solution)/shard_map/slice | solution.py:85
  32.0 0.9 fusion.38
  32.9 0.7 fusion.53
  33.6 3.5 %collective-permute-done.1 = bf16[4,128,640]{2,1,0:T(8,128)(2,1)S(1)} collective-permute-done((bf16[4,128,640]{2,1,0:T(8,128)(2,1)S(1)}, bf16[4,128,640]{2,1,0:T(8,128)(2,1)S(1)}, u32[]{:S(2)}, u32[]{:S(2)}) %collective-permute-start.1) | collective-permute-done | bytes 655392 | tf_op jit(solution)/shard_map/ppermute | solution.py:35
  37.1 5.3 %collective-permute-done.2 = bf16[4,128,640]{2,1,0:T(8,128)(2,1)S(1)} collective-permute-done((bf16[4,128,640]{2,1,0:T(8,128)(2,1)S(1)}, bf16[4,128,640]{2,1,0:T(8,128)(2,1)S(1)}, u32[]{:S(2)}, u32[]{:S(2)}) %collective-permute-start.2) | collective-permute-done | bytes 655392 | tf_op jit(solution)/shard_map/ppermute | solution.py:36
  42.4 0.2 pad_maximum_fusion.1
  42.7 2.0 %constant_dynamic-slice_fusion.20 = (bf16[2,128,640]{2,1,0:T(8,128)(2,1)S(1)}, bf16[2,128,640]{2,1,0:T(8,128)(2,1)S(1)}, bf16[2,128,640]{2,1,0:T(8,128)(2,1)S(1)}) fusion(bf16[12,128,640]{2,1,0:T(8,128)(2,1)S(1)} %pad_maximum_fusion.1, s32[]{:T(128)} %bitcast.2, s32[]{:T(128)} %bitcast.6, s32[]{:T(128)} %bitcast.4), kind=kLoop, calls=%fused_computation.86 | loop fusion | bytes 1966092 | tf_op jit(solution)/shard_map/dynamic_slice | solution.py:14
  44.7 0.2 pad_maximum_fusion.2
  44.9 0.2 convert_reduce_fusion
  45.1 1.9 %collective-permute-start.3 = (bf16[896,640]{1,0:T(8,128)(2,1)S(1)}, bf16[896,640]{1,0:T(8,128)(2,1)S(1)}, u32[]{:S(2)}, u32[]{:S(2)}) collective-permute-start(bf16[896,640]{1,0:T(8,128)(2,1)S(1)} %get-tuple-element.14), channel_id=1, source_target_pairs={{0,1},{1,0},{2,3},{3,2},{4,5},{5,4},{6,7},{7,6},{8,9},{9,8},{10,11... | collective-permute-start | bytes 3440648 | tf_op jit(solution)/shard_map/ppermute | solution.py:47
  47.1 0.5 fusion.1
  47.6 21.5 %all-gather.2 = f32[16,2,896]{2,1,0:T(2,128)S(1)} all-gather(f32[1,2,896]{2,1,0:T(2,128)S(1)} %maximum_bitcast_fusion), channel_id=3, replica_groups=mesh['ly'=8,'lx'=4,'tz'=8,'tc'=2] {'tz','tc'}, dimensions={0}, use_global_device_ids=true | all-gather | bytes 121856 | tf_op jit(solution)/shard_map/all_gather | solution.py:51
  69.0 0.1 slice_reduce_fusion.1
  69.2 0.0 collective-permute-done.3
  69.2 1.0 fusion.5
  70.2 0.1 slice.85
  70.3 1.2 select_convert_fusion
  71.5 0.1 slice.91
  71.6 0.2 slice.92
  71.9 6.2 %constant_dynamic-slice_fusion = (bf16[64,1024]{1,0:T(8,128)(2,1)S(1)}, bf16[64,1024]{1,0:T(8,128)(2,1)S(1)}, bf16[64,1024]{1,0:T(8,128)(2,1)S(1)}, bf16[64,1024...) fusion(bf16[64,1152]{1,0:T(8,128)(2,1)S(1)} %dynamic-slice_bitc, ...), kind=kLoop, calls=%fused_computation.66 | loop fusion | bytes 2621476 | tf_op jit(solution)/shard_map/dynamic_slice | solution.py:14
  78.1 0.7 constant_dynamic-slice_fusion.1
  78.9 1.8 %convolution_dynamic-update-slice_fusion.8 = f32[64,6912]{1,0:T(8,128)} fusion(bf16[64,1024]{1,0:T(8,128)(2,1)S(1)} %get-tuple-element.33, bf16[64,1152]{1,0:T(8,128)(2,1)S(1)} %get-tuple-element.24, bf16[768,1024]{1,0:T(8,128)(2,1)S(1)} %slice.92, bf16[768,1152]{1,0:T(8,128)(2,1)S(1)} %slice.91), kind=kOutput, calls=%fused_computation.19 | convolution fusion | flops 221151232 | bytes 3817472 | tf_op jit(solution)/shard_map/dot_general | solution.py:94
  80.6 1.8 %convolution_dynamic-update-slice_fusion.7 = f32[64,6912]{1,0:T(8,128)} fusion(f32[64,6912]{1,0:T(8,128)} %convolution_dynamic-update-slice_fusion.8, bf16[64,1024]{1,0:T(8,128)(2,1)S(1)} %get-tuple-element.32, bf16[64,1152]{1,0:T(8,128)(2,1)S(1)} %get-tuple-element.23, bf16[768,1024]{1,0:T(8,128)(2,1)S(1)} %slice.92, bf16[768,1152]{1,0:T(8,128)(2,1)S(1)} %slice.91), kind=kOutput, calls=%fused_computation.18 | convolution fusion | flops 221151232 | bytes 3817472 | tf_op jit(solution)/shard_map/dot_general | solution.py:94
  82.4 1.8 %convolution_dynamic-update-slice_fusion.6 = f32[64,6912]{1,0:T(8,128)} fusion(f32[64,6912]{1,0:T(8,128)} %convolution_dynamic-update-slice_fusion.7, bf16[64,1024]{1,0:T(8,128)(2,1)S(1)} %get-tuple-element.31, bf16[64,1152]{1,0:T(8,128)(2,1)S(1)} %get-tuple-element.22, bf16[768,1024]{1,0:T(8,128)(2,1)S(1)} %slice.92, bf16[768,1152]{1,0:T(8,128)(2,1)S(1)} %slice.91), kind=kOutput, calls=%fused_computation.17 | convolution fusion | flops 221151232 | bytes 3817472 | tf_op jit(solution)/shard_map/dot_general | solution.py:94
  84.2 1.8 %convolution_dynamic-update-slice_fusion.5 = f32[64,6912]{1,0:T(8,128)} fusion(f32[64,6912]{1,0:T(8,128)} %convolution_dynamic-update-slice_fusion.6, bf16[64,1024]{1,0:T(8,128)(2,1)S(1)} %get-tuple-element.30, bf16[64,1152]{1,0:T(8,128)(2,1)S(1)} %get-tuple-element.21, bf16[768,1024]{1,0:T(8,128)(2,1)S(1)} %slice.92, bf16[768,1152]{1,0:T(8,128)(2,1)S(1)} %slice.91), kind=kOutput, calls=%fused_computation.16 | convolution fusion | flops 221151232 | bytes 3817472 | tf_op jit(solution)/shard_map/dot_general | solution.py:94
  86.0 1.8 %convolution_dynamic-update-slice_fusion.4 = f32[64,6912]{1,0:T(8,128)} fusion(f32[64,6912]{1,0:T(8,128)} %convolution_dynamic-update-slice_fusion.5, bf16[64,1024]{1,0:T(8,128)(2,1)S(1)} %get-tuple-element.29, bf16[64,1152]{1,0:T(8,128)(2,1)S(1)} %get-tuple-element.20, bf16[768,1024]{1,0:T(8,128)(2,1)S(1)} %slice.92, bf16[768,1152]{1,0:T(8,128)(2,1)S(1)} %slice.91), kind=kOutput, calls=%fused_computation.15 | convolution fusion | flops 221151232 | bytes 3817472 | tf_op jit(solution)/shard_map/dot_general | solution.py:94
  87.8 1.8 %convolution_dynamic-update-slice_fusion.3 = f32[64,6912]{1,0:T(8,128)} fusion(f32[64,6912]{1,0:T(8,128)} %convolution_dynamic-update-slice_fusion.4, bf16[64,1024]{1,0:T(8,128)(2,1)S(1)} %get-tuple-element.28, bf16[64,1152]{1,0:T(8,128)(2,1)S(1)} %get-tuple-element.19, bf16[768,1024]{1,0:T(8,128)(2,1)S(1)} %slice.92, bf16[768,1152]{1,0:T(8,128)(2,1)S(1)} %slice.91), kind=kOutput, calls=%fused_computation.14 | convolution fusion | flops 221151232 | bytes 3817472 | tf_op jit(solution)/shard_map/dot_general | solution.py:94
  89.6 1.8 %convolution_dynamic-update-slice_fusion.2 = f32[64,6912]{1,0:T(8,128)} fusion(f32[64,6912]{1,0:T(8,128)} %convolution_dynamic-update-slice_fusion.3, bf16[64,1024]{1,0:T(8,128)(2,1)S(1)} %get-tuple-element.27, bf16[64,1152]{1,0:T(8,128)(2,1)S(1)} %get-tuple-element.18, bf16[768,1024]{1,0:T(8,128)(2,1)S(1)} %slice.92, bf16[768,1152]{1,0:T(8,128)(2,1)S(1)} %slice.91), kind=kOutput, calls=%fused_computation.13 | convolution fusion | flops 221151232 | bytes 3817472 | tf_op jit(solution)/shard_map/dot_general | solution.py:94
  91.3 1.8 %convolution_dynamic-update-slice_fusion.1 = f32[64,6912]{1,0:T(8,128)} fusion(f32[64,6912]{1,0:T(8,128)} %convolution_dynamic-update-slice_fusion.2, bf16[64,1024]{1,0:T(8,128)(2,1)S(1)} %get-tuple-element.26, bf16[64,1152]{1,0:T(8,128)(2,1)S(1)} %get-tuple-element.17, bf16[768,1024]{1,0:T(8,128)(2,1)S(1)} %slice.92, bf16[768,1152]{1,0:T(8,128)(2,1)S(1)} %slice.91), kind=kOutput, calls=%fused_computation.12 | convolution fusion | flops 221151232 | bytes 3817472 | tf_op jit(solution)/shard_map/dot_general | solution.py:94
  93.1 1.8 %convolution_dynamic-update-slice_fusion = f32[64,6912]{1,0:T(8,128)} fusion(f32[64,6912]{1,0:T(8,128)} %convolution_dynamic-update-slice_fusion.1, bf16[64,1024]{1,0:T(8,128)(2,1)S(1)} %get-tuple-element.25, bf16[64,1152]{1,0:T(8,128)(2,1)S(1)} %get-tuple-element.16, bf16[768,1024]{1,0:T(8,128)(2,1)S(1)} %slice.92, bf16[768,1152]{1,0:T(8,128)(2,1)S(1)} %slice.91), kind=kOutput, calls=%fused_computation.11 | convolution fusion | flops 221151232 | bytes 3817472 | tf_op jit(solution)/shard_map/dot_general | solution.py:94
  94.9 5.0 %all-to-all-start = ((f32[8,8,6912]{2,1,0:T(8,128)}), f32[8,8,6912]{2,1,0:T(8,128)S(1)}, u32[]{:S(2)}, u32[]{:S(2)}) async-start(f32[8,8,6912]{2,1,0:T(8,128)} %bitcast.24), calls=%async_computation | async-start | bytes 3538944 | tf_op jit(solution)/shard_map/all_to_all | solution.py:100
  99.9 0.0 copy-done.1
  99.9 0.6 dynamic_slice.78
  101.2 0.7 iota_compare_fusion.1
  101.8 0.0 copy-done
  101.9 42.8 %all-to-all-done = f32[8,8,6912]{2,1,0:T(8,128)S(1)} async-done(((f32[8,8,6912]{2,1,0:T(8,128)}), f32[8,8,6912]{2,1,0:T(8,128)S(1)}, u32[]{:S(2)}, u32[]{:S(2)}) %all-to-all-start) | async-done | bytes 1769504 | tf_op jit(solution)/shard_map/all_to_all | solution.py:100
  144.6 0.1 reduce_sum.68
  144.7 0.1 reshape.78
  144.8 0.3 multiply_reduce_fusion
  145.1 0.1 divide_bitcast_fusion
  145.3 0.7 copy.6
  (18 shorter events, 0.2 us)
Async XLA Ops:
  0.8 3.1 %collective-permute-start = (bf16[128,128]{1,0:T(8,128)(2,1)S(1)}, bf16[128,128]{1,0:T(8,128)(2,1)S(1)}, u32[]{:S(2)}, u32[]{:S(2)}) collective-permute-start(bf16[128,128]{1,0:T(8,128)(2,1)S(1)} %slice.64), channel_id=1, source_target_pairs={{1,0},{2,1},{3,2},{4,3},{5,4},{6,5},{7,6},{8,7},{9,8},{10,9},{11,1... | collective-permute-start | bytes 98312 | tf_op jit(solution)/shard_map/ppermute | solution.py:25
  18.1 18.9 %collective-permute-start.1 = (bf16[4,128,640]{2,1,0:T(8,128)(2,1)S(1)}, bf16[4,128,640]{2,1,0:T(8,128)(2,1)S(1)}, u32[]{:S(2)}, u32[]{:S(2)}) collective-permute-start(bf16[4,128,640]{2,1,0:T(8,128)(2,1)S(1)} %bitcast.39), channel_id=1, source_target_pairs={{0,64},{64,128},{128,192},{192,256},{256,320},{320,384},{384,448},... | collective-permute-start | bytes 1966088 | tf_op jit(solution)/shard_map/ppermute | solution.py:35
  22.8 19.6 %collective-permute-start.2 = (bf16[4,128,640]{2,1,0:T(8,128)(2,1)S(1)}, bf16[4,128,640]{2,1,0:T(8,128)(2,1)S(1)}, u32[]{:S(2)}, u32[]{:S(2)}) collective-permute-start(bf16[4,128,640]{2,1,0:T(8,128)(2,1)S(1)} %bitcast.40), channel_id=1, source_target_pairs={{0,448},{64,0},{128,64},{192,128},{256,192},{320,256},{384,320},{4... | collective-permute-start | bytes 1966088 | tf_op jit(solution)/shard_map/ppermute | solution.py:36
  45.1 24.1 %collective-permute-start.3 = (bf16[896,640]{1,0:T(8,128)(2,1)S(1)}, bf16[896,640]{1,0:T(8,128)(2,1)S(1)}, u32[]{:S(2)}, u32[]{:S(2)}) collective-permute-start(bf16[896,640]{1,0:T(8,128)(2,1)S(1)} %get-tuple-element.14), channel_id=1, source_target_pairs={{0,1},{1,0},{2,3},{3,2},{4,5},{5,4},{6,7},{7,6},{8,9},{9,8},{10,11... | collective-permute-start | bytes 3440648 | tf_op jit(solution)/shard_map/ppermute | solution.py:47
  94.9 5.0 %copy-start.1 = (s32[16]{0:T(128)S(1)}, s32[16]{0:T(128)}, u32[]{:S(2)}) copy-start(s32[16]{0:T(128)} %param.6) | copy-start | bytes 196
  94.9 6.9 %copy-start = (s32[9]{0:T(128)S(1)}, s32[9]{0:T(128)}, u32[]{:S(2)}) copy-start(s32[9]{0:T(128)} %param.7) | copy-start | bytes 112
  94.9 49.7 %all-to-all-start = ((f32[8,8,6912]{2,1,0:T(8,128)}), f32[8,8,6912]{2,1,0:T(8,128)S(1)}, u32[]{:S(2)}, u32[]{:S(2)}) async-start(f32[8,8,6912]{2,1,0:T(8,128)} %bitcast.24), calls=%async_computation | async-start | bytes 3538944 | tf_op jit(solution)/shard_map/all_to_all | solution.py:100
